TPU v7x, 128 devices: a whole 4x4x4 slice. The times are simulated.
128 devices in a mesh: region: 64 (over y, x, z), rep: 2 (over core).
Axes of the slice: x: 4, y: 4, z: 4, core: 2. Of those that a mesh axis runs over, the one named last changes fastest.
Arguments:
- emb: bfloat16 [262144, 128], P('region'), may hold values from -6 to 6
- lengths: bfloat16 [6144, 14, 128, 128], P(('region', 'rep')), may hold values from 0 to 0.003616333
- pair_block: int32 [6144, 14], P(('region', 'rep')), may hold values from 0 to 255, as said below
- feats: bfloat16 [16, 786432], P(None, ('region', 'rep')), may hold values from -6 to 6
- proj: bfloat16 [16, 128], replicated, may hold values from -1.5 to 1.5
- targets: float32 [786432], P(('region', 'rep')), may hold values from -6 to 6
- trip_weight: float32 [786432], P(('region', 'rep')), may hold values from 0.5 to 5
- send_list: int32 [64, 2, 64, 4], P('region', 'rep'), may hold values from -1 to 31, as said below
- nb_index: int32 [64, 4, 4096], P('region'), may hold values from 0 to 4351, as said below
- nb_weight: float32 [64, 4, 4096], P('region'), may hold values from 0.2 to 1
Outputs:
- predicted: float32 [786432], P(('region', 'rep'))
- gradient: bfloat16 [262144, 128], P('region')
Inputs may be any that keep to these rules, and one draw needn't show every extreme that they name: `send_list`: entry [q, p, r, j] names a block of region q's embedding rows that region r's device with rep index p needs; in each list over j the live entries come first and the rest are -1; each list holds 1 to 4 live entries and some hold exactly 4. `pair_block`: entry [t, k] is q * 4 + j for a live slot j of the list that region q sends to the device holding trip block t. `nb_index`: entry [r, k, i] is a position in region r's rows extended by 128 rows of each neighbouring region on either side (regions wrap around); it differs from the segment's own position i + 128 by 1 to 128.
All inputs are finite; a program needn't handle non-finite values.
Results may differ from a plain program's by a relative error of at most 0.0034.
Values may be sent and summed in bfloat16 or wider, within the bound.
No kernel may reach another device: no remote copies, remote signals or barrier semaphores. Data moves between devices by JAX's collectives and lax.ppermute only.
A program may use at most 192 MiB of HBM per device.

v0:
```python
import jax
import jax.numpy as jnp
from jax import lax
from jax.sharding import PartitionSpec as P

LAM = 0.25


def with_halo(cells, sides, width):
    for axis, dim in sides:
        count = lax.axis_size(axis)
        head = lax.slice_in_dim(cells, 0, width, axis=dim)
        tail = lax.slice_in_dim(cells, cells.shape[dim] - width, cells.shape[dim], axis=dim)
        cells = jnp.concatenate(
            [
                lax.ppermute(tail, axis, [(i, (i + 1) % count) for i in range(count)]),
                cells,
                lax.ppermute(head, axis, [((i + 1) % count, i) for i in range(count)]),
            ],
            axis=dim,
        )
    return cells


def local(
    emb, lengths, pair_block, feats, proj, targets, trip_weight, send_list, nb_index, nb_weight
):
    block_size = lengths.shape[2]
    rank_width = emb.shape[1]
    seg_rows = emb.shape[0]
    block_count = seg_rows // block_size
    regions = lax.axis_size("region")
    blocks = emb.reshape(block_count, block_size, rank_width)
    send_rows = send_list[0, 0]
    live_mask = send_rows >= 0
    slot_count = send_rows.shape[1]
    outgoing = blocks[jnp.where(live_mask, send_rows, 0)] * live_mask[:, :, None, None].astype(
        jnp.bfloat16
    )
    incoming = lax.all_to_all(outgoing, "region", split_axis=0, concat_axis=0, tiled=True)
    incoming = incoming.reshape(regions * slot_count, block_size, rank_width)
    trip_blocks = lengths.shape[0]
    pair_count = lengths.shape[1]
    trip_query = jnp.einsum("ft,fr->tr", feats, proj, preferred_element_type=jnp.float32)
    query_blocks = trip_query.reshape(trip_blocks, block_size, rank_width)

    def forward(column, hidden_sum):
        length_block = lax.dynamic_index_in_dim(lengths, column, 1, keepdims=False)
        pair_index = lax.dynamic_index_in_dim(pair_block, column, 1, keepdims=False)
        picked = incoming[pair_index]
        return hidden_sum + jnp.einsum(
            "tas,tsr->tar", length_block, picked, preferred_element_type=jnp.float32
        )

    hidden_sum = lax.fori_loop(
        0, pair_count, forward, jnp.zeros((trip_blocks, block_size, rank_width), jnp.float32)
    )
    predicted = jnp.sum(hidden_sum * query_blocks, axis=-1).reshape(trip_blocks * block_size)
    scaled = ((trip_weight * (predicted - targets))[:, None] * trip_query).astype(jnp.bfloat16)
    scaled = scaled.reshape(trip_blocks, block_size, rank_width)

    def backward(column, slot_grad):
        length_block = lax.dynamic_index_in_dim(lengths, column, 1, keepdims=False)
        pair_index = lax.dynamic_index_in_dim(pair_block, column, 1, keepdims=False)
        term = jnp.einsum("tas,tar->tsr", length_block, scaled, preferred_element_type=jnp.float32)
        return slot_grad.at[pair_index].add(term)

    slot_grad = lax.fori_loop(
        0,
        pair_count,
        backward,
        jnp.zeros((regions * slot_count, block_size, rank_width), jnp.float32),
    )
    returned = lax.all_to_all(
        slot_grad.reshape(regions, slot_count, block_size, rank_width),
        "region",
        split_axis=0,
        concat_axis=0,
        tiled=True,
    )
    returned = returned.reshape(regions * slot_count, block_size * rank_width)
    target_rows = jnp.where(live_mask, send_rows, block_count).reshape(-1)
    owned = (
        jnp.zeros((block_count + 1, block_size * rank_width), jnp.float32)
        .at[target_rows]
        .add(returned)
    )
    owned = owned[:block_count]
    owned = owned.reshape(seg_rows, rank_width)
    extended = with_halo(emb, (("region", 0),), block_size)
    own_rows = emb.astype(jnp.float32)
    smoothed = jnp.zeros((seg_rows, rank_width), jnp.float32)
    for column in range(nb_index.shape[1]):
        neighbour = nb_index[0, column]
        edge_weight = nb_weight[0, column]
        smoothed = smoothed + edge_weight[:, None] * (
            own_rows - extended[neighbour].astype(jnp.float32)
        )
    gradient = lax.psum(owned, "rep") + LAM * smoothed
    return (predicted, gradient.astype(jnp.bfloat16))


def solution(mesh):
    placed = (
        P("region", None),
        P(("region", "rep"), None, None, None),
        P(("region", "rep"), None),
        P(None, ("region", "rep")),
        P(),
        P(("region", "rep")),
        P(("region", "rep")),
        P("region", "rep", None, None),
        P("region", None, None),
        P("region", None, None),
    )
    return jax.shard_map(
        local,
        mesh=mesh,
        in_specs=placed,
        out_specs=(P(("region", "rep")), P("region", None)),
        check_vma=False,
    )
```

profile of v0, /device:TPU:34, one launch (start us, length us, event | category | flops | bytes accessed | tf_op | source)
XLA Modules:
  0.0 843.8 jit_solution(11588652391888412704)
XLA Ops:
  8.9 9.7 %gather_fusion.1 = bf16[256,128,128]{2,1,0:T(8,128)(2,1)} fusion(bf16[32,128,128]{2,1,0:T(8,128)(2,1)} %bitcast.68, s32[1024]{0:T(1024)S(1)} %pad_clamp_fusion.1), kind=kCustom, calls=%fused_computation.1 | custom fusion | bytes 16778240 | tf_op jit(solution)/shard_map/gather | solution.py:37
  18.7 7.2 broadcast_multiply_fusion
  25.9 11.3 %all-to-all-start = ((bf16[64,4,128,128]{3,2,1,0:T(8,128)(2,1)}), bf16[64,4,128,128]{3,2,1,0:T(8,128)(2,1)}, u32[]{:S(2)}, u32[]{:S(2)}) async-start(bf16[64,4,128,128]{3,2,1,0:T(8,128)(2,1)} %broadcast_multiply_fusion), calls=%async_computation | async-start | bytes 16777216 | tf_op jit(solution)/shard_map/all_to_all | solution.py:40
  39.5 114.2 %all-to-all-done = bf16[64,4,128,128]{3,2,1,0:T(8,128)(2,1)} async-done(((bf16[64,4,128,128]{3,2,1,0:T(8,128)(2,1)}), bf16[64,4,128,128]{3,2,1,0:T(8,128)(2,1)}, u32[]{:S(2)}, u32[]{:S(2)}) %all-to-all-start) | async-done | bytes 8388640 | tf_op jit(solution)/shard_map/all_to_all | solution.py:40
  153.7 134.5 %while.28 = (s32[]{:T(128)}, f32[48,128,128]{2,1,0:T(8,128)}, bf16[48,14,128,128]{3,2,1,0:T(8,128)(2,1)}, s32[48,14]{0,1:T(8,128)}, bf16[256,128,128]{2,1,0:T(8,128)(2,1)}, /*index=5*/s32[]{:T(128)}, s32[]{:T(128)}) while((s32[]{:T(128)}, f32[48,128,128]{2,1,0:T(8,128)}, bf16[48,14,128,128]{3,2,1,0:T(8,128)(2,1)}, ...), condition=%wide.region_1.2_spmd.clone, body=%wide.region_0.1_spmd.clone.sunk | while | flops 202900624 | bytes 12588379 | solution.py:55
  244.8 4.7 select_add_fusion.2
  264.1 4.7 select_add_fusion.2
  283.5 4.7 select_add_fusion.2
  294.1 7.9 broadcast_in_dim.28
  301.9 172.8 %while.27 = (s32[]{:T(128)}, f32[256,128,128]{2,1,0:T(8,128)}, s32[48,14]{0,1:T(8,128)}, bf16[48,14,128,128]{3,2,1,0:T(8,128)(2,1)}, bf16[48,128,128]{2,1,0:T(8,128)(2,1)}, /*index=5*/s32[]{:T(128)}) while((s32[]{:T(128)}, f32[256,128,128]{2,1,0:T(8,128)}, s32[48,14]{0,1:T(8,128)}, bf16[48,14,128,128]{3,2,1,0:T(8,128)(2,1)}, ...), condition=%wide.region_5.6_spmd, body=%wide.region_3.5_spmd.sunk | while | flops 202113168 | bytes 15729801 | solution.py:68
  305.2 9.1 %scatter_fusion = f32[256,128,128]{2,1,0:T(8,128)} fusion(f32[256,128,128]{2,1,0:T(8,128)} %get-tuple-element.350, s32[48]{0:T(128)S(1)} %fusion.40, f32[48,128,128]{2,1,0:T(8,128)S(1)} %fusion.41), kind=kCustom, calls=%fused_computation.6.clone.1 | custom fusion | flops 786432 | bytes 9437376 | tf_op jit(solution)/shard_map/while/body/eval_jaxpr/scatter-add | solution.py:66
  317.5 9.0 %scatter_fusion = f32[256,128,128]{2,1,0:T(8,128)} fusion(f32[256,128,128]{2,1,0:T(8,128)} %get-tuple-element.350, s32[48]{0:T(128)S(1)} %fusion.40, f32[48,128,128]{2,1,0:T(8,128)S(1)} %fusion.41), kind=kCustom, calls=%fused_computation.6.clone.1 | custom fusion | flops 786432 | bytes 9437376 | tf_op jit(solution)/shard_map/while/body/eval_jaxpr/scatter-add | solution.py:66
  329.8 9.0 %scatter_fusion = f32[256,128,128]{2,1,0:T(8,128)} fusion(f32[256,128,128]{2,1,0:T(8,128)} %get-tuple-element.350, s32[48]{0:T(128)S(1)} %fusion.40, f32[48,128,128]{2,1,0:T(8,128)S(1)} %fusion.41), kind=kCustom, calls=%fused_computation.6.clone.1 | custom fusion | flops 786432 | bytes 9437376 | tf_op jit(solution)/shard_map/while/body/eval_jaxpr/scatter-add | solution.py:66
  342.2 9.0 %scatter_fusion = f32[256,128,128]{2,1,0:T(8,128)} fusion(f32[256,128,128]{2,1,0:T(8,128)} %get-tuple-element.350, s32[48]{0:T(128)S(1)} %fusion.40, f32[48,128,128]{2,1,0:T(8,128)S(1)} %fusion.41), kind=kCustom, calls=%fused_computation.6.clone.1 | custom fusion | flops 786432 | bytes 9437376 | tf_op jit(solution)/shard_map/while/body/eval_jaxpr/scatter-add | solution.py:66
  354.4 9.0 %scatter_fusion = f32[256,128,128]{2,1,0:T(8,128)} fusion(f32[256,128,128]{2,1,0:T(8,128)} %get-tuple-element.350, s32[48]{0:T(128)S(1)} %fusion.40, f32[48,128,128]{2,1,0:T(8,128)S(1)} %fusion.41), kind=kCustom, calls=%fused_computation.6.clone.1 | custom fusion | flops 786432 | bytes 9437376 | tf_op jit(solution)/shard_map/while/body/eval_jaxpr/scatter-add | solution.py:66
  366.7 9.1 %scatter_fusion = f32[256,128,128]{2,1,0:T(8,128)} fusion(f32[256,128,128]{2,1,0:T(8,128)} %get-tuple-element.350, s32[48]{0:T(128)S(1)} %fusion.40, f32[48,128,128]{2,1,0:T(8,128)S(1)} %fusion.41), kind=kCustom, calls=%fused_computation.6.clone.1 | custom fusion | flops 786432 | bytes 9437376 | tf_op jit(solution)/shard_map/while/body/eval_jaxpr/scatter-add | solution.py:66
  379.1 9.1 %scatter_fusion = f32[256,128,128]{2,1,0:T(8,128)} fusion(f32[256,128,128]{2,1,0:T(8,128)} %get-tuple-element.350, s32[48]{0:T(128)S(1)} %fusion.40, f32[48,128,128]{2,1,0:T(8,128)S(1)} %fusion.41), kind=kCustom, calls=%fused_computation.6.clone.1 | custom fusion | flops 786432 | bytes 9437376 | tf_op jit(solution)/shard_map/while/body/eval_jaxpr/scatter-add | solution.py:66
  391.5 9.0 %scatter_fusion = f32[256,128,128]{2,1,0:T(8,128)} fusion(f32[256,128,128]{2,1,0:T(8,128)} %get-tuple-element.350, s32[48]{0:T(128)S(1)} %fusion.40, f32[48,128,128]{2,1,0:T(8,128)S(1)} %fusion.41), kind=kCustom, calls=%fused_computation.6.clone.1 | custom fusion | flops 786432 | bytes 9437376 | tf_op jit(solution)/shard_map/while/body/eval_jaxpr/scatter-add | solution.py:66
  403.8 9.1 %scatter_fusion = f32[256,128,128]{2,1,0:T(8,128)} fusion(f32[256,128,128]{2,1,0:T(8,128)} %get-tuple-element.350, s32[48]{0:T(128)S(1)} %fusion.40, f32[48,128,128]{2,1,0:T(8,128)S(1)} %fusion.41), kind=kCustom, calls=%fused_computation.6.clone.1 | custom fusion | flops 786432 | bytes 9437376 | tf_op jit(solution)/shard_map/while/body/eval_jaxpr/scatter-add | solution.py:66
  416.2 9.1 %scatter_fusion = f32[256,128,128]{2,1,0:T(8,128)} fusion(f32[256,128,128]{2,1,0:T(8,128)} %get-tuple-element.350, s32[48]{0:T(128)S(1)} %fusion.40, f32[48,128,128]{2,1,0:T(8,128)S(1)} %fusion.41), kind=kCustom, calls=%fused_computation.6.clone.1 | custom fusion | flops 786432 | bytes 9437376 | tf_op jit(solution)/shard_map/while/body/eval_jaxpr/scatter-add | solution.py:66
  428.5 9.1 %scatter_fusion = f32[256,128,128]{2,1,0:T(8,128)} fusion(f32[256,128,128]{2,1,0:T(8,128)} %get-tuple-element.350, s32[48]{0:T(128)S(1)} %fusion.40, f32[48,128,128]{2,1,0:T(8,128)S(1)} %fusion.41), kind=kCustom, calls=%fused_computation.6.clone.1 | custom fusion | flops 786432 | bytes 9437376 | tf_op jit(solution)/shard_map/while/body/eval_jaxpr/scatter-add | solution.py:66
  440.9 9.1 %scatter_fusion = f32[256,128,128]{2,1,0:T(8,128)} fusion(f32[256,128,128]{2,1,0:T(8,128)} %get-tuple-element.350, s32[48]{0:T(128)S(1)} %fusion.40, f32[48,128,128]{2,1,0:T(8,128)S(1)} %fusion.41), kind=kCustom, calls=%fused_computation.6.clone.1 | custom fusion | flops 786432 | bytes 9437376 | tf_op jit(solution)/shard_map/while/body/eval_jaxpr/scatter-add | solution.py:66
  453.2 9.1 %scatter_fusion = f32[256,128,128]{2,1,0:T(8,128)} fusion(f32[256,128,128]{2,1,0:T(8,128)} %get-tuple-element.350, s32[48]{0:T(128)S(1)} %fusion.40, f32[48,128,128]{2,1,0:T(8,128)S(1)} %fusion.41), kind=kCustom, calls=%fused_computation.6.clone.1 | custom fusion | flops 786432 | bytes 9437376 | tf_op jit(solution)/shard_map/while/body/eval_jaxpr/scatter-add | solution.py:66
  465.6 9.1 %scatter_fusion = f32[256,128,128]{2,1,0:T(8,128)} fusion(f32[256,128,128]{2,1,0:T(8,128)} %get-tuple-element.350, s32[48]{0:T(128)S(1)} %fusion.40, f32[48,128,128]{2,1,0:T(8,128)S(1)} %fusion.41), kind=kCustom, calls=%fused_computation.6.clone.1 | custom fusion | flops 786432 | bytes 9437376 | tf_op jit(solution)/shard_map/while/body/eval_jaxpr/scatter-add | solution.py:66
  474.7 5.6 all-to-all-start.1
  483.5 250.6 %all-to-all-done.1 = f32[64,4,128,128]{3,2,1,0:T(8,128)} async-done(((f32[64,4,128,128]{3,2,1,0:T(8,128)}), f32[64,4,128,128]{3,2,1,0:T(8,128)}, u32[]{:S(2)}, u32[]{:S(2)}) %all-to-all-start.1) | async-done | bytes 16777248 | tf_op jit(solution)/shard_map/all_to_all | solution.py:74
  734.1 35.5 %scatter_custom_fusion.1 = f32[33,16384]{1,0:T(8,128)} fusion(s32[256]{0:T(256)S(1)} %bitcast.81, f32[32,8,128,128]{3,2,1,0:T(8,128)} %bitcast.32, f32[]{:T(128)} %constant.80.clone.1), kind=kCustom, calls=%fused_computation.21 | custom fusion | flops 4194304 | bytes 18939908 | tf_op jit(solution)/shard_map/scatter-add | solution.py:86
  773.0 12.1 %gather_fusion.2 = bf16[4096,128]{1,0:T(8,128)(2,1)S(1)} fusion(bf16[4352,128]{1,0:T(8,128)(2,1)S(1)} %constant_dynamic-update-slice_fusion, s32[4096]{0:T(1024)S(1)} %broadcast_clamp_fusion.3), kind=kCustom, calls=%fused_computation.2 | custom fusion | bytes 2113536 | tf_op jit(solution)/shard_map/gather | solution.py:97
  785.2 14.9 %gather_fusion.3 = bf16[4096,128]{1,0:T(8,128)(2,1)} fusion(bf16[4352,128]{1,0:T(8,128)(2,1)S(1)} %constant_dynamic-update-slice_fusion, s32[4096]{0:T(1024)S(1)} %broadcast_clamp_fusion.2), kind=kCustom, calls=%fused_computation.3 | custom fusion | bytes 2113536 | tf_op jit(solution)/shard_map/gather | solution.py:97
  800.1 14.9 %gather_fusion.4 = bf16[4096,128]{1,0:T(8,128)(2,1)} fusion(bf16[4352,128]{1,0:T(8,128)(2,1)S(1)} %constant_dynamic-update-slice_fusion, s32[4096]{0:T(1024)S(1)} %broadcast_clamp_fusion.1), kind=kCustom, calls=%fused_computation.4 | custom fusion | bytes 2113536 | tf_op jit(solution)/shard_map/gather | solution.py:97
  814.9 15.0 %gather_fusion.5 = bf16[4096,128]{1,0:T(8,128)(2,1)} fusion(bf16[4352,128]{1,0:T(8,128)(2,1)S(1)} %constant_dynamic-update-slice_fusion, s32[4096]{0:T(1024)S(1)} %broadcast_clamp_fusion), kind=kCustom, calls=%fused_computation.5 | custom fusion | bytes 2113536 | tf_op jit(solution)/shard_map/gather | solution.py:97
  830.0 6.6 fusion.18
  (137 shorter events, 182.1 us)
Async XLA Ops:
  7.2 30.1 %copy-start = (bf16[16,6144]{1,0:T(8,128)(2,1)S(1)}, bf16[16,6144]{1,0:T(8,128)(2,1)}, u32[]{:S(2)}) copy-start(bf16[16,6144]{1,0:T(8,128)(2,1)} %param.17) | copy-start | bytes 589828
  25.9 11.4 %copy-start.10 = (bf16[16,128]{1,0:T(8,128)(2,1)S(1)}, bf16[16,128]{1,0:T(8,128)(2,1)}, u32[]{:S(2)}) copy-start(bf16[16,128]{1,0:T(8,128)(2,1)} %param.18) | copy-start | bytes 12292
  25.9 127.8 %all-to-all-start = ((bf16[64,4,128,128]{3,2,1,0:T(8,128)(2,1)}), bf16[64,4,128,128]{3,2,1,0:T(8,128)(2,1)}, u32[]{:S(2)}, u32[]{:S(2)}) async-start(bf16[64,4,128,128]{3,2,1,0:T(8,128)(2,1)} %broadcast_multiply_fusion), calls=%async_computation | async-start | bytes 16777216 | tf_op jit(solution)/shard_map/all_to_all | solution.py:40
  288.2 3.9 copy-start.7
  288.2 3.9 copy-start.8
  288.2 3.9 copy-start.3
  292.1 9.8 %copy-start.4 = (f32[48,128]{1,0:T(8,128)}, f32[48,128]{1,0:T(8,128)S(1)}, u32[]{:S(2)}) copy-start(f32[48,128]{1,0:T(8,128)S(1)} %multiply_reduce_fusion) | copy-start | bytes 73732
  474.7 5.6 copy-start.2
  474.7 8.4 copy-start.9
  474.7 8.7 %copy-start.5 = (s32[1,4,4096]{2,1,0:T(4,128)S(1)}, s32[1,4,4096]{2,1,0:T(4,128)}, u32[]{:S(2)}) copy-start(s32[1,4,4096]{2,1,0:T(4,128)} %param.22) | copy-start | bytes 196612
  474.7 259.4 %all-to-all-start.1 = ((f32[64,4,128,128]{3,2,1,0:T(8,128)}), f32[64,4,128,128]{3,2,1,0:T(8,128)}, u32[]{:S(2)}, u32[]{:S(2)}) async-start(f32[64,4,128,128]{3,2,1,0:T(8,128)} %bitcast.67), calls=%async_computation.1 | async-start | bytes 33554432 | tf_op jit(solution)/shard_map/all_to_all | solution.py:74
  480.3 349.7 %all-reduce.2.cloned.1.call-start = ((), (), s32[]{:S(2)}) async-start(), calls=%async_computation.2 | async-start | bytes 4194304 | tf_op jit(solution)/shard_map/psum | solution.py:99
  481.0 291.9 %collective-permute-start = (bf16[128,128]{1,0:T(8,128)(2,1)}, bf16[128,128]{1,0:T(8,128)(2,1)S(1)}, u32[]{:S(2)}, u32[]{:S(2)}) collective-permute-start(bf16[128,128]{1,0:T(8,128)(2,1)} %get-tuple-element.251), channel_id=1, source_target_pairs={{0,2},{2,4},{4,6},{6,8},{8,10},{10,12},{12,14},{14,16},{16,18},{18... | collective-permute-start | bytes 98312 | tf_op jit(solution)/shard_map/ppermute | solution.py:16
  482.4 290.7 %collective-permute-start.1 = (bf16[128,128]{1,0:T(8,128)(2,1)S(1)}, bf16[128,128]{1,0:T(8,128)(2,1)S(1)}, u32[]{:S(2)}, u32[]{:S(2)}) collective-permute-start(bf16[128,128]{1,0:T(8,128)(2,1)S(1)} %get-tuple-element.250), channel_id=1, source_target_pairs={{2,0},{4,2},{6,4},{8,6},{10,8},{12,10},{14,12},{16,14},{18,16},{20... | collective-permute-start | bytes 98312 | tf_op jit(solution)/shard_map/ppermute | solution.py:18
  769.6 1.6 slice-start
  771.2 1.5 copy-start.6
  830.0 6.6 copy-start.1
Sparse Core Ops, SparseCore 0:
  772.9 22.5 all-reduce.1
where the time goes:
time: 857 us; the launch traced here: 844 us
  waiting for transfers between devices  365 us (43%)
  other arithmetic  203 us (24%)
  local copies, waits for them, and re-layouts  138 us (16%)
  matrix products  104 us (12%)
  starting transfers between devices  19.1 us (2%)
  between operations  14.6 us (2%)
    all_to_all x1, waiting for transfers between devices, local(): lax.all_to_all(slot_grad.reshape(regions, slot_count, block_size, rank_wi...  251 us
    scatter-add x14, other arithmetic, backward(): return slot_grad.at[pair_index].add(term)  127 us
    all_to_all x1, waiting for transfers between devices, local(): lax.all_to_all(outgoing, 'region', split_axis=0, concat_axis=0, tiled=True)  114 us
    dot_general x14, matrix products, forward(): jnp.einsum('tas,tsr->tar', length_block, picked, preferred_element_type=j...  65.3 us
    gather x14, local copies, waits for them, and re-layouts, forward(): picked = incoming[pair_index]  59.2 us
    gather x4, local copies, waits for them, and re-layouts, local(): extended[neighbour].astype(jnp.float32)  56.9 us
    dot_general x14, matrix products, backward(): jnp.einsum('tas,tar->tsr', length_block, scaled, preferred_element_type=j...  36 us
    scatter-add x1, other arithmetic, local(): owned = jnp.zeros((block_count + 1, block_size * rank_width), jnp.float32...  35.5 us
  transfers between devices with their start and end apart: 5, of which 2 were waited for; matrix products, arithmetic and copies ran while one was open for 12% of the time, Pallas kernels for 0%

commit v1 on v0

v1 whole, which is shorter than its diff:
```python
import functools

import jax
import jax.numpy as jnp
from jax import lax
from jax.experimental import pallas as pl
from jax.experimental.pallas import tpu as pltpu
from jax.sharding import PartitionSpec as P

LAM = 0.25
F32 = jnp.float32
BF16 = jnp.bfloat16
TN = (((0,), (0,)), ((), ()))


def with_halo(cells, sides, width):
    for axis, dim in sides:
        count = lax.axis_size(axis)
        head = lax.slice_in_dim(cells, 0, width, axis=dim)
        tail = lax.slice_in_dim(cells, cells.shape[dim] - width, cells.shape[dim], axis=dim)
        cells = jnp.concatenate(
            [
                lax.ppermute(tail, axis, [(i, (i + 1) % count) for i in range(count)]),
                cells,
                lax.ppermute(head, axis, [((i + 1) % count, i) for i in range(count)]),
            ],
            axis=dim,
        )
    return cells


def trip_kernel(pair_count, pb_ref, len_ref, inc_ref, q_ref, tgt_ref, w_ref, pred_ref, acc_ref):
    t = pl.program_id(0)

    @pl.when(t == 0)
    def _():
        acc_ref[...] = jnp.zeros_like(acc_ref)

    hidden = None
    for k in range(pair_count):
        p = pb_ref[t * pair_count + k]
        term = jnp.dot(len_ref[0, k], inc_ref[p], preferred_element_type=F32)
        hidden = term if hidden is None else hidden + term
    q = q_ref[0]
    pred_row = jnp.sum((hidden * q).T, axis=0, keepdims=True)
    pred_ref[0] = pred_row
    err_row = w_ref[0] * (pred_row - tgt_ref[0])
    err_col = jnp.broadcast_to(err_row, q.shape).T
    scaled = (err_col * q).astype(BF16)
    for k in range(pair_count):
        p = pb_ref[t * pair_count + k]
        acc_ref[p] += lax.dot_general(len_ref[0, k], scaled, TN, preferred_element_type=F32)


def trip_pass(pair_flat, lengths, incoming, query, tgt, wts):
    trip_blocks, pair_count, block, rank = lengths.shape
    slots = incoming.shape[0]
    const3 = lambda t, pb: (0, 0, 0)
    return pl.pallas_call(
        functools.partial(trip_kernel, pair_count),
        grid_spec=pltpu.PrefetchScalarGridSpec(
            num_scalar_prefetch=1,
            grid=(trip_blocks,),
            in_specs=[
                pl.BlockSpec((1, pair_count, block, block), lambda t, pb: (t, 0, 0, 0)),
                pl.BlockSpec((slots, block, rank), const3, pipeline_mode=pl.Buffered(1)),
                pl.BlockSpec((1, block, rank), lambda t, pb: (t, 0, 0)),
                pl.BlockSpec((1, 1, block), lambda t, pb: (t, 0, 0)),
                pl.BlockSpec((1, 1, block), lambda t, pb: (t, 0, 0)),
            ],
            out_specs=[
                pl.BlockSpec((1, 1, block), lambda t, pb: (t, 0, 0)),
                pl.BlockSpec((slots, block, rank), const3, pipeline_mode=pl.Buffered(1)),
            ],
        ),
        out_shape=[
            jax.ShapeDtypeStruct((trip_blocks, 1, block), F32),
            jax.ShapeDtypeStruct((slots, block, rank), F32),
        ],
        compiler_params=pltpu.CompilerParams(
            dimension_semantics=("arbitrary",), vmem_limit_bytes=60 * 1024 * 1024
        ),
    )(pair_flat, lengths, incoming, query, tgt, wts)


def smooth_kernel(ext_ref, nb_ref, w_ref, out_ref):
    i = pl.program_id(0)
    rows = out_ref.shape[0]
    span = 3 * rows
    base = i * rows
    window = ext_ref[pl.ds(pl.multiple_of(base, rows), span), :]
    col = lax.broadcasted_iota(jnp.int32, (rows, span), 1)
    own = lax.broadcasted_iota(jnp.int32, (rows, span), 0) + rows
    band = jnp.zeros((rows, span), F32)
    for k in range(nb_ref.shape[1]):
        rel = nb_ref[:, k : k + 1] - base
        wk = w_ref[:, k : k + 1]
        band = band + jnp.where(col == own, wk, 0.0) - jnp.where(col == rel, wk, 0.0)
    hi = band.astype(BF16)
    lo = (band - hi.astype(F32)).astype(BF16)
    out_ref[...] = jnp.dot(hi, window, preferred_element_type=F32) + jnp.dot(
        lo, window, preferred_element_type=F32
    )


def smooth_pass(extended, nb_t, w_t):
    seg_rows = nb_t.shape[0]
    rank = extended.shape[1]
    rows = 128
    return pl.pallas_call(
        smooth_kernel,
        grid=(seg_rows // rows,),
        in_specs=[
            pl.BlockSpec(extended.shape, lambda i: (0, 0), pipeline_mode=pl.Buffered(1)),
            pl.BlockSpec((rows, nb_t.shape[1]), lambda i: (i, 0)),
            pl.BlockSpec((rows, w_t.shape[1]), lambda i: (i, 0)),
        ],
        out_specs=pl.BlockSpec((rows, rank), lambda i: (i, 0)),
        out_shape=jax.ShapeDtypeStruct((seg_rows, rank), F32),
        compiler_params=pltpu.CompilerParams(dimension_semantics=("arbitrary",)),
    )(extended, nb_t, w_t)


def local(
    emb, lengths, pair_block, feats, proj, targets, trip_weight, send_list, nb_index, nb_weight
):
    block_size = lengths.shape[2]
    rank_width = emb.shape[1]
    seg_rows = emb.shape[0]
    block_count = seg_rows // block_size
    regions = lax.axis_size("region")
    blocks = emb.reshape(block_count, block_size, rank_width)
    send_rows = send_list[0, 0]
    live_mask = send_rows >= 0
    slot_count = send_rows.shape[1]
    outgoing = blocks[jnp.where(live_mask, send_rows, 0)]
    incoming = lax.all_to_all(outgoing, "region", split_axis=0, concat_axis=0, tiled=True)
    incoming = incoming.reshape(regions * slot_count, block_size, rank_width)
    trip_blocks = lengths.shape[0]
    trip_query = jnp.einsum("ft,fr->tr", feats, proj, preferred_element_type=jnp.float32)
    query_blocks = trip_query.reshape(trip_blocks, block_size, rank_width)

    pred_rows, slot_grad = trip_pass(
        pair_block.reshape(-1),
        lengths,
        incoming,
        query_blocks,
        targets.reshape(trip_blocks, 1, block_size),
        trip_weight.reshape(trip_blocks, 1, block_size),
    )
    predicted = pred_rows.reshape(trip_blocks * block_size)

    returned = lax.all_to_all(
        slot_grad.reshape(regions, slot_count, block_size, rank_width),
        "region",
        split_axis=0,
        concat_axis=0,
        tiled=True,
    )
    returned = returned.reshape(regions * slot_count, block_size * rank_width)
    target_rows = jnp.where(live_mask, send_rows, -1).reshape(-1)
    onehot = (target_rows[None, :] == jnp.arange(block_count, dtype=jnp.int32)[:, None]).astype(F32)
    owned = jnp.dot(onehot, returned, precision=lax.Precision.HIGHEST, preferred_element_type=F32)
    owned = owned.reshape(seg_rows, rank_width)

    extended = with_halo(emb, (("region", 0),), block_size)
    smoothed = smooth_pass(extended, nb_index[0].T, nb_weight[0].T)
    gradient = lax.psum(owned, "rep") + LAM * smoothed
    return (predicted, gradient.astype(jnp.bfloat16))


def solution(mesh):
    placed = (
        P("region", None),
        P(("region", "rep"), None, None, None),
        P(("region", "rep"), None),
        P(None, ("region", "rep")),
        P(),
        P(("region", "rep")),
        P(("region", "rep")),
        P("region", "rep", None, None),
        P("region", None, None),
        P("region", None, None),
    )
    return jax.shard_map(
        local,
        mesh=mesh,
        in_specs=placed,
        out_specs=(P(("region", "rep")), P("region", None)),
        check_vma=False,
    )
```

time: 857 us -> 539 us (0.63)
  the two profiles are of different devices: /device:TPU:34 before, /device:TPU:13 now
where the time goes in v1:
time: 539 us; the launch traced here: 533 us
  waiting for transfers between devices  370 us (69%)
  Pallas kernels  82.4 us (15%)
  matrix products  22.7 us (4%)
  starting transfers between devices  22.5 us (4%)
  local copies, waits for them, and re-layouts  16.6 us (3%)
  between operations  14.2 us (3%)
    all_to_all x1, waiting for transfers between devices, local(): lax.all_to_all(slot_grad.reshape(regions, slot_count, block_size, rank_wi...  255 us
    all_to_all x1, waiting for transfers between devices, local(): lax.all_to_all(outgoing, 'region', split_axis=0, concat_axis=0, tiled=True)  108 us
    pallas_call x1, Pallas kernels, trip_pass(): pl.pallas_call(functools.partial(trip_kernel, pair_count), grid_spec=pltp...  59.5 us
    pallas_call x1, Pallas kernels, smooth_pass(): pl.pallas_call(smooth_kernel, grid=(seg_rows // rows,), in_specs=[pl.Bloc...  22.9 us
    dot_general x1, matrix products, local(): jnp.dot(onehot, returned, precision=lax.Precision.HIGHEST, preferred_elem...  20.3 us
    all_to_all x1, starting transfers between devices, local(): lax.all_to_all(outgoing, 'region', split_axis=0, concat_axis=0, tiled=True)  11.1 us
  transfers between devices with their start and end apart: 5, of which 3 were waited for; matrix products, arithmetic and copies ran while one was open for 2% of the time, Pallas kernels for 4%

profile of v1, /device:TPU:13, one launch (start us, length us, event | category | flops | bytes accessed | tf_op | source)
XLA Modules:
  0.0 533.2 jit_solution(807001760880009602)
XLA Ops:
  7.2 0.0 copy-start
  7.2 0.7 compare_select_fusion
  7.9 0.1 copy.15
  8.0 0.1 reshape.83
  8.1 9.8 %gather_fusion = bf16[256,128,128]{2,1,0:T(8,128)(2,1)} fusion(bf16[32,128,128]{2,1,0:T(8,128)(2,1)} %bitcast.27, s32[1024]{0:T(1024)S(1)} %pad_clamp_fusion), kind=kCustom, calls=%fused_computation | custom fusion | bytes 16778240 | tf_op jit(solution)/shard_map/gather | solution.py:136
  18.0 11.1 %all-to-all-start = ((bf16[64,4,128,128]{3,2,1,0:T(8,128)(2,1)}), bf16[64,4,128,128]{3,2,1,0:T(8,128)(2,1)}, u32[]{:S(2)}, u32[]{:S(2)}) async-start(bf16[64,4,128,128]{3,2,1,0:T(8,128)(2,1)} %bitcast.28), calls=%async_computation | async-start | bytes 16777216 | tf_op jit(solution)/shard_map/all_to_all | solution.py:137
  29.1 0.1 copy.14
  29.1 0.7 reshape.71.pb_ref
  29.9 0.0 copy-done.7
  29.9 2.3 fusion.5
  32.2 107.9 %all-to-all-done = bf16[64,4,128,128]{3,2,1,0:T(8,128)(2,1)} async-done(((bf16[64,4,128,128]{3,2,1,0:T(8,128)(2,1)}), bf16[64,4,128,128]{3,2,1,0:T(8,128)(2,1)}, u32[]{:S(2)}, u32[]{:S(2)}) %all-to-all-start) | async-done | bytes 8388640 | tf_op jit(solution)/shard_map/all_to_all | solution.py:137
  140.1 59.5 %shard_map.113 = (f32[48,1,128]{2,1,0:T(1,128)}, f32[256,128,128]{2,1,0:T(8,128)}) custom-call(s32[672]{0:T(1024)} %reshape.71.pb_ref, bf16[48,14,128,128]{3,2,1,0:T(8,128)(2,1)} %len_ref.1, bf16[256,128,128]{2,1,0:T(8,128)(2,1)} %bitcast.3.inc_ref, f32[48,128,128]{2,1,0:T(8,128)} %bitcast.30, f32[48,1,128]{2,1,0:T(1,128)} %bitcast.33, f32[48,1,128]{2,1,0:T(1,128)} %bitcast.34), custom_call_target="tpu_custom_call" | custom-call | tf_op jit(solution)/shard_map/pallas_call | solution.py:59
  199.6 9.7 %all-to-all-start.1 = ((f32[64,4,128,128]{3,2,1,0:T(8,128)}), f32[64,4,128,128]{3,2,1,0:T(8,128)}, u32[]{:S(2)}, u32[]{:S(2)}) async-start(f32[64,4,128,128]{3,2,1,0:T(8,128)} %bitcast.29), calls=%async_computation.1 | async-start | bytes 33554432 | tf_op jit(solution)/shard_map/all_to_all | solution.py:153
  209.3 0.2 all-reduce.2.cloned.1.call-start
  209.5 0.1 copy.16
  209.6 0.1 squeeze.12
  209.7 254.7 %all-to-all-done.1 = f32[64,4,128,128]{3,2,1,0:T(8,128)} async-done(((f32[64,4,128,128]{3,2,1,0:T(8,128)}), f32[64,4,128,128]{3,2,1,0:T(8,128)}, u32[]{:S(2)}, u32[]{:S(2)}) %all-to-all-start.1) | async-done | bytes 16777248 | tf_op jit(solution)/shard_map/all_to_all | solution.py:153
  464.5 20.3 %fusion = f32[32,16384]{1,0:T(8,128)S(1)} fusion(f32[32,8,128,128]{3,2,1,0:T(8,128)} %bitcast.18, s32[256]{0:T(256)S(1)} %compare_select_fusion.2), kind=kOutput, calls=%fused_computation.1 | convolution fusion | flops 1610620928 | bytes 18875392 | tf_op jit(solution)/shard_map/dot_general | solution.py:163
  484.8 0.0 copy-start.2
  484.8 0.0 copy-start.3
  484.8 1.5 reshape.80
  486.4 0.0 all-reduce.2.cloned.1.call-update
  486.4 0.1 collective-permute-start.1
  486.5 1.5 collective-permute-start
  487.9 2.0 copy.17
  490.0 2.0 copy.18
  492.0 0.0 collective-permute-done.1
  492.0 0.0 collective-permute-done
  492.0 1.1 pad_maximum_fusion.ext_ref
  493.1 22.9 %shard_map.114 = f32[4096,128]{1,0:T(8,128)} custom-call(bf16[4352,128]{1,0:T(8,128)(2,1)} %pad_maximum_fusion.ext_ref, s32[4096,4]{1,0:T(8,128)} %bitcast.31, f32[4096,4]{1,0:T(8,128)} %bitcast.32), custom_call_target="tpu_custom_call" | custom-call | tf_op jit(solution)/shard_map/pallas_call | solution.py:110
  516.0 7.0 %all-reduce.2.cloned.1.call-done = f32[4096,128]{1,0:T(8,128)} async-done(((f32[4096,128]{1,0:T(8,128)}), f32[4096,128]{1,0:T(8,128)}) %all-reduce.2.cloned.1.call-update) | async-done | bytes 2097168 | tf_op jit(solution)/shard_map/psum | solution.py:168
  523.0 3.4 add_convert_fusion
  (15 shorter events, 0.0 us)
Async XLA Ops:
  7.2 22.7 %copy-start = (bf16[16,6144]{1,0:T(8,128)(2,1)S(1)}, bf16[16,6144]{1,0:T(8,128)(2,1)}, u32[]{:S(2)}) copy-start(bf16[16,6144]{1,0:T(8,128)(2,1)} %param.13) | copy-start | bytes 589828
  18.0 11.1 %copy-start.6 = (s32[48,14]{0,1:T(8,128)S(1)}, s32[48,14]{0,1:T(8,128)}, u32[]{:S(2)}) copy-start(s32[48,14]{0,1:T(8,128)} %param.12) | copy-start | bytes 8068
  18.0 11.9 %copy-start.7 = (bf16[16,128]{1,0:T(8,128)(2,1)S(1)}, bf16[16,128]{1,0:T(8,128)(2,1)}, u32[]{:S(2)}) copy-start(bf16[16,128]{1,0:T(8,128)(2,1)} %param.14) | copy-start | bytes 12292
  18.0 122.1 %all-to-all-start = ((bf16[64,4,128,128]{3,2,1,0:T(8,128)(2,1)}), bf16[64,4,128,128]{3,2,1,0:T(8,128)(2,1)}, u32[]{:S(2)}, u32[]{:S(2)}) async-start(bf16[64,4,128,128]{3,2,1,0:T(8,128)(2,1)} %bitcast.28), calls=%async_computation | async-start | bytes 16777216 | tf_op jit(solution)/shard_map/all_to_all | solution.py:137
  199.6 9.9 %copy-start.5 = (s32[1,1,64,4]{2,3,1,0:T(4,128)S(1)}, s32[1,1,64,4]{2,3,1,0:T(4,128)}, u32[]{:S(2)}) copy-start(s32[1,1,64,4]{2,3,1,0:T(4,128)} %param.17) | copy-start | bytes 3076
  199.6 264.9 %all-to-all-start.1 = ((f32[64,4,128,128]{3,2,1,0:T(8,128)}), f32[64,4,128,128]{3,2,1,0:T(8,128)}, u32[]{:S(2)}, u32[]{:S(2)}) async-start(f32[64,4,128,128]{3,2,1,0:T(8,128)} %bitcast.29), calls=%async_computation.1 | async-start | bytes 33554432 | tf_op jit(solution)/shard_map/all_to_all | solution.py:153
  209.3 313.7 %all-reduce.2.cloned.1.call-start = ((), (), s32[]{:S(2)}) async-start(), calls=%async_computation.2 | async-start | bytes 4194304 | tf_op jit(solution)/shard_map/psum | solution.py:168
  484.8 1.6 copy-start.2
  484.8 3.1 copy-start.3
  486.4 3.6 copy-start.4
  486.4 5.6 %collective-permute-start.1 = (bf16[128,128]{1,0:T(8,128)(2,1)S(1)}, bf16[128,128]{1,0:T(8,128)(2,1)S(1)}, u32[]{:S(2)}, u32[]{:S(2)}) collective-permute-start(bf16[128,128]{1,0:T(8,128)(2,1)S(1)} %get-tuple-element.7), channel_id=1, source_target_pairs={{2,0},{4,2},{6,4},{8,6},{10,8},{12,10},{14,12},{16,14},{18,16},{20... | collective-permute-start | bytes 98312 | tf_op jit(solution)/shard_map/ppermute | solution.py:25
  486.5 5.5 %collective-permute-start = (bf16[128,128]{1,0:T(8,128)(2,1)S(1)}, bf16[128,128]{1,0:T(8,128)(2,1)S(1)}, u32[]{:S(2)}, u32[]{:S(2)}) collective-permute-start(bf16[128,128]{1,0:T(8,128)(2,1)S(1)} %get-tuple-element.6), channel_id=1, source_target_pairs={{0,2},{2,4},{4,6},{6,8},{8,10},{10,12},{12,14},{14,16},{16,18},{18... | collective-permute-start | bytes 98312 | tf_op jit(solution)/shard_map/ppermute | solution.py:23
  493.1 33.3 %copy-start.1 = (bf16[16,6144]{1,0:T(8,128)(2,1)S(1)}, bf16[16,6144]{1,0:T(8,128)(2,1)}, u32[]{:S(2)}) copy-start(bf16[16,6144]{1,0:T(8,128)(2,1)} %param.13) | copy-start | bytes 589828
Sparse Core Ops, SparseCore 0:
  486.5 36.4 all-reduce.1

commit v2 on v1

v2 whole, which is shorter than its diff:
```python
import functools

import jax
import jax.numpy as jnp
from jax import lax
from jax.experimental import pallas as pl
from jax.experimental.pallas import tpu as pltpu
from jax.sharding import PartitionSpec as P

LAM = 0.25
F32 = jnp.float32
BF16 = jnp.bfloat16


def trip_kernel(pair_count, pb_ref, len_ref, inc_ref, qt_ref, tgt_ref, w_ref, pred_ref, acc_ref):
    t = pl.program_id(0)

    @pl.when(t == 0)
    def _():
        acc_ref[...] = jnp.zeros_like(acc_ref)

    hidden = None
    for k in range(pair_count):
        p = pb_ref[t * pair_count + k]
        term = jnp.dot(len_ref[0, k], inc_ref[p], preferred_element_type=F32)
        hidden = term if hidden is None else hidden + term
    q_t = qt_ref[...]
    pred_row = jnp.sum(hidden.T * q_t, axis=0, keepdims=True)
    pred_ref[0] = pred_row
    err_row = w_ref[0] * (pred_row - tgt_ref[0])
    scaled_t = (err_row * q_t).astype(BF16)
    for k in range(pair_count):
        p = pb_ref[t * pair_count + k]
        acc_ref[p] += jnp.dot(scaled_t, len_ref[0, k], preferred_element_type=F32)


def trip_pass(pair_flat, lengths, incoming, query_t, tgt, wts):
    trip_blocks, pair_count, block, rank = lengths.shape
    slots = incoming.shape[0]
    const3 = lambda t, pb: (0, 0, 0)
    return pl.pallas_call(
        functools.partial(trip_kernel, pair_count),
        grid_spec=pltpu.PrefetchScalarGridSpec(
            num_scalar_prefetch=1,
            grid=(trip_blocks,),
            in_specs=[
                pl.BlockSpec((1, pair_count, block, block), lambda t, pb: (t, 0, 0, 0)),
                pl.BlockSpec((slots, block, rank), const3, pipeline_mode=pl.Buffered(1)),
                pl.BlockSpec((rank, block), lambda t, pb: (0, t)),
                pl.BlockSpec((1, 1, block), lambda t, pb: (t, 0, 0)),
                pl.BlockSpec((1, 1, block), lambda t, pb: (t, 0, 0)),
            ],
            out_specs=[
                pl.BlockSpec((1, 1, block), lambda t, pb: (t, 0, 0)),
                pl.BlockSpec((slots, block, rank), const3, pipeline_mode=pl.Buffered(1)),
            ],
        ),
        out_shape=[
            jax.ShapeDtypeStruct((trip_blocks, 1, block), F32),
            jax.ShapeDtypeStruct((slots, block, rank), F32),
        ],
        compiler_params=pltpu.CompilerParams(
            dimension_semantics=("arbitrary",), vmem_limit_bytes=60 * 1024 * 1024
        ),
    )(pair_flat, lengths, incoming, query_t, tgt, wts)


def band_of(nb_ref, w_ref, base, rows):
    span = 3 * rows
    col = lax.broadcasted_iota(jnp.int32, (rows, span), 1)
    own = lax.broadcasted_iota(jnp.int32, (rows, span), 0) + rows
    band = jnp.zeros((rows, span), F32)
    for k in range(nb_ref.shape[1]):
        rel = nb_ref[:, k : k + 1] - base
        wk = w_ref[:, k : k + 1]
        band = band + jnp.where(col == own, wk, 0.0) - jnp.where(col == rel, wk, 0.0)
    hi = band.astype(BF16)
    lo = (band - hi.astype(F32)).astype(BF16)
    return hi, lo


def apply_band(hi, lo, window):
    return jnp.dot(hi, window, preferred_element_type=F32) + jnp.dot(
        lo, window, preferred_element_type=F32
    )


def smooth_inner_kernel(emb_ref, nb_ref, w_ref, out_ref):
    rows = out_ref.shape[0]
    i = pl.program_id(0) + 1
    hi, lo = band_of(nb_ref, w_ref, i * rows, rows)
    window = emb_ref[pl.ds(pl.multiple_of((i - 1) * rows, rows), 3 * rows), :]
    out_ref[...] = apply_band(hi, lo, window)


def smooth_edge_kernel(last, win_ref, nb_ref, w_ref, out_ref):
    rows = out_ref.shape[0]
    i = pl.program_id(0) * last
    hi, lo = band_of(nb_ref, w_ref, i * rows, rows)
    out_ref[...] = apply_band(hi, lo, win_ref[0])


def smooth_inner(emb, nb_t, w_t, rows):
    seg_rows, rank = emb.shape
    inner = seg_rows // rows - 2
    return pl.pallas_call(
        smooth_inner_kernel,
        grid=(inner,),
        in_specs=[
            pl.BlockSpec(emb.shape, lambda i: (0, 0), pipeline_mode=pl.Buffered(1)),
            pl.BlockSpec((rows, nb_t.shape[1]), lambda i: (i + 1, 0)),
            pl.BlockSpec((rows, w_t.shape[1]), lambda i: (i + 1, 0)),
        ],
        out_specs=pl.BlockSpec((rows, rank), lambda i: (i, 0)),
        out_shape=jax.ShapeDtypeStruct((inner * rows, rank), F32),
        compiler_params=pltpu.CompilerParams(dimension_semantics=("arbitrary",)),
    )(emb, nb_t, w_t)


def smooth_edge(windows, nb_t, w_t, rows):
    rank = windows.shape[2]
    last = nb_t.shape[0] // rows - 1
    return pl.pallas_call(
        functools.partial(smooth_edge_kernel, last),
        grid=(2,),
        in_specs=[
            pl.BlockSpec((1,) + windows.shape[1:], lambda i: (i, 0, 0)),
            pl.BlockSpec((rows, nb_t.shape[1]), lambda i: (i * last, 0)),
            pl.BlockSpec((rows, w_t.shape[1]), lambda i: (i * last, 0)),
        ],
        out_specs=pl.BlockSpec((rows, rank), lambda i: (i, 0)),
        out_shape=jax.ShapeDtypeStruct((2 * rows, rank), F32),
        compiler_params=pltpu.CompilerParams(dimension_semantics=("arbitrary",)),
    )(windows, nb_t, w_t)


def owned_kernel(tgt_ref, ret_ref, out_ref, acc_ref):
    c = pl.program_id(0)
    chunk = ret_ref.shape[0]

    @pl.when(c == 0)
    def _():
        acc_ref[...] = jnp.zeros_like(acc_ref)

    for s in range(chunk):
        b = tgt_ref[c * chunk + s]

        @pl.when(b >= 0)
        def _():
            acc_ref[b] += ret_ref[s]

    @pl.when(c == pl.num_programs(0) - 1)
    def _():
        for b in range(acc_ref.shape[0]):
            out_ref[b] = acc_ref[b].T


def owned_pass(targets, returned, block_count, chunk=32):
    slots, rank, block = returned.shape
    return pl.pallas_call(
        owned_kernel,
        grid_spec=pltpu.PrefetchScalarGridSpec(
            num_scalar_prefetch=1,
            grid=(slots // chunk,),
            in_specs=[pl.BlockSpec((chunk, rank, block), lambda c, tg: (c, 0, 0))],
            out_specs=pl.BlockSpec(
                (block_count, block, rank), lambda c, tg: (0, 0, 0), pipeline_mode=pl.Buffered(1)
            ),
            scratch_shapes=[pltpu.VMEM((block_count, rank, block), F32)],
        ),
        out_shape=jax.ShapeDtypeStruct((block_count, block, rank), F32),
        compiler_params=pltpu.CompilerParams(dimension_semantics=("arbitrary",)),
    )(targets, returned)


def local(
    emb, lengths, pair_block, feats, proj, targets, trip_weight, send_list, nb_index, nb_weight
):
    block_size = lengths.shape[2]
    rank_width = emb.shape[1]
    seg_rows = emb.shape[0]
    block_count = seg_rows // block_size
    regions = lax.axis_size("region")
    blocks = emb.reshape(block_count, block_size, rank_width)
    send_rows = send_list[0, 0]
    live_mask = send_rows >= 0
    slot_count = send_rows.shape[1]
    outgoing = blocks[jnp.where(live_mask, send_rows, 0)]
    incoming = lax.all_to_all(outgoing, "region", split_axis=0, concat_axis=0, tiled=True)
    incoming = incoming.reshape(regions * slot_count, block_size, rank_width)
    trip_blocks = lengths.shape[0]
    query_t = jnp.einsum("fr,ft->rt", proj, feats, preferred_element_type=F32)

    nb_t = nb_index[0].T
    w_t = nb_weight[0].T
    inner = smooth_inner(emb, nb_t, w_t, block_size)

    pred_rows, slot_grad = trip_pass(
        pair_block.reshape(-1),
        lengths,
        incoming,
        query_t,
        targets.reshape(trip_blocks, 1, block_size),
        trip_weight.reshape(trip_blocks, 1, block_size),
    )
    predicted = pred_rows.reshape(trip_blocks * block_size)

    returned = lax.all_to_all(
        slot_grad.reshape(regions, slot_count, rank_width, block_size),
        "region",
        split_axis=0,
        concat_axis=0,
        tiled=True,
    )
    returned = returned.reshape(regions * slot_count, rank_width, block_size)

    count = regions
    head = emb[:block_size]
    tail = emb[seg_rows - block_size :]
    prev_tail = lax.ppermute(tail, "region", [(i, (i + 1) % count) for i in range(count)])
    next_head = lax.ppermute(head, "region", [((i + 1) % count, i) for i in range(count)])
    windows = jnp.stack(
        [
            jnp.concatenate([prev_tail, emb[: 2 * block_size]], axis=0),
            jnp.concatenate([emb[seg_rows - 2 * block_size :], next_head], axis=0),
        ]
    )
    edge = smooth_edge(windows, nb_t, w_t, block_size)
    smoothed = jnp.concatenate([edge[:block_size], inner, edge[block_size:]], axis=0)

    target_rows = jnp.where(live_mask, send_rows, -1).reshape(-1)
    owned = owned_pass(target_rows, returned, block_count).reshape(seg_rows, rank_width)
    partner = lax.ppermute(owned, "rep", [(0, 1), (1, 0)])
    gradient = (owned + partner) + LAM * smoothed
    return (predicted, gradient.astype(jnp.bfloat16))


def solution(mesh):
    placed = (
        P("region", None),
        P(("region", "rep"), None, None, None),
        P(("region", "rep"), None),
        P(None, ("region", "rep")),
        P(),
        P(("region", "rep")),
        P(("region", "rep")),
        P("region", "rep", None, None),
        P("region", None, None),
        P("region", None, None),
    )
    return jax.shard_map(
        local,
        mesh=mesh,
        in_specs=placed,
        out_specs=(P(("region", "rep")), P("region", None)),
        check_vma=False,
    )
```

time: 539 us -> 505 us (0.937)
  the two profiles are of different devices: /device:TPU:13 before, /device:TPU:3 now
where the time goes in v2:
time: 505 us; the launch traced here: 502 us
  waiting for transfers between devices  342 us (68%)
  Pallas kernels  93.2 us (18%)
  starting transfers between devices  41.2 us (8%)
  local copies, waits for them, and re-layouts  17.6 us (3%)
  other arithmetic  5.49 us (1%)
    all_to_all x1, waiting for transfers between devices, local(): lax.all_to_all(slot_grad.reshape(regions, slot_count, rank_width, block_s...  234 us
    all_to_all x1, waiting for transfers between devices, local(): lax.all_to_all(outgoing, 'region', split_axis=0, concat_axis=0, tiled=True)  108 us
    pallas_call x1, Pallas kernels, trip_pass(): pl.pallas_call(functools.partial(trip_kernel, pair_count), grid_spec=pltp...  57.3 us
    pallas_call x1, Pallas kernels, smooth_inner(): pl.pallas_call(smooth_inner_kernel, grid=(inner,), in_specs=[pl.BlockSpec...  21.5 us
    ppermute x1, starting transfers between devices, local(): lax.ppermute(tail, 'region', [(i, (i + 1) % count) for i in range(count)])  15.8 us
    pallas_call x1, Pallas kernels, owned_pass(): pl.pallas_call(owned_kernel, grid_spec=pltpu.PrefetchScalarGridSpec(num_s...  11.8 us
    all_to_all x1, starting transfers between devices, local(): lax.all_to_all(outgoing, 'region', split_axis=0, concat_axis=0, tiled=True)  11.3 us
  transfers between devices with their start and end apart: 5, of which 2 were waited for; matrix products, arithmetic and copies ran while one was open for 2% of the time, Pallas kernels for 5%

profile of v2, /device:TPU:3, one launch (start us, length us, event | category | flops | bytes accessed | tf_op | source)
XLA Modules:
  0.0 502.2 jit_solution(8512958128193800914)
XLA Ops:
  0.6 0.0 copy-start
  0.6 0.7 compare_select_fusion
  1.4 0.1 copy.15
  1.5 0.1 reshape.72
  1.6 9.7 %gather_fusion = bf16[256,128,128]{2,1,0:T(8,128)(2,1)} fusion(bf16[32,128,128]{2,1,0:T(8,128)(2,1)} %bitcast.28, s32[1024]{0:T(1024)S(1)} %pad_clamp_fusion), kind=kCustom, calls=%fused_computation | custom fusion | bytes 16778240 | tf_op jit(solution)/shard_map/gather | solution.py:188
  11.3 11.3 %all-to-all-start = ((bf16[64,4,128,128]{3,2,1,0:T(8,128)(2,1)}), bf16[64,4,128,128]{3,2,1,0:T(8,128)(2,1)}, u32[]{:S(2)}, u32[]{:S(2)}) async-start(bf16[64,4,128,128]{3,2,1,0:T(8,128)(2,1)} %bitcast.29), calls=%async_computation | async-start | bytes 16777216 | tf_op jit(solution)/shard_map/all_to_all | solution.py:189
  22.6 0.1 copy.14
  22.7 0.7 reshape.61.pb_ref
  23.4 2.3 fusion.5.qt_ref
  25.7 108.0 %all-to-all-done = bf16[64,4,128,128]{3,2,1,0:T(8,128)(2,1)} async-done(((bf16[64,4,128,128]{3,2,1,0:T(8,128)(2,1)}), bf16[64,4,128,128]{3,2,1,0:T(8,128)(2,1)}, u32[]{:S(2)}, u32[]{:S(2)}) %all-to-all-start) | async-done | bytes 8388640 | tf_op jit(solution)/shard_map/all_to_all | solution.py:189
  133.7 57.3 %shard_map.113 = (f32[48,1,128]{2,1,0:T(1,128)}, f32[256,128,128]{2,1,0:T(8,128)}) custom-call(s32[672]{0:T(1024)} %reshape.61.pb_ref, bf16[48,14,128,128]{3,2,1,0:T(8,128)(2,1)} %len_ref.1, bf16[256,128,128]{2,1,0:T(8,128)(2,1)} %bitcast.3.inc_ref, f32[128,6144]{1,0:T(8,128)} %fusion.5.qt_ref, f32[48,1,128]{2,1,0:T(1,128)} %bitcast.36, f32[48,1,128]{2,1,0:T(1,128)} %bitcast.37), custom_call_target="tpu_custom_call" | custom-call | tf_op jit(solution)/shard_map/pallas_call | solution.py:41
  191.0 9.4 %all-to-all-start.1 = ((f32[64,4,128,128]{3,2,1,0:T(8,128)}), f32[64,4,128,128]{3,2,1,0:T(8,128)}, u32[]{:S(2)}, u32[]{:S(2)}) async-start(f32[64,4,128,128]{3,2,1,0:T(8,128)} %bitcast.34), calls=%async_computation.1 | async-start | bytes 33554432 | tf_op jit(solution)/shard_map/all_to_all | solution.py:208
  200.4 0.1 copy.16
  200.5 0.1 squeeze.12
  200.6 0.6 compare_select_fusion.2.tgt_ref
  201.2 233.8 %all-to-all-done.1 = f32[64,4,128,128]{3,2,1,0:T(8,128)} async-done(((f32[64,4,128,128]{3,2,1,0:T(8,128)}), f32[64,4,128,128]{3,2,1,0:T(8,128)}, u32[]{:S(2)}, u32[]{:S(2)}) %all-to-all-start.1) | async-done | bytes 16777248 | tf_op jit(solution)/shard_map/all_to_all | solution.py:208
  435.0 11.8 %shard_map.114 = f32[32,128,128]{2,1,0:T(8,128)} custom-call(s32[256]{0:T(256)} %compare_select_fusion.2.tgt_ref, f32[256,128,128]{2,1,0:T(8,128)} %bitcast.8.ret_ref), custom_call_target="tpu_custom_call" | custom-call | tf_op jit(solution)/shard_map/pallas_call | solution.py:160
  446.8 4.7 collective-permute-start
  451.5 0.8 fusion.2
  452.3 15.8 %collective-permute-start.1 = (bf16[128,128]{1,0:T(8,128)(2,1)S(1)}, bf16[128,128]{1,0:T(8,128)(2,1)S(1)}, u32[]{:S(2)}, u32[]{:S(2)}) collective-permute-start(bf16[128,128]{1,0:T(8,128)(2,1)S(1)} %get-tuple-element.6), channel_id=1, source_target_pairs={{0,2},{2,4},{4,6},{6,8},{8,10},{10,12},{12,14},{14,16},{16,18},{18... | collective-permute-start | bytes 98312 | tf_op jit(solution)/shard_map/ppermute | solution.py:220
  468.1 0.0 collective-permute-start.2
  468.1 0.9 fusion.3
  469.0 2.0 copy.17
  471.0 2.0 copy.18
  473.1 21.5 %shard_map.116 = f32[3840,128]{1,0:T(8,128)} custom-call(bf16[4096,128]{1,0:T(8,128)(2,1)} %emb_ref.1, s32[4096,4]{1,0:T(8,128)} %bitcast.30, f32[4096,4]{1,0:T(8,128)} %bitcast.32), custom_call_target="tpu_custom_call" | custom-call | tf_op jit(solution)/shard_map/pallas_call | solution.py:106
  494.6 0.0 collective-permute-done.1
  494.6 0.7 pad_maximum_fusion.win_ref
  495.3 2.5 shard_map.115
  497.8 0.9 fusion.4
  498.7 0.0 collective-permute-done
  498.7 0.0 copy-start.1
  498.8 3.5 fusion.1
  (18 shorter events, 0.1 us)
Async XLA Ops:
  0.6 22.8 %copy-start = (bf16[16,6144]{1,0:T(8,128)(2,1)S(1)}, bf16[16,6144]{1,0:T(8,128)(2,1)}, u32[]{:S(2)}) copy-start(bf16[16,6144]{1,0:T(8,128)(2,1)} %param.13) | copy-start | bytes 589828
  11.3 11.3 %copy-start.6 = (s32[48,14]{0,1:T(8,128)S(1)}, s32[48,14]{0,1:T(8,128)}, u32[]{:S(2)}) copy-start(s32[48,14]{0,1:T(8,128)} %param.12) | copy-start | bytes 8068
  11.3 12.1 %copy-start.7 = (bf16[16,128]{1,0:T(8,128)(2,1)S(1)}, bf16[16,128]{1,0:T(8,128)(2,1)}, u32[]{:S(2)}) copy-start(bf16[16,128]{1,0:T(8,128)(2,1)} %param.14) | copy-start | bytes 12292
  11.3 122.4 %all-to-all-start = ((bf16[64,4,128,128]{3,2,1,0:T(8,128)(2,1)}), bf16[64,4,128,128]{3,2,1,0:T(8,128)(2,1)}, u32[]{:S(2)}, u32[]{:S(2)}) async-start(bf16[64,4,128,128]{3,2,1,0:T(8,128)(2,1)} %bitcast.29), calls=%async_computation | async-start | bytes 16777216 | tf_op jit(solution)/shard_map/all_to_all | solution.py:189
  191.0 9.4 %copy-start.5 = (s32[1,1,64,4]{2,3,1,0:T(4,128)S(1)}, s32[1,1,64,4]{2,3,1,0:T(4,128)}, u32[]{:S(2)}) copy-start(s32[1,1,64,4]{2,3,1,0:T(4,128)} %param.17) | copy-start | bytes 3076
  191.0 244.0 %all-to-all-start.1 = ((f32[64,4,128,128]{3,2,1,0:T(8,128)}), f32[64,4,128,128]{3,2,1,0:T(8,128)}, u32[]{:S(2)}, u32[]{:S(2)}) async-start(f32[64,4,128,128]{3,2,1,0:T(8,128)} %bitcast.34), calls=%async_computation.1 | async-start | bytes 33554432 | tf_op jit(solution)/shard_map/all_to_all | solution.py:208
  435.0 34.0 %copy-start.3 = (s32[1,4,4096]{2,1,0:T(4,128)S(1)}, s32[1,4,4096]{2,1,0:T(4,128)}, u32[]{:S(2)}) copy-start(s32[1,4,4096]{2,1,0:T(4,128)} %param.18) | copy-start | bytes 196612
  446.8 24.2 %copy-start.4 = (f32[1,4,4096]{2,1,0:T(4,128)S(1)}, f32[1,4,4096]{2,1,0:T(4,128)}, u32[]{:S(2)}) copy-start(f32[1,4,4096]{2,1,0:T(4,128)} %param.19) | copy-start | bytes 196612
  446.8 51.9 %collective-permute-start = (f32[4096,128]{1,0:T(8,128)}, f32[4096,128]{1,0:T(8,128)}, u32[]{:S(2)}, u32[]{:S(2)}) collective-permute-start(f32[4096,128]{1,0:T(8,128)} %bitcast.35), channel_id=1, source_target_pairs={{0,1},{1,0},{2,3},{3,2},{4,5},{5,4},{6,7},{7,6},{8,9},{9,8},{10,11... | collective-permute-start | bytes 6291464 | tf_op jit(solution)/shard_map/ppermute | solution.py:233
  452.3 42.3 %collective-permute-start.1 = (bf16[128,128]{1,0:T(8,128)(2,1)S(1)}, bf16[128,128]{1,0:T(8,128)(2,1)S(1)}, u32[]{:S(2)}, u32[]{:S(2)}) collective-permute-start(bf16[128,128]{1,0:T(8,128)(2,1)S(1)} %get-tuple-element.6), channel_id=1, source_target_pairs={{0,2},{2,4},{4,6},{6,8},{8,10},{10,12},{12,14},{14,16},{16,18},{18... | collective-permute-start | bytes 98312 | tf_op jit(solution)/shard_map/ppermute | solution.py:220
  468.1 26.4 %collective-permute-start.2 = (bf16[128,128]{1,0:T(8,128)(2,1)S(1)}, bf16[128,128]{1,0:T(8,128)(2,1)S(1)}, u32[]{:S(2)}, u32[]{:S(2)}) collective-permute-start(bf16[128,128]{1,0:T(8,128)(2,1)S(1)} %get-tuple-element.7), channel_id=1, source_target_pairs={{2,0},{4,2},{6,4},{8,6},{10,8},{12,10},{14,12},{16,14},{18,16},{20... | collective-permute-start | bytes 98312 | tf_op jit(solution)/shard_map/ppermute | solution.py:221
  495.3 3.5 copy-start.2
  498.7 3.5 copy-start.1

commit v3 on v2

--- a/solution.py
+++ b/solution.py
@@ -12,7 +12,9 @@
 BF16 = jnp.bfloat16
 
 
-def trip_kernel(pair_count, pb_ref, len_ref, inc_ref, qt_ref, tgt_ref, w_ref, pred_ref, acc_ref):
+def trip_kernel(
+    pair_count, pb_ref, len_ref, inc_ref, qt_ref, tgt_ref, w_ref, pred_ref, out_ref, acc_ref
+):
     t = pl.program_id(0)
 
     @pl.when(t == 0)
@@ -32,6 +34,10 @@
     for k in range(pair_count):
         p = pb_ref[t * pair_count + k]
         acc_ref[p] += jnp.dot(scaled_t, len_ref[0, k], preferred_element_type=F32)
+
+    @pl.when(t == pl.num_programs(0) - 1)
+    def _():
+        out_ref[...] = acc_ref[...].astype(out_ref.dtype)
 
 
 def trip_pass(pair_flat, lengths, incoming, query_t, tgt, wts):
@@ -54,10 +60,11 @@
                 pl.BlockSpec((1, 1, block), lambda t, pb: (t, 0, 0)),
                 pl.BlockSpec((slots, block, rank), const3, pipeline_mode=pl.Buffered(1)),
             ],
+            scratch_shapes=[pltpu.VMEM((slots, block, rank), F32)],
         ),
         out_shape=[
             jax.ShapeDtypeStruct((trip_blocks, 1, block), F32),
-            jax.ShapeDtypeStruct((slots, block, rank), F32),
+            jax.ShapeDtypeStruct((slots, block, rank), BF16),
         ],
         compiler_params=pltpu.CompilerParams(
             dimension_semantics=("arbitrary",), vmem_limit_bytes=60 * 1024 * 1024
@@ -147,7 +154,7 @@
 
         @pl.when(b >= 0)
         def _():
-            acc_ref[b] += ret_ref[s]
+            acc_ref[b] += ret_ref[s].astype(F32)
 
     @pl.when(c == pl.num_programs(0) - 1)
     def _():

time: 505 us -> 372 us (0.74)
  the two profiles are of different devices: /device:TPU:3 before, /device:TPU:13 now
where the time goes in v3:
time: 372 us; the launch traced here: 369 us
  waiting for transfers between devices  223 us (60%)
  Pallas kernels  89.6 us (24%)
  starting transfers between devices  30.4 us (8%)
  local copies, waits for them, and re-layouts  17.5 us (5%)
  other arithmetic  5.49 us (1%)
    all_to_all x1, waiting for transfers between devices, local(): lax.all_to_all(slot_grad.reshape(regions, slot_count, rank_width, block_s...  115 us
    all_to_all x1, waiting for transfers between devices, local(): lax.all_to_all(outgoing, 'region', split_axis=0, concat_axis=0, tiled=True)  108 us
    pallas_call x1, Pallas kernels, trip_pass(): pl.pallas_call(functools.partial(trip_kernel, pair_count), grid_spec=pltp...  55.7 us
    pallas_call x1, Pallas kernels, smooth_inner(): pl.pallas_call(smooth_inner_kernel, grid=(inner,), in_specs=[pl.BlockSpec...  21.5 us
    all_to_all x1, starting transfers between devices, local(): lax.all_to_all(outgoing, 'region', split_axis=0, concat_axis=0, tiled=True)  11.2 us
    pallas_call x1, Pallas kernels, owned_pass(): pl.pallas_call(owned_kernel, grid_spec=pltpu.PrefetchScalarGridSpec(num_s...  9.88 us
    gather x1, local copies, waits for them, and re-layouts, local(): outgoing = blocks[jnp.where(live_mask, send_rows, 0)]  9.77 us
    all_to_all x1, starting transfers between devices, local(): lax.all_to_all(slot_grad.reshape(regions, slot_count, rank_width, block_s...  9.66 us
  transfers between devices with their start and end apart: 5, of which 2 were waited for; matrix products, arithmetic and copies ran while one was open for 3% of the time, Pallas kernels for 7%

profile of v3, /device:TPU:13, one launch (start us, length us, event | category | flops | bytes accessed | tf_op | source)
XLA Modules:
  0.0 368.5 jit_solution(9345944672010073197)
XLA Ops:
  0.6 0.0 copy-start
  0.6 0.7 compare_select_fusion
  1.4 0.1 copy.15
  1.5 0.1 reshape.72
  1.6 9.8 %gather_fusion = bf16[256,128,128]{2,1,0:T(8,128)(2,1)} fusion(bf16[32,128,128]{2,1,0:T(8,128)(2,1)} %bitcast.28, s32[1024]{0:T(1024)S(1)} %pad_clamp_fusion), kind=kCustom, calls=%fused_computation | custom fusion | bytes 16778240 | tf_op jit(solution)/shard_map/gather | solution.py:195
  11.4 11.2 %all-to-all-start = ((bf16[64,4,128,128]{3,2,1,0:T(8,128)(2,1)}), bf16[64,4,128,128]{3,2,1,0:T(8,128)(2,1)}, u32[]{:S(2)}, u32[]{:S(2)}) async-start(bf16[64,4,128,128]{3,2,1,0:T(8,128)(2,1)} %bitcast.29), calls=%async_computation | async-start | bytes 16777216 | tf_op jit(solution)/shard_map/all_to_all | solution.py:196
  22.5 0.1 copy.14
  22.6 0.7 reshape.61.pb_ref
  23.3 2.2 fusion.5.qt_ref
  25.6 107.9 %all-to-all-done = bf16[64,4,128,128]{3,2,1,0:T(8,128)(2,1)} async-done(((bf16[64,4,128,128]{3,2,1,0:T(8,128)(2,1)}), bf16[64,4,128,128]{3,2,1,0:T(8,128)(2,1)}, u32[]{:S(2)}, u32[]{:S(2)}) %all-to-all-start) | async-done | bytes 8388640 | tf_op jit(solution)/shard_map/all_to_all | solution.py:196
  133.5 55.7 %shard_map.113 = (f32[48,1,128]{2,1,0:T(1,128)}, bf16[256,128,128]{2,1,0:T(8,128)(2,1)}) custom-call(s32[672]{0:T(1024)} %reshape.61.pb_ref, bf16[48,14,128,128]{3,2,1,0:T(8,128)(2,1)} %len_ref.1, bf16[256,128,128]{2,1,0:T(8,128)(2,1)} %bitcast.3.inc_ref, f32[128,6144]{1,0:T(8,128)} %fusion.5.qt_ref, f32[48,1,128]{2,1,0:T(1,128)} %bitcast.36, ...), custom_call_target="tpu_custom_call" | custom-call | tf_op jit(solution)/shard_map/pallas_call | solution.py:47
  189.2 9.7 %all-to-all-start.1 = ((bf16[64,4,128,128]{3,2,1,0:T(8,128)(2,1)}), bf16[64,4,128,128]{3,2,1,0:T(8,128)(2,1)}, u32[]{:S(2)}, u32[]{:S(2)}) async-start(bf16[64,4,128,128]{3,2,1,0:T(8,128)(2,1)} %bitcast.34), calls=%async_computation.1 | async-start | bytes 16777216 | tf_op jit(solution)/shard_map/all_to_all | solution.py:215
  198.8 0.1 copy.16
  198.9 0.1 squeeze.12
  199.0 0.6 compare_select_fusion.2.tgt_ref
  199.6 114.6 %all-to-all-done.1 = bf16[64,4,128,128]{3,2,1,0:T(8,128)(2,1)} async-done(((bf16[64,4,128,128]{3,2,1,0:T(8,128)(2,1)}), bf16[64,4,128,128]{3,2,1,0:T(8,128)(2,1)}, u32[]{:S(2)}, u32[]{:S(2)}) %all-to-all-start.1) | async-done | bytes 8388640 | tf_op jit(solution)/shard_map/all_to_all | solution.py:215
  314.3 9.9 %shard_map.114 = f32[32,128,128]{2,1,0:T(8,128)} custom-call(s32[256]{0:T(256)} %compare_select_fusion.2.tgt_ref, bf16[256,128,128]{2,1,0:T(8,128)(2,1)} %bitcast.8.ret_ref), custom_call_target="tpu_custom_call" | custom-call | tf_op jit(solution)/shard_map/pallas_call | solution.py:167
  324.1 5.3 %collective-permute-start = (f32[4096,128]{1,0:T(8,128)}, f32[4096,128]{1,0:T(8,128)}, u32[]{:S(2)}, u32[]{:S(2)}) collective-permute-start(f32[4096,128]{1,0:T(8,128)} %bitcast.35), channel_id=1, source_target_pairs={{0,1},{1,0},{2,3},{3,2},{4,5},{5,4},{6,7},{7,6},{8,9},{9,8},{10,11... | collective-permute-start | bytes 6291464 | tf_op jit(solution)/shard_map/ppermute | solution.py:240
  329.5 0.8 fusion.2
  330.3 0.0 collective-permute-start.2
  330.3 4.2 %collective-permute-start.1 = (bf16[128,128]{1,0:T(8,128)(2,1)S(1)}, bf16[128,128]{1,0:T(8,128)(2,1)S(1)}, u32[]{:S(2)}, u32[]{:S(2)}) collective-permute-start(bf16[128,128]{1,0:T(8,128)(2,1)S(1)} %get-tuple-element.6), channel_id=1, source_target_pairs={{0,2},{2,4},{4,6},{6,8},{8,10},{10,12},{12,14},{14,16},{16,18},{18... | collective-permute-start | bytes 98312 | tf_op jit(solution)/shard_map/ppermute | solution.py:227
  334.5 0.9 fusion.3
  335.4 2.0 copy.17
  337.3 2.0 copy.18
  339.4 21.5 %shard_map.116 = f32[3840,128]{1,0:T(8,128)} custom-call(bf16[4096,128]{1,0:T(8,128)(2,1)} %emb_ref.1, s32[4096,4]{1,0:T(8,128)} %bitcast.30, f32[4096,4]{1,0:T(8,128)} %bitcast.32), custom_call_target="tpu_custom_call" | custom-call | tf_op jit(solution)/shard_map/pallas_call | solution.py:113
  360.9 0.0 collective-permute-done.1
  360.9 0.7 pad_maximum_fusion.win_ref
  361.6 2.5 shard_map.115
  364.1 0.9 fusion.4
  365.0 0.0 collective-permute-done
  365.0 0.0 copy-start.1
  365.1 3.5 fusion.1
  (18 shorter events, 0.1 us)
Async XLA Ops:
  0.6 22.7 %copy-start = (bf16[16,6144]{1,0:T(8,128)(2,1)S(1)}, bf16[16,6144]{1,0:T(8,128)(2,1)}, u32[]{:S(2)}) copy-start(bf16[16,6144]{1,0:T(8,128)(2,1)} %param.13) | copy-start | bytes 589828
  11.4 11.2 %copy-start.6 = (s32[48,14]{0,1:T(8,128)S(1)}, s32[48,14]{0,1:T(8,128)}, u32[]{:S(2)}) copy-start(s32[48,14]{0,1:T(8,128)} %param.12) | copy-start | bytes 8068
  11.4 12.0 %copy-start.7 = (bf16[16,128]{1,0:T(8,128)(2,1)S(1)}, bf16[16,128]{1,0:T(8,128)(2,1)}, u32[]{:S(2)}) copy-start(bf16[16,128]{1,0:T(8,128)(2,1)} %param.14) | copy-start | bytes 12292
  11.4 122.1 %all-to-all-start = ((bf16[64,4,128,128]{3,2,1,0:T(8,128)(2,1)}), bf16[64,4,128,128]{3,2,1,0:T(8,128)(2,1)}, u32[]{:S(2)}, u32[]{:S(2)}) async-start(bf16[64,4,128,128]{3,2,1,0:T(8,128)(2,1)} %bitcast.29), calls=%async_computation | async-start | bytes 16777216 | tf_op jit(solution)/shard_map/all_to_all | solution.py:196
  189.2 9.7 %copy-start.5 = (s32[1,1,64,4]{2,3,1,0:T(4,128)S(1)}, s32[1,1,64,4]{2,3,1,0:T(4,128)}, u32[]{:S(2)}) copy-start(s32[1,1,64,4]{2,3,1,0:T(4,128)} %param.17) | copy-start | bytes 3076
  189.2 125.1 %all-to-all-start.1 = ((bf16[64,4,128,128]{3,2,1,0:T(8,128)(2,1)}), bf16[64,4,128,128]{3,2,1,0:T(8,128)(2,1)}, u32[]{:S(2)}, u32[]{:S(2)}) async-start(bf16[64,4,128,128]{3,2,1,0:T(8,128)(2,1)} %bitcast.34), calls=%async_computation.1 | async-start | bytes 16777216 | tf_op jit(solution)/shard_map/all_to_all | solution.py:215
  314.3 21.1 %copy-start.3 = (s32[1,4,4096]{2,1,0:T(4,128)S(1)}, s32[1,4,4096]{2,1,0:T(4,128)}, u32[]{:S(2)}) copy-start(s32[1,4,4096]{2,1,0:T(4,128)} %param.18) | copy-start | bytes 196612
  324.1 13.2 %copy-start.4 = (f32[1,4,4096]{2,1,0:T(4,128)S(1)}, f32[1,4,4096]{2,1,0:T(4,128)}, u32[]{:S(2)}) copy-start(f32[1,4,4096]{2,1,0:T(4,128)} %param.19) | copy-start | bytes 196612
  324.1 40.9 %collective-permute-start = (f32[4096,128]{1,0:T(8,128)}, f32[4096,128]{1,0:T(8,128)}, u32[]{:S(2)}, u32[]{:S(2)}) collective-permute-start(f32[4096,128]{1,0:T(8,128)} %bitcast.35), channel_id=1, source_target_pairs={{0,1},{1,0},{2,3},{3,2},{4,5},{5,4},{6,7},{7,6},{8,9},{9,8},{10,11... | collective-permute-start | bytes 6291464 | tf_op jit(solution)/shard_map/ppermute | solution.py:240
  330.3 30.6 %collective-permute-start.2 = (bf16[128,128]{1,0:T(8,128)(2,1)S(1)}, bf16[128,128]{1,0:T(8,128)(2,1)S(1)}, u32[]{:S(2)}, u32[]{:S(2)}) collective-permute-start(bf16[128,128]{1,0:T(8,128)(2,1)S(1)} %get-tuple-element.7), channel_id=1, source_target_pairs={{2,0},{4,2},{6,4},{8,6},{10,8},{12,10},{14,12},{16,14},{18,16},{20... | collective-permute-start | bytes 98312 | tf_op jit(solution)/shard_map/ppermute | solution.py:228
  330.3 30.6 %collective-permute-start.1 = (bf16[128,128]{1,0:T(8,128)(2,1)S(1)}, bf16[128,128]{1,0:T(8,128)(2,1)S(1)}, u32[]{:S(2)}, u32[]{:S(2)}) collective-permute-start(bf16[128,128]{1,0:T(8,128)(2,1)S(1)} %get-tuple-element.6), channel_id=1, source_target_pairs={{0,2},{2,4},{4,6},{6,8},{8,10},{10,12},{12,14},{14,16},{16,18},{18... | collective-permute-start | bytes 98312 | tf_op jit(solution)/shard_map/ppermute | solution.py:227
  361.6 3.4 copy-start.2
  365.0 3.5 copy-start.1

commit v4 on v3

--- a/solution.py
+++ b/solution.py
@@ -10,10 +10,11 @@
 LAM = 0.25
 F32 = jnp.float32
 BF16 = jnp.bfloat16
+TN = (((0,), (0,)), ((), ()))
 
 
 def trip_kernel(
-    pair_count, pb_ref, len_ref, inc_ref, qt_ref, tgt_ref, w_ref, pred_ref, out_ref, acc_ref
+    pair_count, pb_ref, len_ref, inc_ref, qt_ref, tgt_ref, w_ref, _, pred_ref, out_ref, acc_ref
 ):
     t = pl.program_id(0)
 
@@ -40,7 +41,7 @@
         out_ref[...] = acc_ref[...].astype(out_ref.dtype)
 
 
-def trip_pass(pair_flat, lengths, incoming, query_t, tgt, wts):
+def trip_pass(pair_flat, lengths, incoming, query_t, tgt, wts, after):
     trip_blocks, pair_count, block, rank = lengths.shape
     slots = incoming.shape[0]
     const3 = lambda t, pb: (0, 0, 0)
@@ -55,6 +56,7 @@
                 pl.BlockSpec((rank, block), lambda t, pb: (0, t)),
                 pl.BlockSpec((1, 1, block), lambda t, pb: (t, 0, 0)),
                 pl.BlockSpec((1, 1, block), lambda t, pb: (t, 0, 0)),
+                pl.BlockSpec(memory_space=pl.ANY),
             ],
             out_specs=[
                 pl.BlockSpec((1, 1, block), lambda t, pb: (t, 0, 0)),
@@ -69,26 +71,29 @@
         compiler_params=pltpu.CompilerParams(
             dimension_semantics=("arbitrary",), vmem_limit_bytes=60 * 1024 * 1024
         ),
-    )(pair_flat, lengths, incoming, query_t, tgt, wts)
+    )(pair_flat, lengths, incoming, query_t, tgt, wts, after)
 
 
 def band_of(nb_ref, w_ref, base, rows):
     span = 3 * rows
-    col = lax.broadcasted_iota(jnp.int32, (rows, span), 1)
-    own = lax.broadcasted_iota(jnp.int32, (rows, span), 0) + rows
-    band = jnp.zeros((rows, span), F32)
-    for k in range(nb_ref.shape[1]):
-        rel = nb_ref[:, k : k + 1] - base
-        wk = w_ref[:, k : k + 1]
-        band = band + jnp.where(col == own, wk, 0.0) - jnp.where(col == rel, wk, 0.0)
+    row = lax.broadcasted_iota(jnp.int32, (span, rows), 0)
+    band = jnp.zeros((span, rows), F32)
+    for k in range(nb_ref.shape[0]):
+        rel = nb_ref[k : k + 1, :] - base
+        band = band - jnp.where(row == rel, w_ref[k : k + 1, :], 0.0)
+    mid_row = lax.broadcasted_iota(jnp.int32, (rows, rows), 0)
+    mid_col = lax.broadcasted_iota(jnp.int32, (rows, rows), 1)
+    total = jnp.sum(w_ref[...], axis=0, keepdims=True)
+    mid = band[rows : 2 * rows] + jnp.where(mid_row == mid_col, total, 0.0)
+    band = jnp.concatenate([band[:rows], mid, band[2 * rows :]], axis=0)
     hi = band.astype(BF16)
     lo = (band - hi.astype(F32)).astype(BF16)
     return hi, lo
 
 
 def apply_band(hi, lo, window):
-    return jnp.dot(hi, window, preferred_element_type=F32) + jnp.dot(
-        lo, window, preferred_element_type=F32
+    return lax.dot_general(hi, window, TN, preferred_element_type=F32) + lax.dot_general(
+        lo, window, TN, preferred_element_type=F32
     )
 
 
@@ -115,8 +120,8 @@
         grid=(inner,),
         in_specs=[
             pl.BlockSpec(emb.shape, lambda i: (0, 0), pipeline_mode=pl.Buffered(1)),
-            pl.BlockSpec((rows, nb_t.shape[1]), lambda i: (i + 1, 0)),
-            pl.BlockSpec((rows, w_t.shape[1]), lambda i: (i + 1, 0)),
+            pl.BlockSpec((nb_t.shape[0], rows), lambda i: (0, i + 1)),
+            pl.BlockSpec((w_t.shape[0], rows), lambda i: (0, i + 1)),
         ],
         out_specs=pl.BlockSpec((rows, rank), lambda i: (i, 0)),
         out_shape=jax.ShapeDtypeStruct((inner * rows, rank), F32),
@@ -126,14 +131,14 @@
 
 def smooth_edge(windows, nb_t, w_t, rows):
     rank = windows.shape[2]
-    last = nb_t.shape[0] // rows - 1
+    last = nb_t.shape[1] // rows - 1
     return pl.pallas_call(
         functools.partial(smooth_edge_kernel, last),
         grid=(2,),
         in_specs=[
             pl.BlockSpec((1,) + windows.shape[1:], lambda i: (i, 0, 0)),
-            pl.BlockSpec((rows, nb_t.shape[1]), lambda i: (i * last, 0)),
-            pl.BlockSpec((rows, w_t.shape[1]), lambda i: (i * last, 0)),
+            pl.BlockSpec((nb_t.shape[0], rows), lambda i: (0, i * last)),
+            pl.BlockSpec((w_t.shape[0], rows), lambda i: (0, i * last)),
         ],
         out_specs=pl.BlockSpec((rows, rank), lambda i: (i, 0)),
         out_shape=jax.ShapeDtypeStruct((2 * rows, rank), F32),
@@ -198,29 +203,9 @@
     trip_blocks = lengths.shape[0]
     query_t = jnp.einsum("fr,ft->rt", proj, feats, preferred_element_type=F32)
 
-    nb_t = nb_index[0].T
-    w_t = nb_weight[0].T
+    nb_t = nb_index[0]
+    w_t = nb_weight[0]
     inner = smooth_inner(emb, nb_t, w_t, block_size)
-
-    pred_rows, slot_grad = trip_pass(
-        pair_block.reshape(-1),
-        lengths,
-        incoming,
-        query_t,
-        targets.reshape(trip_blocks, 1, block_size),
-        trip_weight.reshape(trip_blocks, 1, block_size),
-    )
-    predicted = pred_rows.reshape(trip_blocks * block_size)
-
-    returned = lax.all_to_all(
-        slot_grad.reshape(regions, slot_count, rank_width, block_size),
-        "region",
-        split_axis=0,
-        concat_axis=0,
-        tiled=True,
-    )
-    returned = returned.reshape(regions * slot_count, rank_width, block_size)
-
     count = regions
     head = emb[:block_size]
     tail = emb[seg_rows - block_size :]
@@ -234,6 +219,26 @@
     )
     edge = smooth_edge(windows, nb_t, w_t, block_size)
     smoothed = jnp.concatenate([edge[:block_size], inner, edge[block_size:]], axis=0)
+
+    pred_rows, slot_grad = trip_pass(
+        pair_block.reshape(-1),
+        lengths,
+        incoming,
+        query_t,
+        targets.reshape(trip_blocks, 1, block_size),
+        trip_weight.reshape(trip_blocks, 1, block_size),
+        smoothed,
+    )
+    predicted = pred_rows.reshape(trip_blocks * block_size)
+
+    returned = lax.all_to_all(
+        slot_grad.reshape(regions, slot_count, rank_width, block_size),
+        "region",
+        split_axis=0,
+        concat_axis=0,
+        tiled=True,
+    )
+    returned = returned.reshape(regions * slot_count, rank_width, block_size)
 
     target_rows = jnp.where(live_mask, send_rows, -1).reshape(-1)
     owned = owned_pass(target_rows, returned, block_count).reshape(seg_rows, rank_width)

time: 372 us -> 349 us (0.938)
  waiting for transfers between devices: 223 us -> 195 us
  starting transfers between devices: 30.4 us -> 39.2 us
  local copies, waits for them, and re-layouts: 17.5 us -> 13.6 us
    all_to_all x1, waiting for transfers between devices: 108 us -> 1.1 us  [local(): lax.all_to_all(outgoing, 'region', split_axis=0, concat_axis=0, tiled=True)]
    ppermute x1, waiting for transfers between devices: 0.01 us -> 74.2 us  [local(): lax.ppermute(tail, 'region', [(i, (i + 1) % count) for i in range(count)])]
    all_to_all x1, starting transfers between devices: 9.66 us -> 18.6 us  [local(): lax.all_to_all(slot_grad.reshape(regions, slot_count, rank_width, block_s...]
    ppermute x1, waiting for transfers between devices: 0.01 us -> 4 us  [local(): partner = lax.ppermute(owned, 'rep', [(0, 1), (1, 0)])]
    unnamed x20 -> x14, local copies, waits for them, and re-layouts: 4.21 us -> 0.22 us
  transfers between devices with their start and end apart: 5 -> 5, of which waited for: 2 -> 5; matrix products, arithmetic and copies ran while one was open for 3% -> 3% of each run, Pallas kernels for 7% -> 6%
where the time goes in v4:
time: 349 us; the launch traced here: 345 us
  waiting for transfers between devices  195 us (56%)
  Pallas kernels  85.9 us (25%)
  starting transfers between devices  39.2 us (11%)
  local copies, waits for them, and re-layouts  13.6 us (4%)
  other arithmetic  8.1 us (2%)
    all_to_all x1, waiting for transfers between devices, local(): lax.all_to_all(slot_grad.reshape(regions, slot_count, rank_width, block_s...  114 us
    ppermute x1, waiting for transfers between devices, local(): lax.ppermute(tail, 'region', [(i, (i + 1) % count) for i in range(count)])  74.2 us
    pallas_call x1, Pallas kernels, trip_pass(): pl.pallas_call(functools.partial(trip_kernel, pair_count), grid_spec=pltp...  55.7 us
    all_to_all x1, starting transfers between devices, local(): lax.all_to_all(slot_grad.reshape(regions, slot_count, rank_width, block_s...  18.6 us
    pallas_call x1, Pallas kernels, smooth_inner(): pl.pallas_call(smooth_inner_kernel, grid=(inner,), in_specs=[pl.BlockSpec...  17.9 us
    all_to_all x1, starting transfers between devices, local(): lax.all_to_all(outgoing, 'region', split_axis=0, concat_axis=0, tiled=True)  11 us
    pallas_call x1, Pallas kernels, owned_pass(): pl.pallas_call(owned_kernel, grid_spec=pltpu.PrefetchScalarGridSpec(num_s...  10 us
    gather x1, local copies, waits for them, and re-layouts, local(): outgoing = blocks[jnp.where(live_mask, send_rows, 0)]  9.86 us
  transfers between devices with their start and end apart: 5, of which 5 were waited for; matrix products, arithmetic and copies ran while one was open for 3% of the time, Pallas kernels for 6%

profile of v4, /device:TPU:13, one launch (start us, length us, event | category | flops | bytes accessed | tf_op | source)
XLA Modules:
  0.0 344.8 jit_solution(8765489887395241370)
XLA Ops:
  0.6 0.0 copy-start
  0.6 0.7 compare_select_fusion
  1.4 0.1 copy.13
  1.5 0.1 reshape.72
  1.6 9.9 %gather_fusion = bf16[256,128,128]{2,1,0:T(8,128)(2,1)} fusion(bf16[32,128,128]{2,1,0:T(8,128)(2,1)} %bitcast.24, s32[1024]{0:T(1024)S(1)} %pad_clamp_fusion), kind=kCustom, calls=%fused_computation | custom fusion | bytes 16778240 | tf_op jit(solution)/shard_map/gather | solution.py:200
  11.4 11.0 %all-to-all-start = ((bf16[64,4,128,128]{3,2,1,0:T(8,128)(2,1)}), bf16[64,4,128,128]{3,2,1,0:T(8,128)(2,1)}, u32[]{:S(2)}, u32[]{:S(2)}) async-start(bf16[64,4,128,128]{3,2,1,0:T(8,128)(2,1)} %bitcast.25), calls=%async_computation | async-start | bytes 16777216 | tf_op jit(solution)/shard_map/all_to_all | solution.py:201
  22.5 0.0 copy-start.4
  22.5 0.8 fusion
  23.3 1.2 collective-permute-start
  24.5 2.4 collective-permute-start.1
  26.9 2.2 fusion.3.qt_ref
  29.1 0.9 fusion.1
  30.0 0.1 copy.12
  30.1 0.7 reshape.61.pb_ref
  30.8 17.9 %shard_map.114 = f32[3840,128]{1,0:T(8,128)} custom-call(bf16[4096,128]{1,0:T(8,128)(2,1)} %emb_ref.1, s32[4,4096]{1,0:T(4,128)} %bitcast.28, f32[4,4096]{1,0:T(4,128)} %bitcast.30), custom_call_target="tpu_custom_call" | custom-call | tf_op jit(solution)/shard_map/pallas_call | solution.py:118
  48.8 74.2 %collective-permute-done = bf16[128,128]{1,0:T(8,128)(2,1)S(1)} collective-permute-done((bf16[128,128]{1,0:T(8,128)(2,1)S(1)}, bf16[128,128]{1,0:T(8,128)(2,1)S(1)}, u32[]{:S(2)}, u32[]{:S(2)}) %collective-permute-start) | collective-permute-done | bytes 32800 | tf_op jit(solution)/shard_map/ppermute | solution.py:212
  122.9 2.0 collective-permute-done.1
  124.9 0.7 pad_maximum_fusion.1.win_ref
  125.6 2.2 shard_map.113
  127.8 0.9 fusion.2
  128.7 3.0 pad_maximum_fusion._
  131.8 1.1 all-to-all-done
  132.9 55.7 %shard_map.115 = (f32[48,1,128]{2,1,0:T(1,128)}, bf16[256,128,128]{2,1,0:T(8,128)(2,1)}) custom-call(s32[672]{0:T(1024)} %reshape.61.pb_ref, bf16[48,14,128,128]{3,2,1,0:T(8,128)(2,1)} %len_ref.1, bf16[256,128,128]{2,1,0:T(8,128)(2,1)} %bitcast.3.inc_ref, f32[128,6144]{1,0:T(8,128)} %fusion.3.qt_ref, f32[48,1,128]{2,1,0:T(1,128)} %bitcast.32, ...), custom_call_target="tpu_custom_call" | custom-call | tf_op jit(solution)/shard_map/pallas_call | solution.py:48
  188.6 18.6 %all-to-all-start.1 = ((bf16[64,4,128,128]{3,2,1,0:T(8,128)(2,1)}), bf16[64,4,128,128]{3,2,1,0:T(8,128)(2,1)}, u32[]{:S(2)}, u32[]{:S(2)}) async-start(bf16[64,4,128,128]{3,2,1,0:T(8,128)(2,1)} %bitcast.26), calls=%async_computation.1 | async-start | bytes 16777216 | tf_op jit(solution)/shard_map/all_to_all | solution.py:234
  207.2 0.1 copy.14
  207.3 0.1 squeeze.14
  207.4 0.6 compare_select_fusion.2.tgt_ref
  208.0 113.7 %all-to-all-done.1 = bf16[64,4,128,128]{3,2,1,0:T(8,128)(2,1)} async-done(((bf16[64,4,128,128]{3,2,1,0:T(8,128)(2,1)}), bf16[64,4,128,128]{3,2,1,0:T(8,128)(2,1)}, u32[]{:S(2)}, u32[]{:S(2)}) %all-to-all-start.1) | async-done | bytes 8388640 | tf_op jit(solution)/shard_map/all_to_all | solution.py:234
  321.7 10.0 %shard_map.116 = f32[32,128,128]{2,1,0:T(8,128)} custom-call(s32[256]{0:T(256)} %compare_select_fusion.2.tgt_ref, bf16[256,128,128]{2,1,0:T(8,128)(2,1)} %bitcast.12.ret_ref), custom_call_target="tpu_custom_call" | custom-call | tf_op jit(solution)/shard_map/pallas_call | solution.py:172
  331.8 6.0 %collective-permute-start.2 = (f32[4096,128]{1,0:T(8,128)}, f32[4096,128]{1,0:T(8,128)S(1)}, u32[]{:S(2)}, u32[]{:S(2)}) collective-permute-start(f32[4096,128]{1,0:T(8,128)} %bitcast.27), channel_id=1, source_target_pairs={{0,1},{1,0},{2,3},{3,2},{4,5},{5,4},{6,7},{7,6},{8,9},{9,8},{10,11... | collective-permute-start | bytes 6291464 | tf_op jit(solution)/shard_map/ppermute | solution.py:245
  337.7 4.0 %collective-permute-done.2 = f32[4096,128]{1,0:T(8,128)S(1)} collective-permute-done((f32[4096,128]{1,0:T(8,128)}, f32[4096,128]{1,0:T(8,128)S(1)}, u32[]{:S(2)}, u32[]{:S(2)}) %collective-permute-start.2) | collective-permute-done | bytes 2097184 | tf_op jit(solution)/shard_map/ppermute | solution.py:245
  341.7 3.0 add_convert_fusion
  (13 shorter events, 0.0 us)
Async XLA Ops:
  0.6 26.2 %copy-start = (bf16[16,6144]{1,0:T(8,128)(2,1)S(1)}, bf16[16,6144]{1,0:T(8,128)(2,1)}, u32[]{:S(2)}) copy-start(bf16[16,6144]{1,0:T(8,128)(2,1)} %param.13) | copy-start | bytes 589828
  11.4 15.4 %copy-start.5 = (bf16[16,128]{1,0:T(8,128)(2,1)S(1)}, bf16[16,128]{1,0:T(8,128)(2,1)}, u32[]{:S(2)}) copy-start(bf16[16,128]{1,0:T(8,128)(2,1)} %param.14) | copy-start | bytes 12292
  11.4 121.4 %all-to-all-start = ((bf16[64,4,128,128]{3,2,1,0:T(8,128)(2,1)}), bf16[64,4,128,128]{3,2,1,0:T(8,128)(2,1)}, u32[]{:S(2)}, u32[]{:S(2)}) async-start(bf16[64,4,128,128]{3,2,1,0:T(8,128)(2,1)} %bitcast.25), calls=%async_computation | async-start | bytes 16777216 | tf_op jit(solution)/shard_map/all_to_all | solution.py:201
  22.5 7.5 %copy-start.4 = (s32[48,14]{0,1:T(8,128)S(1)}, s32[48,14]{0,1:T(8,128)}, u32[]{:S(2)}) copy-start(s32[48,14]{0,1:T(8,128)} %param.12) | copy-start | bytes 8068
  23.3 99.6 %collective-permute-start = (bf16[128,128]{1,0:T(8,128)(2,1)S(1)}, bf16[128,128]{1,0:T(8,128)(2,1)S(1)}, u32[]{:S(2)}, u32[]{:S(2)}) collective-permute-start(bf16[128,128]{1,0:T(8,128)(2,1)S(1)} %get-tuple-element.6), channel_id=1, source_target_pairs={{0,2},{2,4},{4,6},{6,8},{8,10},{10,12},{12,14},{14,16},{16,18},{18... | collective-permute-start | bytes 98312 | tf_op jit(solution)/shard_map/ppermute | solution.py:212
  24.5 100.4 %collective-permute-start.1 = (bf16[128,128]{1,0:T(8,128)(2,1)S(1)}, bf16[128,128]{1,0:T(8,128)(2,1)S(1)}, u32[]{:S(2)}, u32[]{:S(2)}) collective-permute-start(bf16[128,128]{1,0:T(8,128)(2,1)S(1)} %get-tuple-element.7), channel_id=1, source_target_pairs={{2,0},{4,2},{6,4},{8,6},{10,8},{12,10},{14,12},{16,14},{18,16},{20... | collective-permute-start | bytes 98312 | tf_op jit(solution)/shard_map/ppermute | solution.py:213
  188.6 18.6 %copy-start.3 = (s32[1,1,64,4]{2,3,1,0:T(4,128)S(1)}, s32[1,1,64,4]{2,3,1,0:T(4,128)}, u32[]{:S(2)}) copy-start(s32[1,1,64,4]{2,3,1,0:T(4,128)} %param.17) | copy-start | bytes 3076
  188.6 133.2 %all-to-all-start.1 = ((bf16[64,4,128,128]{3,2,1,0:T(8,128)(2,1)}), bf16[64,4,128,128]{3,2,1,0:T(8,128)(2,1)}, u32[]{:S(2)}, u32[]{:S(2)}) async-start(bf16[64,4,128,128]{3,2,1,0:T(8,128)(2,1)} %bitcast.26), calls=%async_computation.1 | async-start | bytes 16777216 | tf_op jit(solution)/shard_map/all_to_all | solution.py:234
  321.7 20.0 %copy-start.2 = (f32[3840,128]{1,0:T(8,128)S(1)}, f32[3840,128]{1,0:T(8,128)}, u32[]{:S(2)}) copy-start(f32[3840,128]{1,0:T(8,128)} %shard_map.114) | copy-start | bytes 5898244
  331.8 13.0 %copy-start.1 = (bf16[16,6144]{1,0:T(8,128)(2,1)S(1)}, bf16[16,6144]{1,0:T(8,128)(2,1)}, u32[]{:S(2)}) copy-start(bf16[16,6144]{1,0:T(8,128)(2,1)} %param.13) | copy-start | bytes 589828
  331.8 10.0 %collective-permute-start.2 = (f32[4096,128]{1,0:T(8,128)}, f32[4096,128]{1,0:T(8,128)S(1)}, u32[]{:S(2)}, u32[]{:S(2)}) collective-permute-start(f32[4096,128]{1,0:T(8,128)} %bitcast.27), channel_id=1, source_target_pairs={{0,1},{1,0},{2,3},{3,2},{4,5},{5,4},{6,7},{7,6},{8,9},{9,8},{10,11... | collective-permute-start | bytes 6291464 | tf_op jit(solution)/shard_map/ppermute | solution.py:245

commit v5 on v4

--- a/solution.py
+++ b/solution.py
@@ -23,18 +23,26 @@
         acc_ref[...] = jnp.zeros_like(acc_ref)
 
     hidden = None
-    for k in range(pair_count):
-        p = pb_ref[t * pair_count + k]
-        term = jnp.dot(len_ref[0, k], inc_ref[p], preferred_element_type=F32)
+    for k in range(0, pair_count, 2):
+        p0 = pb_ref[t * pair_count + k]
+        p1 = pb_ref[t * pair_count + k + 1]
+        lhs = jnp.concatenate([len_ref[0, k], len_ref[0, k + 1]], axis=1)
+        rhs = jnp.concatenate([inc_ref[p0], inc_ref[p1]], axis=0)
+        term = jnp.dot(lhs, rhs, preferred_element_type=F32)
         hidden = term if hidden is None else hidden + term
     q_t = qt_ref[...]
     pred_row = jnp.sum(hidden.T * q_t, axis=0, keepdims=True)
     pred_ref[0] = pred_row
     err_row = w_ref[0] * (pred_row - tgt_ref[0])
     scaled_t = (err_row * q_t).astype(BF16)
-    for k in range(pair_count):
-        p = pb_ref[t * pair_count + k]
-        acc_ref[p] += jnp.dot(scaled_t, len_ref[0, k], preferred_element_type=F32)
+    block = q_t.shape[1]
+    for k in range(0, pair_count, 2):
+        p0 = pb_ref[t * pair_count + k]
+        p1 = pb_ref[t * pair_count + k + 1]
+        rhs = jnp.concatenate([len_ref[0, k], len_ref[0, k + 1]], axis=1)
+        both = jnp.dot(scaled_t, rhs, preferred_element_type=F32)
+        acc_ref[p0] += both[:, :block]
+        acc_ref[p1] += both[:, block:]
 
     @pl.when(t == pl.num_programs(0) - 1)
     def _():
@@ -146,7 +154,7 @@
     )(windows, nb_t, w_t)
 
 
-def owned_kernel(tgt_ref, ret_ref, out_ref, acc_ref):
+def owned_kernel(tgt_ref, ret_ref, _, out_ref, acc_ref):
     c = pl.program_id(0)
     chunk = ret_ref.shape[0]
 
@@ -167,14 +175,17 @@
             out_ref[b] = acc_ref[b].T
 
 
-def owned_pass(targets, returned, block_count, chunk=32):
+def owned_pass(targets, returned, after, block_count, chunk=32):
     slots, rank, block = returned.shape
     return pl.pallas_call(
         owned_kernel,
         grid_spec=pltpu.PrefetchScalarGridSpec(
             num_scalar_prefetch=1,
             grid=(slots // chunk,),
-            in_specs=[pl.BlockSpec((chunk, rank, block), lambda c, tg: (c, 0, 0))],
+            in_specs=[
+                pl.BlockSpec((chunk, rank, block), lambda c, tg: (c, 0, 0)),
+                pl.BlockSpec(memory_space=pl.ANY),
+            ],
             out_specs=pl.BlockSpec(
                 (block_count, block, rank), lambda c, tg: (0, 0, 0), pipeline_mode=pl.Buffered(1)
             ),
@@ -182,7 +193,7 @@
         ),
         out_shape=jax.ShapeDtypeStruct((block_count, block, rank), F32),
         compiler_params=pltpu.CompilerParams(dimension_semantics=("arbitrary",)),
-    )(targets, returned)
+    )(targets, returned, after)
 
 
 def local(
@@ -218,7 +229,6 @@
         ]
     )
     edge = smooth_edge(windows, nb_t, w_t, block_size)
-    smoothed = jnp.concatenate([edge[:block_size], inner, edge[block_size:]], axis=0)
 
     pred_rows, slot_grad = trip_pass(
         pair_block.reshape(-1),
@@ -227,7 +237,7 @@
         query_t,
         targets.reshape(trip_blocks, 1, block_size),
         trip_weight.reshape(trip_blocks, 1, block_size),
-        smoothed,
+        inner,
     )
     predicted = pred_rows.reshape(trip_blocks * block_size)
 
@@ -241,8 +251,9 @@
     returned = returned.reshape(regions * slot_count, rank_width, block_size)
 
     target_rows = jnp.where(live_mask, send_rows, -1).reshape(-1)
-    owned = owned_pass(target_rows, returned, block_count).reshape(seg_rows, rank_width)
+    owned = owned_pass(target_rows, returned, edge, block_count).reshape(seg_rows, rank_width)
     partner = lax.ppermute(owned, "rep", [(0, 1), (1, 0)])
+    smoothed = jnp.concatenate([edge[:block_size], inner, edge[block_size:]], axis=0)
     gradient = (owned + partner) + LAM * smoothed
     return (predicted, gradient.astype(jnp.bfloat16))
 

time: 349 us -> 339 us (0.971)
  starting transfers between devices: 39.2 us -> 29.4 us
  waiting for transfers between devices: 195 us -> 201 us
  Pallas kernels: 85.9 us -> 81 us
    all_to_all x1, waiting for transfers between devices: 114 us -> 20.5 us  [local(): lax.all_to_all(slot_grad.reshape(regions, slot_count, rank_width, block_s...]
    all_to_all x1, waiting for transfers between devices: 1.1 us -> 89.9 us  [local(): lax.all_to_all(outgoing, 'region', split_axis=0, concat_axis=0, tiled=True)]
    ppermute x1, waiting for transfers between devices: 1.98 us -> 86.6 us  [local(): lax.ppermute(head, 'region', [((i + 1) % count, i) for i in range(count)])]
    ppermute x1, waiting for transfers between devices: 74.2 us -> 0.01 us  [local(): lax.ppermute(tail, 'region', [(i, (i + 1) % count) for i in range(count)])]
    all_to_all x1, starting transfers between devices: 18.6 us -> 9.65 us  [local(): lax.all_to_all(slot_grad.reshape(regions, slot_count, rank_width, block_s...]
    pallas_call x1, Pallas kernels: 55.7 us -> 51.2 us  [trip_pass(): pl.pallas_call(functools.partial(trip_kernel, pair_count), grid_spec=pltp...]
  transfers between devices with their start and end apart: 5 -> 5, of which waited for: 5 -> 4; matrix products, arithmetic and copies ran while one was open for 3% -> 2% of each run, Pallas kernels for 6% -> 6%
where the time goes in v5:
time: 339 us; the launch traced here: 332 us
  waiting for transfers between devices  201 us (59%)
  Pallas kernels  81 us (24%)
  starting transfers between devices  29.4 us (9%)
  local copies, waits for them, and re-layouts  12.6 us (4%)
  other arithmetic  5.1 us (2%)
    all_to_all x1, waiting for transfers between devices, local(): lax.all_to_all(outgoing, 'region', split_axis=0, concat_axis=0, tiled=True)  89.9 us
    ppermute x1, waiting for transfers between devices, local(): lax.ppermute(head, 'region', [((i + 1) % count, i) for i in range(count)])  86.6 us
    pallas_call x1, Pallas kernels, trip_pass(): pl.pallas_call(functools.partial(trip_kernel, pair_count), grid_spec=pltp...  51.2 us
    all_to_all x1, waiting for transfers between devices, local(): lax.all_to_all(slot_grad.reshape(regions, slot_count, rank_width, block_s...  20.5 us
    pallas_call x1, Pallas kernels, smooth_inner(): pl.pallas_call(smooth_inner_kernel, grid=(inner,), in_specs=[pl.BlockSpec...  17.9 us
    all_to_all x1, starting transfers between devices, local(): lax.all_to_all(outgoing, 'region', split_axis=0, concat_axis=0, tiled=True)  11.2 us
    pallas_call x1, Pallas kernels, owned_pass(): pl.pallas_call(owned_kernel, grid_spec=pltpu.PrefetchScalarGridSpec(num_s...  9.74 us
    gather x1, local copies, waits for them, and re-layouts, local(): outgoing = blocks[jnp.where(live_mask, send_rows, 0)]  9.72 us
  transfers between devices with their start and end apart: 5, of which 4 were waited for; matrix products, arithmetic and copies ran while one was open for 2% of the time, Pallas kernels for 6%

profile of v5, /device:TPU:13, one launch (start us, length us, event | category | flops | bytes accessed | tf_op | source)
XLA Modules:
  0.0 331.9 jit_solution(2566520364984169746)
XLA Ops:
  0.6 0.0 copy-start
  0.6 0.7 compare_select_fusion
  1.4 0.1 copy.13
  1.5 0.1 reshape.72
  1.6 9.7 %gather_fusion = bf16[256,128,128]{2,1,0:T(8,128)(2,1)} fusion(bf16[32,128,128]{2,1,0:T(8,128)(2,1)} %bitcast.24, s32[1024]{0:T(1024)S(1)} %pad_clamp_fusion), kind=kCustom, calls=%fused_computation | custom fusion | bytes 16778240 | tf_op jit(solution)/shard_map/gather | solution.py:211
  11.3 11.2 %all-to-all-start = ((bf16[64,4,128,128]{3,2,1,0:T(8,128)(2,1)}), bf16[64,4,128,128]{3,2,1,0:T(8,128)(2,1)}, u32[]{:S(2)}, u32[]{:S(2)}) async-start(bf16[64,4,128,128]{3,2,1,0:T(8,128)(2,1)} %bitcast.25), calls=%async_computation | async-start | bytes 16777216 | tf_op jit(solution)/shard_map/all_to_all | solution.py:212
  22.5 0.0 copy-start.6
  22.5 0.1 copy.12
  22.6 0.7 reshape.61.pb_ref
  23.3 17.9 %shard_map.113._ = f32[3840,128]{1,0:T(8,128)} custom-call(bf16[4096,128]{1,0:T(8,128)(2,1)} %emb_ref.1, s32[4,4096]{1,0:T(4,128)} %bitcast.28, f32[4,4096]{1,0:T(4,128)} %bitcast.30), custom_call_target="tpu_custom_call" | custom-call | tf_op jit(solution)/shard_map/pallas_call | solution.py:126
  41.2 0.0 copy-done
  41.2 2.2 fusion.5.qt_ref
  43.5 89.9 %all-to-all-done = bf16[64,4,128,128]{3,2,1,0:T(8,128)(2,1)} async-done(((bf16[64,4,128,128]{3,2,1,0:T(8,128)(2,1)}), bf16[64,4,128,128]{3,2,1,0:T(8,128)(2,1)}, u32[]{:S(2)}, u32[]{:S(2)}) %all-to-all-start) | async-done | bytes 8388640 | tf_op jit(solution)/shard_map/all_to_all | solution.py:212
  133.3 51.2 %shard_map.114 = (f32[48,1,128]{2,1,0:T(1,128)}, bf16[256,128,128]{2,1,0:T(8,128)(2,1)}) custom-call(s32[672]{0:T(1024)} %reshape.61.pb_ref, bf16[48,14,128,128]{3,2,1,0:T(8,128)(2,1)} %len_ref.1, bf16[256,128,128]{2,1,0:T(8,128)(2,1)} %bitcast.3.inc_ref, f32[128,6144]{1,0:T(8,128)} %fusion.5.qt_ref, f32[48,1,128]{2,1,0:T(1,128)} %bitcast.32, ...), custom_call_target="tpu_custom_call" | custom-call | tf_op jit(solution)/shard_map/pallas_call | solution.py:56
  184.5 9.7 %all-to-all-start.1 = ((bf16[64,4,128,128]{3,2,1,0:T(8,128)(2,1)}), bf16[64,4,128,128]{3,2,1,0:T(8,128)(2,1)}, u32[]{:S(2)}, u32[]{:S(2)}) async-start(bf16[64,4,128,128]{3,2,1,0:T(8,128)(2,1)} %bitcast.26), calls=%async_computation.1 | async-start | bytes 16777216 | tf_op jit(solution)/shard_map/all_to_all | solution.py:244
  194.2 0.8 fusion.2
  195.0 2.4 collective-permute-start.1
  197.4 0.0 collective-permute-start
  197.4 0.1 copy.14
  197.5 0.1 squeeze.14
  197.6 0.9 fusion.3
  198.4 0.6 compare_select_fusion.2.tgt_ref
  199.0 86.6 %collective-permute-done.1 = bf16[128,128]{1,0:T(8,128)(2,1)S(1)} collective-permute-done((bf16[128,128]{1,0:T(8,128)(2,1)S(1)}, bf16[128,128]{1,0:T(8,128)(2,1)S(1)}, u32[]{:S(2)}, u32[]{:S(2)}) %collective-permute-start.1) | collective-permute-done | bytes 32800 | tf_op jit(solution)/shard_map/ppermute | solution.py:224
  285.6 0.0 collective-permute-done
  285.7 0.7 pad_maximum_fusion.win_ref
  286.4 2.2 shard_map.115._
  288.5 20.5 %all-to-all-done.1 = bf16[64,4,128,128]{3,2,1,0:T(8,128)(2,1)} async-done(((bf16[64,4,128,128]{3,2,1,0:T(8,128)(2,1)}), bf16[64,4,128,128]{3,2,1,0:T(8,128)(2,1)}, u32[]{:S(2)}, u32[]{:S(2)}) %all-to-all-start.1) | async-done | bytes 8388640 | tf_op jit(solution)/shard_map/all_to_all | solution.py:244
  309.0 9.7 %shard_map.116 = f32[32,128,128]{2,1,0:T(8,128)} custom-call(s32[256]{0:T(256)} %compare_select_fusion.2.tgt_ref, bf16[256,128,128]{2,1,0:T(8,128)(2,1)} %bitcast.10.ret_ref, f32[256,128]{1,0:T(8,128)} %shard_map.115._), custom_call_target="tpu_custom_call" | custom-call | tf_op jit(solution)/shard_map/pallas_call | solution.py:180
  318.7 6.1 %collective-permute-start.2 = (f32[4096,128]{1,0:T(8,128)}, f32[4096,128]{1,0:T(8,128)S(1)}, u32[]{:S(2)}, u32[]{:S(2)}) collective-permute-start(f32[4096,128]{1,0:T(8,128)} %bitcast.27), channel_id=1, source_target_pairs={{0,1},{1,0},{2,3},{3,2},{4,5},{5,4},{6,7},{7,6},{8,9},{9,8},{10,11... | collective-permute-start | bytes 6291464 | tf_op jit(solution)/shard_map/ppermute | solution.py:255
  324.9 0.0 copy-done.3
  324.9 4.0 %collective-permute-done.2 = f32[4096,128]{1,0:T(8,128)S(1)} collective-permute-done((f32[4096,128]{1,0:T(8,128)}, f32[4096,128]{1,0:T(8,128)S(1)}, u32[]{:S(2)}, u32[]{:S(2)}) %collective-permute-start.2) | collective-permute-done | bytes 2097184 | tf_op jit(solution)/shard_map/ppermute | solution.py:255
  328.9 3.1 fusion.1
  (14 shorter events, 0.1 us)
Async XLA Ops:
  0.6 40.6 %copy-start = (bf16[16,6144]{1,0:T(8,128)(2,1)S(1)}, bf16[16,6144]{1,0:T(8,128)(2,1)}, u32[]{:S(2)}) copy-start(bf16[16,6144]{1,0:T(8,128)(2,1)} %param.13) | copy-start | bytes 589828
  11.3 11.2 %copy-start.5 = (s32[48,14]{0,1:T(8,128)S(1)}, s32[48,14]{0,1:T(8,128)}, u32[]{:S(2)}) copy-start(s32[48,14]{0,1:T(8,128)} %param.12) | copy-start | bytes 8068
  11.3 122.0 %all-to-all-start = ((bf16[64,4,128,128]{3,2,1,0:T(8,128)(2,1)}), bf16[64,4,128,128]{3,2,1,0:T(8,128)(2,1)}, u32[]{:S(2)}, u32[]{:S(2)}) async-start(bf16[64,4,128,128]{3,2,1,0:T(8,128)(2,1)} %bitcast.25), calls=%async_computation | async-start | bytes 16777216 | tf_op jit(solution)/shard_map/all_to_all | solution.py:212
  22.5 18.7 %copy-start.6 = (bf16[16,128]{1,0:T(8,128)(2,1)S(1)}, bf16[16,128]{1,0:T(8,128)(2,1)}, u32[]{:S(2)}) copy-start(bf16[16,128]{1,0:T(8,128)(2,1)} %param.14) | copy-start | bytes 12292
  184.5 12.8 %copy-start.4 = (s32[1,1,64,4]{2,3,1,0:T(4,128)S(1)}, s32[1,1,64,4]{2,3,1,0:T(4,128)}, u32[]{:S(2)}) copy-start(s32[1,1,64,4]{2,3,1,0:T(4,128)} %param.17) | copy-start | bytes 3076
  184.5 124.5 %all-to-all-start.1 = ((bf16[64,4,128,128]{3,2,1,0:T(8,128)(2,1)}), bf16[64,4,128,128]{3,2,1,0:T(8,128)(2,1)}, u32[]{:S(2)}, u32[]{:S(2)}) async-start(bf16[64,4,128,128]{3,2,1,0:T(8,128)(2,1)} %bitcast.26), calls=%async_computation.1 | async-start | bytes 16777216 | tf_op jit(solution)/shard_map/all_to_all | solution.py:244
  195.0 90.7 %collective-permute-start.1 = (bf16[128,128]{1,0:T(8,128)(2,1)S(1)}, bf16[128,128]{1,0:T(8,128)(2,1)S(1)}, u32[]{:S(2)}, u32[]{:S(2)}) collective-permute-start(bf16[128,128]{1,0:T(8,128)(2,1)S(1)} %get-tuple-element.7), channel_id=1, source_target_pairs={{2,0},{4,2},{6,4},{8,6},{10,8},{12,10},{14,12},{16,14},{18,16},{20... | collective-permute-start | bytes 98312 | tf_op jit(solution)/shard_map/ppermute | solution.py:224
  197.4 88.3 %collective-permute-start = (bf16[128,128]{1,0:T(8,128)(2,1)S(1)}, bf16[128,128]{1,0:T(8,128)(2,1)S(1)}, u32[]{:S(2)}, u32[]{:S(2)}) collective-permute-start(bf16[128,128]{1,0:T(8,128)(2,1)S(1)} %get-tuple-element.6), channel_id=1, source_target_pairs={{0,2},{2,4},{4,6},{6,8},{8,10},{10,12},{12,14},{14,16},{16,18},{18... | collective-permute-start | bytes 98312 | tf_op jit(solution)/shard_map/ppermute | solution.py:223
  309.0 15.9 %copy-start.3 = (f32[256,128]{1,0:T(8,128)S(1)}, f32[256,128]{1,0:T(8,128)}, u32[]{:S(2)}) copy-start(f32[256,128]{1,0:T(8,128)} %shard_map.115._) | copy-start | bytes 393220
  309.0 19.9 %copy-start.2 = (f32[3840,128]{1,0:T(8,128)S(1)}, f32[3840,128]{1,0:T(8,128)}, u32[]{:S(2)}) copy-start(f32[3840,128]{1,0:T(8,128)} %shard_map.113._) | copy-start | bytes 5898244
  318.7 10.1 %collective-permute-start.2 = (f32[4096,128]{1,0:T(8,128)}, f32[4096,128]{1,0:T(8,128)S(1)}, u32[]{:S(2)}, u32[]{:S(2)}) collective-permute-start(f32[4096,128]{1,0:T(8,128)} %bitcast.27), channel_id=1, source_target_pairs={{0,1},{1,0},{2,3},{3,2},{4,5},{5,4},{6,7},{7,6},{8,9},{9,8},{10,11... | collective-permute-start | bytes 6291464 | tf_op jit(solution)/shard_map/ppermute | solution.py:255
  328.9 3.1 copy-start.1

commit v6 on v5

--- a/solution.py
+++ b/solution.py
@@ -196,6 +196,36 @@
     )(targets, returned, after)
 
 
+def gather_kernel(idx_ref, src_ref, out_ref, sems):
+    count = out_ref.shape[0]
+
+    def start(s, carry):
+        pltpu.make_async_copy(src_ref.at[idx_ref[s]], out_ref.at[s], sems.at[s]).start()
+        return carry
+
+    def wait(s, carry):
+        pltpu.make_async_copy(src_ref.at[0], out_ref.at[s], sems.at[s]).wait()
+        return carry
+
+    lax.fori_loop(0, count, start, 0)
+    lax.fori_loop(0, count, wait, 0)
+
+
+def gather_blocks(idx, blocks):
+    count = idx.shape[0]
+    return pl.pallas_call(
+        gather_kernel,
+        grid_spec=pltpu.PrefetchScalarGridSpec(
+            num_scalar_prefetch=1,
+            grid=(1,),
+            in_specs=[pl.BlockSpec(memory_space=pl.ANY)],
+            out_specs=pl.BlockSpec(memory_space=pl.ANY),
+            scratch_shapes=[pltpu.SemaphoreType.DMA((count,))],
+        ),
+        out_shape=jax.ShapeDtypeStruct((count,) + blocks.shape[1:], blocks.dtype),
+    )(idx, blocks)
+
+
 def local(
     emb, lengths, pair_block, feats, proj, targets, trip_weight, send_list, nb_index, nb_weight
 ):
@@ -208,7 +238,8 @@
     send_rows = send_list[0, 0]
     live_mask = send_rows >= 0
     slot_count = send_rows.shape[1]
-    outgoing = blocks[jnp.where(live_mask, send_rows, 0)]
+    outgoing = gather_blocks(jnp.where(live_mask, send_rows, 0).reshape(-1), blocks)
+    outgoing = outgoing.reshape(regions, slot_count, block_size, rank_width)
     incoming = lax.all_to_all(outgoing, "region", split_axis=0, concat_axis=0, tiled=True)
     incoming = incoming.reshape(regions * slot_count, block_size, rank_width)
     trip_blocks = lengths.shape[0]

time: 339 us -> 586 us (1.73)
  Pallas kernels: 81 us -> 339 us
  local copies, waits for them, and re-layouts: 12.6 us -> 3.43 us
    pallas_call x0 -> x1, Pallas kernels: none -> 258 us  [gather_blocks(): pl.pallas_call(gather_kernel, grid_spec=pltpu.PrefetchScalarGridSpec(num_...]
    gather x1 -> x0, local copies, waits for them, and re-layouts: 9.72 us -> none  [local(): outgoing = blocks[jnp.where(live_mask, send_rows, 0)]]
  transfers between devices with their start and end apart: 5 -> 5, of which waited for: 4 -> 4; matrix products, arithmetic and copies ran while one was open for 2% -> 1% of each run, Pallas kernels for 6% -> 3%
where the time goes in v6:
time: 586 us; the launch traced here: 581 us
  Pallas kernels  339 us (58%)
  waiting for transfers between devices  203 us (35%)
  starting transfers between devices  28.5 us (5%)
    pallas_call x1, Pallas kernels, gather_blocks(): pl.pallas_call(gather_kernel, grid_spec=pltpu.PrefetchScalarGridSpec(num_...  258 us
    all_to_all x1, waiting for transfers between devices, local(): lax.all_to_all(outgoing, 'region', split_axis=0, concat_axis=0, tiled=True)  89.9 us
    ppermute x1, waiting for transfers between devices, local(): lax.ppermute(head, 'region', [((i + 1) % count, i) for i in range(count)])  88.2 us
    pallas_call x1, Pallas kernels, trip_pass(): pl.pallas_call(functools.partial(trip_kernel, pair_count), grid_spec=pltp...  51.2 us
    all_to_all x1, waiting for transfers between devices, local(): lax.all_to_all(slot_grad.reshape(regions, slot_count, rank_width, block_s...  20.6 us
    pallas_call x1, Pallas kernels, smooth_inner(): pl.pallas_call(smooth_inner_kernel, grid=(inner,), in_specs=[pl.BlockSpec...  17.9 us
  transfers between devices with their start and end apart: 5, of which 4 were waited for; matrix products, arithmetic and copies ran while one was open for 1% of the time, Pallas kernels for 3%

profile of v6, /device:TPU:13, one launch (start us, length us, event | category | flops | bytes accessed | tf_op | source)
XLA Modules:
  0.0 581.5 jit_solution(13210216301096183076)
XLA Ops:
  0.6 0.0 copy-start
  0.6 0.8 copy.13
  1.5 0.1 squeeze.9
  1.6 0.6 compare_select_fusion
  2.2 258.2 %shard_map.113 = bf16[256,128,128]{2,1,0:T(8,128)(2,1)} custom-call(s32[256]{0:T(256)} %get-tuple-element.13.idx_ref, bf16[32,128,128]{2,1,0:T(8,128)(2,1)} %bitcast.23), custom_call_target="tpu_custom_call" | custom-call | tf_op jit(solution)/shard_map/pallas_call | solution.py:216
  260.4 0.0 copy-start.4
  260.4 11.0 %all-to-all-start = ((bf16[64,4,128,128]{3,2,1,0:T(8,128)(2,1)}), bf16[64,4,128,128]{3,2,1,0:T(8,128)(2,1)}, u32[]{:S(2)}, u32[]{:S(2)}) async-start(bf16[64,4,128,128]{3,2,1,0:T(8,128)(2,1)} %bitcast.20), calls=%async_computation | async-start | bytes 16777216 | tf_op jit(solution)/shard_map/all_to_all | solution.py:243
  271.4 0.0 copy-done.4
  271.4 0.0 copy-start.5
  271.4 0.1 copy.12
  271.5 0.7 reshape.38.pb_ref
  272.2 17.9 %shard_map.114._ = f32[3840,128]{1,0:T(8,128)} custom-call(bf16[4096,128]{1,0:T(8,128)(2,1)} %emb_ref.1, s32[4,4096]{1,0:T(4,128)} %bitcast.24, f32[4,4096]{1,0:T(4,128)} %bitcast.26), custom_call_target="tpu_custom_call" | custom-call | tf_op jit(solution)/shard_map/pallas_call | solution.py:126
  290.1 0.0 copy-done
  290.1 0.0 copy-done.5
  290.1 2.2 fusion.5.qt_ref
  292.4 89.9 %all-to-all-done = bf16[64,4,128,128]{3,2,1,0:T(8,128)(2,1)} async-done(((bf16[64,4,128,128]{3,2,1,0:T(8,128)(2,1)}), bf16[64,4,128,128]{3,2,1,0:T(8,128)(2,1)}, u32[]{:S(2)}, u32[]{:S(2)}) %all-to-all-start) | async-done | bytes 8388640 | tf_op jit(solution)/shard_map/all_to_all | solution.py:243
  382.3 51.2 %shard_map.115 = (f32[48,1,128]{2,1,0:T(1,128)}, bf16[256,128,128]{2,1,0:T(8,128)(2,1)}) custom-call(s32[672]{0:T(1024)} %reshape.38.pb_ref, bf16[48,14,128,128]{3,2,1,0:T(8,128)(2,1)} %len_ref.1, bf16[256,128,128]{2,1,0:T(8,128)(2,1)} %bitcast.2.inc_ref, f32[128,6144]{1,0:T(8,128)} %fusion.5.qt_ref, f32[48,1,128]{2,1,0:T(1,128)} %bitcast.28, ...), custom_call_target="tpu_custom_call" | custom-call | tf_op jit(solution)/shard_map/pallas_call | solution.py:56
  433.5 9.7 %all-to-all-start.1 = ((bf16[64,4,128,128]{3,2,1,0:T(8,128)(2,1)}), bf16[64,4,128,128]{3,2,1,0:T(8,128)(2,1)}, u32[]{:S(2)}, u32[]{:S(2)}) async-start(bf16[64,4,128,128]{3,2,1,0:T(8,128)(2,1)} %bitcast.21), calls=%async_computation.1 | async-start | bytes 16777216 | tf_op jit(solution)/shard_map/all_to_all | solution.py:275
  443.1 0.8 fusion.2
  443.9 2.4 collective-permute-start.1
  446.3 0.0 collective-permute-start
  446.3 0.9 fusion.3
  447.2 88.2 %collective-permute-done.1 = bf16[128,128]{1,0:T(8,128)(2,1)S(1)} collective-permute-done((bf16[128,128]{1,0:T(8,128)(2,1)S(1)}, bf16[128,128]{1,0:T(8,128)(2,1)S(1)}, u32[]{:S(2)}, u32[]{:S(2)}) %collective-permute-start.1) | collective-permute-done | bytes 32800 | tf_op jit(solution)/shard_map/ppermute | solution.py:255
  535.4 0.0 collective-permute-done
  535.4 0.7 pad_maximum_fusion.win_ref
  536.1 2.2 shard_map.116._
  538.3 20.6 %all-to-all-done.1 = bf16[64,4,128,128]{3,2,1,0:T(8,128)(2,1)} async-done(((bf16[64,4,128,128]{3,2,1,0:T(8,128)(2,1)}), bf16[64,4,128,128]{3,2,1,0:T(8,128)(2,1)}, u32[]{:S(2)}, u32[]{:S(2)}) %all-to-all-start.1) | async-done | bytes 8388640 | tf_op jit(solution)/shard_map/all_to_all | solution.py:275
  558.9 10.1 %shard_map.117 = f32[32,128,128]{2,1,0:T(8,128)} custom-call(s32[256]{0:T(256)} %get-tuple-element.12.tgt_ref, bf16[256,128,128]{2,1,0:T(8,128)(2,1)} %bitcast.9.ret_ref, f32[256,128]{1,0:T(8,128)} %shard_map.116._), custom_call_target="tpu_custom_call" | custom-call | tf_op jit(solution)/shard_map/pallas_call | solution.py:180
  569.0 5.4 collective-permute-start.2
  574.4 0.0 copy-done.3
  574.4 4.0 collective-permute-done.2
  578.4 3.1 fusion.1
  (8 shorter events, 0.0 us)
Async XLA Ops:
  0.6 289.5 %copy-start = (bf16[16,6144]{1,0:T(8,128)(2,1)S(1)}, bf16[16,6144]{1,0:T(8,128)(2,1)}, u32[]{:S(2)}) copy-start(bf16[16,6144]{1,0:T(8,128)(2,1)} %param.13) | copy-start | bytes 589828
  260.4 11.1 %copy-start.4 = (s32[48,14]{0,1:T(8,128)S(1)}, s32[48,14]{0,1:T(8,128)}, u32[]{:S(2)}) copy-start(s32[48,14]{0,1:T(8,128)} %param.12) | copy-start | bytes 8068
  260.4 121.9 %all-to-all-start = ((bf16[64,4,128,128]{3,2,1,0:T(8,128)(2,1)}), bf16[64,4,128,128]{3,2,1,0:T(8,128)(2,1)}, u32[]{:S(2)}, u32[]{:S(2)}) async-start(bf16[64,4,128,128]{3,2,1,0:T(8,128)(2,1)} %bitcast.20), calls=%async_computation | async-start | bytes 16777216 | tf_op jit(solution)/shard_map/all_to_all | solution.py:243
  271.4 18.7 %copy-start.5 = (bf16[16,128]{1,0:T(8,128)(2,1)S(1)}, bf16[16,128]{1,0:T(8,128)(2,1)}, u32[]{:S(2)}) copy-start(bf16[16,128]{1,0:T(8,128)(2,1)} %param.14) | copy-start | bytes 12292
  433.5 125.4 %all-to-all-start.1 = ((bf16[64,4,128,128]{3,2,1,0:T(8,128)(2,1)}), bf16[64,4,128,128]{3,2,1,0:T(8,128)(2,1)}, u32[]{:S(2)}, u32[]{:S(2)}) async-start(bf16[64,4,128,128]{3,2,1,0:T(8,128)(2,1)} %bitcast.21), calls=%async_computation.1 | async-start | bytes 16777216 | tf_op jit(solution)/shard_map/all_to_all | solution.py:275
  443.9 91.4 %collective-permute-start.1 = (bf16[128,128]{1,0:T(8,128)(2,1)S(1)}, bf16[128,128]{1,0:T(8,128)(2,1)S(1)}, u32[]{:S(2)}, u32[]{:S(2)}) collective-permute-start(bf16[128,128]{1,0:T(8,128)(2,1)S(1)} %get-tuple-element.7), channel_id=1, source_target_pairs={{2,0},{4,2},{6,4},{8,6},{10,8},{12,10},{14,12},{16,14},{18,16},{20... | collective-permute-start | bytes 98312 | tf_op jit(solution)/shard_map/ppermute | solution.py:255
  446.3 89.1 %collective-permute-start = (bf16[128,128]{1,0:T(8,128)(2,1)S(1)}, bf16[128,128]{1,0:T(8,128)(2,1)S(1)}, u32[]{:S(2)}, u32[]{:S(2)}) collective-permute-start(bf16[128,128]{1,0:T(8,128)(2,1)S(1)} %get-tuple-element.6), channel_id=1, source_target_pairs={{0,2},{2,4},{4,6},{6,8},{8,10},{10,12},{12,14},{14,16},{16,18},{18... | collective-permute-start | bytes 98312 | tf_op jit(solution)/shard_map/ppermute | solution.py:254
  558.9 15.5 %copy-start.3 = (f32[256,128]{1,0:T(8,128)S(1)}, f32[256,128]{1,0:T(8,128)}, u32[]{:S(2)}) copy-start(f32[256,128]{1,0:T(8,128)} %shard_map.116._) | copy-start | bytes 393220
  558.9 19.5 %copy-start.2 = (f32[3840,128]{1,0:T(8,128)S(1)}, f32[3840,128]{1,0:T(8,128)}, u32[]{:S(2)}) copy-start(f32[3840,128]{1,0:T(8,128)} %shard_map.114._) | copy-start | bytes 5898244
  569.0 9.4 %collective-permute-start.2 = (f32[4096,128]{1,0:T(8,128)}, f32[4096,128]{1,0:T(8,128)S(1)}, u32[]{:S(2)}, u32[]{:S(2)}) collective-permute-start(f32[4096,128]{1,0:T(8,128)} %bitcast.22), channel_id=1, source_target_pairs={{0,1},{1,0},{2,3},{3,2},{4,5},{5,4},{6,7},{7,6},{8,9},{9,8},{10,11... | collective-permute-start | bytes 6291464 | tf_op jit(solution)/shard_map/ppermute | solution.py:286
  578.4 3.1 copy-start.1

commit v7 on v5

--- a/solution.py
+++ b/solution.py
@@ -16,40 +16,43 @@
 def trip_kernel(
     pair_count, pb_ref, len_ref, inc_ref, qt_ref, tgt_ref, w_ref, _, pred_ref, out_ref, acc_ref
 ):
-    t = pl.program_id(0)
-
-    @pl.when(t == 0)
+    step = pl.program_id(0)
+    per_step = len_ref.shape[0]
+    block = qt_ref.shape[0]
+
+    @pl.when(step == 0)
     def _():
         acc_ref[...] = jnp.zeros_like(acc_ref)
 
-    hidden = None
-    for k in range(0, pair_count, 2):
-        p0 = pb_ref[t * pair_count + k]
-        p1 = pb_ref[t * pair_count + k + 1]
-        lhs = jnp.concatenate([len_ref[0, k], len_ref[0, k + 1]], axis=1)
-        rhs = jnp.concatenate([inc_ref[p0], inc_ref[p1]], axis=0)
-        term = jnp.dot(lhs, rhs, preferred_element_type=F32)
-        hidden = term if hidden is None else hidden + term
-    q_t = qt_ref[...]
-    pred_row = jnp.sum(hidden.T * q_t, axis=0, keepdims=True)
-    pred_ref[0] = pred_row
-    err_row = w_ref[0] * (pred_row - tgt_ref[0])
-    scaled_t = (err_row * q_t).astype(BF16)
-    block = q_t.shape[1]
-    for k in range(0, pair_count, 2):
-        p0 = pb_ref[t * pair_count + k]
-        p1 = pb_ref[t * pair_count + k + 1]
-        rhs = jnp.concatenate([len_ref[0, k], len_ref[0, k + 1]], axis=1)
-        both = jnp.dot(scaled_t, rhs, preferred_element_type=F32)
-        acc_ref[p0] += both[:, :block]
-        acc_ref[p1] += both[:, block:]
-
-    @pl.when(t == pl.num_programs(0) - 1)
+    for u in range(per_step):
+        t = step * per_step + u
+        hidden = None
+        for k in range(0, pair_count, 2):
+            p0 = pb_ref[t * pair_count + k]
+            p1 = pb_ref[t * pair_count + k + 1]
+            lhs = jnp.concatenate([len_ref[u, k], len_ref[u, k + 1]], axis=1)
+            rhs = jnp.concatenate([inc_ref[p0], inc_ref[p1]], axis=0)
+            term = jnp.dot(lhs, rhs, preferred_element_type=F32)
+            hidden = term if hidden is None else hidden + term
+        q_t = qt_ref[:, u * block : (u + 1) * block]
+        pred_row = jnp.sum(hidden.T * q_t, axis=0, keepdims=True)
+        pred_ref[u] = pred_row
+        err_row = w_ref[u] * (pred_row - tgt_ref[u])
+        scaled_t = (err_row * q_t).astype(BF16)
+        for k in range(0, pair_count, 2):
+            p0 = pb_ref[t * pair_count + k]
+            p1 = pb_ref[t * pair_count + k + 1]
+            rhs = jnp.concatenate([len_ref[u, k], len_ref[u, k + 1]], axis=1)
+            both = jnp.dot(scaled_t, rhs, preferred_element_type=F32)
+            acc_ref[p0] += both[:, :block]
+            acc_ref[p1] += both[:, block:]
+
+    @pl.when(step == pl.num_programs(0) - 1)
     def _():
         out_ref[...] = acc_ref[...].astype(out_ref.dtype)
 
 
-def trip_pass(pair_flat, lengths, incoming, query_t, tgt, wts, after):
+def trip_pass(pair_flat, lengths, incoming, query_t, tgt, wts, after, per_step=2):
     trip_blocks, pair_count, block, rank = lengths.shape
     slots = incoming.shape[0]
     const3 = lambda t, pb: (0, 0, 0)
@@ -57,17 +60,17 @@
         functools.partial(trip_kernel, pair_count),
         grid_spec=pltpu.PrefetchScalarGridSpec(
             num_scalar_prefetch=1,
-            grid=(trip_blocks,),
+            grid=(trip_blocks // per_step,),
             in_specs=[
-                pl.BlockSpec((1, pair_count, block, block), lambda t, pb: (t, 0, 0, 0)),
+                pl.BlockSpec((per_step, pair_count, block, block), lambda t, pb: (t, 0, 0, 0)),
                 pl.BlockSpec((slots, block, rank), const3, pipeline_mode=pl.Buffered(1)),
-                pl.BlockSpec((rank, block), lambda t, pb: (0, t)),
-                pl.BlockSpec((1, 1, block), lambda t, pb: (t, 0, 0)),
-                pl.BlockSpec((1, 1, block), lambda t, pb: (t, 0, 0)),
+                pl.BlockSpec((rank, per_step * block), lambda t, pb: (0, t)),
+                pl.BlockSpec((per_step, 1, block), lambda t, pb: (t, 0, 0)),
+                pl.BlockSpec((per_step, 1, block), lambda t, pb: (t, 0, 0)),
                 pl.BlockSpec(memory_space=pl.ANY),
             ],
             out_specs=[
-                pl.BlockSpec((1, 1, block), lambda t, pb: (t, 0, 0)),
+                pl.BlockSpec((per_step, 1, block), lambda t, pb: (t, 0, 0)),
                 pl.BlockSpec((slots, block, rank), const3, pipeline_mode=pl.Buffered(1)),
             ],
             scratch_shapes=[pltpu.VMEM((slots, block, rank), F32)],
@@ -196,6 +199,29 @@
     )(targets, returned, after)
 
 
+def gather_kernel(idx_ref, src_ref, out_ref):
+    c = pl.program_id(0)
+    chunk = out_ref.shape[0]
+    for s in range(chunk):
+        out_ref[s] = src_ref[idx_ref[c * chunk + s]]
+
+
+def gather_blocks(idx, blocks, chunk=32):
+    count = idx.shape[0]
+    return pl.pallas_call(
+        gather_kernel,
+        grid_spec=pltpu.PrefetchScalarGridSpec(
+            num_scalar_prefetch=1,
+            grid=(count // chunk,),
+            in_specs=[
+                pl.BlockSpec(blocks.shape, lambda c, ix: (0, 0, 0), pipeline_mode=pl.Buffered(1))
+            ],
+            out_specs=pl.BlockSpec((chunk,) + blocks.shape[1:], lambda c, ix: (c, 0, 0)),
+        ),
+        out_shape=jax.ShapeDtypeStruct((count,) + blocks.shape[1:], blocks.dtype),
+    )(idx, blocks)
+
+
 def local(
     emb, lengths, pair_block, feats, proj, targets, trip_weight, send_list, nb_index, nb_weight
 ):
@@ -208,7 +234,8 @@
     send_rows = send_list[0, 0]
     live_mask = send_rows >= 0
     slot_count = send_rows.shape[1]
-    outgoing = blocks[jnp.where(live_mask, send_rows, 0)]
+    outgoing = gather_blocks(jnp.where(live_mask, send_rows, 0).reshape(-1), blocks)
+    outgoing = outgoing.reshape(regions, slot_count, block_size, rank_width)
     incoming = lax.all_to_all(outgoing, "region", split_axis=0, concat_axis=0, tiled=True)
     incoming = incoming.reshape(regions * slot_count, block_size, rank_width)
     trip_blocks = lengths.shape[0]

time: 339 us -> 322 us (0.950)
  local copies, waits for them, and re-layouts: 12.6 us -> 3.42 us
  Pallas kernels: 81 us -> 74.6 us
    pallas_call x1, Pallas kernels: 51.2 us -> 38.1 us  [trip_pass(): pl.pallas_call(functools.partial(trip_kernel, pair_count), grid_spec=pltp...]
    gather x1 -> x0, local copies, waits for them, and re-layouts: 9.72 us -> none  [local(): outgoing = blocks[jnp.where(live_mask, send_rows, 0)]]
    pallas_call x0 -> x1, Pallas kernels: none -> 6.57 us  [gather_blocks(): pl.pallas_call(gather_kernel, grid_spec=pltpu.PrefetchScalarGridSpec(num_...]
where the time goes in v7:
time: 322 us; the launch traced here: 318 us
  waiting for transfers between devices  203 us (63%)
  Pallas kernels  74.6 us (23%)
  starting transfers between devices  29.6 us (9%)
  other arithmetic  4.37 us (1%)
  local copies, waits for them, and re-layouts  3.42 us (1%)
    all_to_all x1, waiting for transfers between devices, local(): lax.all_to_all(outgoing, 'region', split_axis=0, concat_axis=0, tiled=True)  89.9 us
    ppermute x1, waiting for transfers between devices, local(): lax.ppermute(head, 'region', [((i + 1) % count, i) for i in range(count)])  88.8 us
    pallas_call x1, Pallas kernels, trip_pass(): pl.pallas_call(functools.partial(trip_kernel, pair_count), grid_spec=pltp...  38.1 us
    all_to_all x1, waiting for transfers between devices, local(): lax.all_to_all(slot_grad.reshape(regions, slot_count, rank_width, block_s...  20.1 us
    pallas_call x1, Pallas kernels, smooth_inner(): pl.pallas_call(smooth_inner_kernel, grid=(inner,), in_specs=[pl.BlockSpec...  17.9 us
    all_to_all x1, starting transfers between devices, local(): lax.all_to_all(outgoing, 'region', split_axis=0, concat_axis=0, tiled=True)  11.2 us
    pallas_call x1, Pallas kernels, owned_pass(): pl.pallas_call(owned_kernel, grid_spec=pltpu.PrefetchScalarGridSpec(num_s...  9.88 us
    all_to_all x1, starting transfers between devices, local(): lax.all_to_all(slot_grad.reshape(regions, slot_count, rank_width, block_s...  9.73 us
  transfers between devices with their start and end apart: 5, of which 4 were waited for; matrix products, arithmetic and copies ran while one was open for 2% of the time, Pallas kernels for 6%

profile of v7, /device:TPU:13, one launch (start us, length us, event | category | flops | bytes accessed | tf_op | source)
XLA Modules:
  0.0 317.8 jit_solution(9963364588330979286)
XLA Ops:
  0.6 0.0 copy-start
  0.6 0.8 copy.13
  1.5 0.1 squeeze.9
  1.6 0.6 compare_select_fusion
  2.2 6.6 %shard_map.113 = bf16[256,128,128]{2,1,0:T(8,128)(2,1)} custom-call(s32[256]{0:T(256)} %get-tuple-element.13.idx_ref, bf16[32,128,128]{2,1,0:T(8,128)(2,1)} %bitcast.23), custom_call_target="tpu_custom_call" | custom-call | tf_op jit(solution)/shard_map/pallas_call | solution.py:211
  8.7 11.2 %all-to-all-start = ((bf16[64,4,128,128]{3,2,1,0:T(8,128)(2,1)}), bf16[64,4,128,128]{3,2,1,0:T(8,128)(2,1)}, u32[]{:S(2)}, u32[]{:S(2)}) async-start(bf16[64,4,128,128]{3,2,1,0:T(8,128)(2,1)} %bitcast.20), calls=%async_computation | async-start | bytes 16777216 | tf_op jit(solution)/shard_map/all_to_all | solution.py:239
  19.9 0.0 copy-done.4
  19.9 0.0 copy-start.5
  19.9 0.1 copy.12
  20.0 0.7 reshape.38.pb_ref
  20.7 17.9 %shard_map.114._ = f32[3840,128]{1,0:T(8,128)} custom-call(bf16[4096,128]{1,0:T(8,128)(2,1)} %emb_ref.1, s32[4,4096]{1,0:T(4,128)} %bitcast.24, f32[4,4096]{1,0:T(4,128)} %bitcast.26), custom_call_target="tpu_custom_call" | custom-call | tf_op jit(solution)/shard_map/pallas_call | solution.py:129
  38.6 0.0 copy-done
  38.6 0.0 copy-done.5
  38.6 2.2 fusion.5.qt_ref
  40.8 89.9 %all-to-all-done = bf16[64,4,128,128]{3,2,1,0:T(8,128)(2,1)} async-done(((bf16[64,4,128,128]{3,2,1,0:T(8,128)(2,1)}), bf16[64,4,128,128]{3,2,1,0:T(8,128)(2,1)}, u32[]{:S(2)}, u32[]{:S(2)}) %all-to-all-start) | async-done | bytes 8388640 | tf_op jit(solution)/shard_map/all_to_all | solution.py:239
  130.8 38.1 %shard_map.115 = (f32[48,1,128]{2,1,0:T(1,128)}, bf16[256,128,128]{2,1,0:T(8,128)(2,1)}) custom-call(s32[672]{0:T(1024)} %reshape.38.pb_ref, bf16[48,14,128,128]{3,2,1,0:T(8,128)(2,1)} %len_ref.1, bf16[256,128,128]{2,1,0:T(8,128)(2,1)} %bitcast.2.inc_ref, f32[128,6144]{1,0:T(8,128)} %fusion.5.qt_ref, f32[48,1,128]{2,1,0:T(1,128)} %bitcast.28, ...), custom_call_target="tpu_custom_call" | custom-call | tf_op jit(solution)/shard_map/pallas_call | solution.py:59
  168.8 9.7 %all-to-all-start.1 = ((bf16[64,4,128,128]{3,2,1,0:T(8,128)(2,1)}), bf16[64,4,128,128]{3,2,1,0:T(8,128)(2,1)}, u32[]{:S(2)}, u32[]{:S(2)}) async-start(bf16[64,4,128,128]{3,2,1,0:T(8,128)(2,1)} %bitcast.21), calls=%async_computation.1 | async-start | bytes 16777216 | tf_op jit(solution)/shard_map/all_to_all | solution.py:271
  178.6 0.8 fusion.2
  179.4 2.4 collective-permute-start.1
  181.8 0.0 collective-permute-start
  181.8 0.9 fusion.3
  182.6 88.8 %collective-permute-done.1 = bf16[128,128]{1,0:T(8,128)(2,1)S(1)} collective-permute-done((bf16[128,128]{1,0:T(8,128)(2,1)S(1)}, bf16[128,128]{1,0:T(8,128)(2,1)S(1)}, u32[]{:S(2)}, u32[]{:S(2)}) %collective-permute-start.1) | collective-permute-done | bytes 32800 | tf_op jit(solution)/shard_map/ppermute | solution.py:251
  271.5 0.0 collective-permute-done
  271.5 0.7 pad_maximum_fusion.win_ref
  272.2 2.2 shard_map.116._
  274.4 20.1 %all-to-all-done.1 = bf16[64,4,128,128]{3,2,1,0:T(8,128)(2,1)} async-done(((bf16[64,4,128,128]{3,2,1,0:T(8,128)(2,1)}), bf16[64,4,128,128]{3,2,1,0:T(8,128)(2,1)}, u32[]{:S(2)}, u32[]{:S(2)}) %all-to-all-start.1) | async-done | bytes 8388640 | tf_op jit(solution)/shard_map/all_to_all | solution.py:271
  294.5 9.9 %shard_map.117 = f32[32,128,128]{2,1,0:T(8,128)} custom-call(s32[256]{0:T(256)} %get-tuple-element.12.tgt_ref, bf16[256,128,128]{2,1,0:T(8,128)(2,1)} %bitcast.9.ret_ref, f32[256,128]{1,0:T(8,128)} %shard_map.116._), custom_call_target="tpu_custom_call" | custom-call | tf_op jit(solution)/shard_map/pallas_call | solution.py:183
  304.4 6.3 %collective-permute-start.2 = (f32[4096,128]{1,0:T(8,128)}, f32[4096,128]{1,0:T(8,128)S(1)}, u32[]{:S(2)}, u32[]{:S(2)}) collective-permute-start(f32[4096,128]{1,0:T(8,128)} %bitcast.22), channel_id=1, source_target_pairs={{0,1},{1,0},{2,3},{3,2},{4,5},{5,4},{6,7},{7,6},{8,9},{9,8},{10,11... | collective-permute-start | bytes 6291464 | tf_op jit(solution)/shard_map/ppermute | solution.py:282
  310.7 0.0 copy-done.3
  310.7 4.0 %collective-permute-done.2 = f32[4096,128]{1,0:T(8,128)S(1)} collective-permute-done((f32[4096,128]{1,0:T(8,128)}, f32[4096,128]{1,0:T(8,128)S(1)}, u32[]{:S(2)}, u32[]{:S(2)}) %collective-permute-start.2) | collective-permute-done | bytes 2097184 | tf_op jit(solution)/shard_map/ppermute | solution.py:282
  314.7 0.0 copy-done.2
  314.7 3.1 fusion.1
  (8 shorter events, 0.0 us)
Async XLA Ops:
  0.6 38.0 %copy-start = (bf16[16,6144]{1,0:T(8,128)(2,1)S(1)}, bf16[16,6144]{1,0:T(8,128)(2,1)}, u32[]{:S(2)}) copy-start(bf16[16,6144]{1,0:T(8,128)(2,1)} %param.13) | copy-start | bytes 589828
  8.7 11.2 %copy-start.4 = (s32[48,14]{0,1:T(8,128)S(1)}, s32[48,14]{0,1:T(8,128)}, u32[]{:S(2)}) copy-start(s32[48,14]{0,1:T(8,128)} %param.12) | copy-start | bytes 8068
  8.7 122.0 %all-to-all-start = ((bf16[64,4,128,128]{3,2,1,0:T(8,128)(2,1)}), bf16[64,4,128,128]{3,2,1,0:T(8,128)(2,1)}, u32[]{:S(2)}, u32[]{:S(2)}) async-start(bf16[64,4,128,128]{3,2,1,0:T(8,128)(2,1)} %bitcast.20), calls=%async_computation | async-start | bytes 16777216 | tf_op jit(solution)/shard_map/all_to_all | solution.py:239
  19.9 18.7 %copy-start.5 = (bf16[16,128]{1,0:T(8,128)(2,1)S(1)}, bf16[16,128]{1,0:T(8,128)(2,1)}, u32[]{:S(2)}) copy-start(bf16[16,128]{1,0:T(8,128)(2,1)} %param.14) | copy-start | bytes 12292
  168.8 125.6 %all-to-all-start.1 = ((bf16[64,4,128,128]{3,2,1,0:T(8,128)(2,1)}), bf16[64,4,128,128]{3,2,1,0:T(8,128)(2,1)}, u32[]{:S(2)}, u32[]{:S(2)}) async-start(bf16[64,4,128,128]{3,2,1,0:T(8,128)(2,1)} %bitcast.21), calls=%async_computation.1 | async-start | bytes 16777216 | tf_op jit(solution)/shard_map/all_to_all | solution.py:271
  179.4 92.1 %collective-permute-start.1 = (bf16[128,128]{1,0:T(8,128)(2,1)S(1)}, bf16[128,128]{1,0:T(8,128)(2,1)S(1)}, u32[]{:S(2)}, u32[]{:S(2)}) collective-permute-start(bf16[128,128]{1,0:T(8,128)(2,1)S(1)} %get-tuple-element.7), channel_id=1, source_target_pairs={{2,0},{4,2},{6,4},{8,6},{10,8},{12,10},{14,12},{16,14},{18,16},{20... | collective-permute-start | bytes 98312 | tf_op jit(solution)/shard_map/ppermute | solution.py:251
  181.8 89.7 %collective-permute-start = (bf16[128,128]{1,0:T(8,128)(2,1)S(1)}, bf16[128,128]{1,0:T(8,128)(2,1)S(1)}, u32[]{:S(2)}, u32[]{:S(2)}) collective-permute-start(bf16[128,128]{1,0:T(8,128)(2,1)S(1)} %get-tuple-element.6), channel_id=1, source_target_pairs={{0,2},{2,4},{4,6},{6,8},{8,10},{10,12},{12,14},{14,16},{16,18},{18... | collective-permute-start | bytes 98312 | tf_op jit(solution)/shard_map/ppermute | solution.py:250
  294.5 16.2 %copy-start.3 = (f32[256,128]{1,0:T(8,128)S(1)}, f32[256,128]{1,0:T(8,128)}, u32[]{:S(2)}) copy-start(f32[256,128]{1,0:T(8,128)} %shard_map.116._) | copy-start | bytes 393220
  294.5 20.2 %copy-start.2 = (f32[3840,128]{1,0:T(8,128)S(1)}, f32[3840,128]{1,0:T(8,128)}, u32[]{:S(2)}) copy-start(f32[3840,128]{1,0:T(8,128)} %shard_map.114._) | copy-start | bytes 5898244
  304.4 10.3 %collective-permute-start.2 = (f32[4096,128]{1,0:T(8,128)}, f32[4096,128]{1,0:T(8,128)S(1)}, u32[]{:S(2)}, u32[]{:S(2)}) collective-permute-start(f32[4096,128]{1,0:T(8,128)} %bitcast.22), channel_id=1, source_target_pairs={{0,1},{1,0},{2,3},{3,2},{4,5},{5,4},{6,7},{7,6},{8,9},{9,8},{10,11... | collective-permute-start | bytes 6291464 | tf_op jit(solution)/shard_map/ppermute | solution.py:282
  314.7 3.1 copy-start.1

commit v8 on v7

--- a/solution.py
+++ b/solution.py
@@ -52,7 +52,7 @@
         out_ref[...] = acc_ref[...].astype(out_ref.dtype)
 
 
-def trip_pass(pair_flat, lengths, incoming, query_t, tgt, wts, after, per_step=2):
+def trip_pass(pair_flat, lengths, incoming, query_t, tgt, wts, after, per_step=4):
     trip_blocks, pair_count, block, rank = lengths.shape
     slots = incoming.shape[0]
     const3 = lambda t, pb: (0, 0, 0)
@@ -206,7 +206,7 @@
         out_ref[s] = src_ref[idx_ref[c * chunk + s]]
 
 
-def gather_blocks(idx, blocks, chunk=32):
+def gather_blocks(idx, blocks, chunk=128):
     count = idx.shape[0]
     return pl.pallas_call(
         gather_kernel,

time: 322 us -> 317 us (0.984)
  Pallas kernels: 74.6 us -> 70.3 us
where the time goes in v8:
time: 317 us; the launch traced here: 312 us
  waiting for transfers between devices  203 us (64%)
  Pallas kernels  70.3 us (22%)
  starting transfers between devices  28.7 us (9%)
  other arithmetic  4.37 us (1%)
  local copies, waits for them, and re-layouts  3.42 us (1%)
    all_to_all x1, waiting for transfers between devices, local(): lax.all_to_all(outgoing, 'region', split_axis=0, concat_axis=0, tiled=True)  89.9 us
    ppermute x1, waiting for transfers between devices, local(): lax.ppermute(head, 'region', [((i + 1) % count, i) for i in range(count)])  86.8 us
    pallas_call x1, Pallas kernels, trip_pass(): pl.pallas_call(functools.partial(trip_kernel, pair_count), grid_spec=pltp...  34.9 us
    all_to_all x1, waiting for transfers between devices, local(): lax.all_to_all(slot_grad.reshape(regions, slot_count, rank_width, block_s...  21.9 us
    pallas_call x1, Pallas kernels, smooth_inner(): pl.pallas_call(smooth_inner_kernel, grid=(inner,), in_specs=[pl.BlockSpec...  17.9 us
    all_to_all x1, starting transfers between devices, local(): lax.all_to_all(outgoing, 'region', split_axis=0, concat_axis=0, tiled=True)  11.2 us
    pallas_call x1, Pallas kernels, owned_pass(): pl.pallas_call(owned_kernel, grid_spec=pltpu.PrefetchScalarGridSpec(num_s...  9.84 us
    all_to_all x1, starting transfers between devices, local(): lax.all_to_all(slot_grad.reshape(regions, slot_count, rank_width, block_s...  9.75 us
  transfers between devices with their start and end apart: 5, of which 4 were waited for; matrix products, arithmetic and copies ran while one was open for 2% of the time, Pallas kernels for 6%

profile of v8, /device:TPU:13, one launch (start us, length us, event | category | flops | bytes accessed | tf_op | source)
XLA Modules:
  0.0 312.3 jit_solution(11948629920168327377)
XLA Ops:
  0.6 0.0 copy-start
  0.6 0.8 copy.13
  1.5 0.1 squeeze.9
  1.6 0.6 compare_select_fusion
  2.2 5.5 %shard_map.113 = bf16[256,128,128]{2,1,0:T(8,128)(2,1)} custom-call(s32[256]{0:T(256)} %get-tuple-element.13.idx_ref, bf16[32,128,128]{2,1,0:T(8,128)(2,1)} %bitcast.23), custom_call_target="tpu_custom_call" | custom-call | tf_op jit(solution)/shard_map/pallas_call | solution.py:211
  7.6 11.2 %all-to-all-start = ((bf16[64,4,128,128]{3,2,1,0:T(8,128)(2,1)}), bf16[64,4,128,128]{3,2,1,0:T(8,128)(2,1)}, u32[]{:S(2)}, u32[]{:S(2)}) async-start(bf16[64,4,128,128]{3,2,1,0:T(8,128)(2,1)} %bitcast.20), calls=%async_computation | async-start | bytes 16777216 | tf_op jit(solution)/shard_map/all_to_all | solution.py:239
  18.8 0.0 copy-done.4
  18.8 0.0 copy-start.5
  18.8 0.1 copy.12
  18.9 0.7 reshape.38.pb_ref
  19.6 17.9 %shard_map.114._ = f32[3840,128]{1,0:T(8,128)} custom-call(bf16[4096,128]{1,0:T(8,128)(2,1)} %emb_ref.1, s32[4,4096]{1,0:T(4,128)} %bitcast.24, f32[4,4096]{1,0:T(4,128)} %bitcast.26), custom_call_target="tpu_custom_call" | custom-call | tf_op jit(solution)/shard_map/pallas_call | solution.py:129
  37.5 0.0 copy-done
  37.5 0.0 copy-done.5
  37.5 2.2 fusion.5.qt_ref
  39.7 89.9 %all-to-all-done = bf16[64,4,128,128]{3,2,1,0:T(8,128)(2,1)} async-done(((bf16[64,4,128,128]{3,2,1,0:T(8,128)(2,1)}), bf16[64,4,128,128]{3,2,1,0:T(8,128)(2,1)}, u32[]{:S(2)}, u32[]{:S(2)}) %all-to-all-start) | async-done | bytes 8388640 | tf_op jit(solution)/shard_map/all_to_all | solution.py:239
  129.6 34.9 %shard_map.115 = (f32[48,1,128]{2,1,0:T(1,128)}, bf16[256,128,128]{2,1,0:T(8,128)(2,1)}) custom-call(s32[672]{0:T(1024)} %reshape.38.pb_ref, bf16[48,14,128,128]{3,2,1,0:T(8,128)(2,1)} %len_ref.1, bf16[256,128,128]{2,1,0:T(8,128)(2,1)} %bitcast.2.inc_ref, f32[128,6144]{1,0:T(8,128)} %fusion.5.qt_ref, f32[48,1,128]{2,1,0:T(1,128)} %bitcast.28, ...), custom_call_target="tpu_custom_call" | custom-call | tf_op jit(solution)/shard_map/pallas_call | solution.py:59
  164.5 9.7 %all-to-all-start.1 = ((bf16[64,4,128,128]{3,2,1,0:T(8,128)(2,1)}), bf16[64,4,128,128]{3,2,1,0:T(8,128)(2,1)}, u32[]{:S(2)}, u32[]{:S(2)}) async-start(bf16[64,4,128,128]{3,2,1,0:T(8,128)(2,1)} %bitcast.21), calls=%async_computation.1 | async-start | bytes 16777216 | tf_op jit(solution)/shard_map/all_to_all | solution.py:271
  174.3 0.8 fusion.2
  175.1 2.4 collective-permute-start.1
  177.5 0.0 collective-permute-start
  177.5 0.9 fusion.3
  178.4 86.8 %collective-permute-done.1 = bf16[128,128]{1,0:T(8,128)(2,1)S(1)} collective-permute-done((bf16[128,128]{1,0:T(8,128)(2,1)S(1)}, bf16[128,128]{1,0:T(8,128)(2,1)S(1)}, u32[]{:S(2)}, u32[]{:S(2)}) %collective-permute-start.1) | collective-permute-done | bytes 32800 | tf_op jit(solution)/shard_map/ppermute | solution.py:251
  265.2 0.0 collective-permute-done
  265.2 0.7 pad_maximum_fusion.win_ref
  265.9 2.2 shard_map.116._
  268.1 21.9 %all-to-all-done.1 = bf16[64,4,128,128]{3,2,1,0:T(8,128)(2,1)} async-done(((bf16[64,4,128,128]{3,2,1,0:T(8,128)(2,1)}), bf16[64,4,128,128]{3,2,1,0:T(8,128)(2,1)}, u32[]{:S(2)}, u32[]{:S(2)}) %all-to-all-start.1) | async-done | bytes 8388640 | tf_op jit(solution)/shard_map/all_to_all | solution.py:271
  290.0 9.8 %shard_map.117 = f32[32,128,128]{2,1,0:T(8,128)} custom-call(s32[256]{0:T(256)} %get-tuple-element.12.tgt_ref, bf16[256,128,128]{2,1,0:T(8,128)(2,1)} %bitcast.9.ret_ref, f32[256,128]{1,0:T(8,128)} %shard_map.116._), custom_call_target="tpu_custom_call" | custom-call | tf_op jit(solution)/shard_map/pallas_call | solution.py:183
  299.8 5.4 %collective-permute-start.2 = (f32[4096,128]{1,0:T(8,128)}, f32[4096,128]{1,0:T(8,128)S(1)}, u32[]{:S(2)}, u32[]{:S(2)}) collective-permute-start(f32[4096,128]{1,0:T(8,128)} %bitcast.22), channel_id=1, source_target_pairs={{0,1},{1,0},{2,3},{3,2},{4,5},{5,4},{6,7},{7,6},{8,9},{9,8},{10,11... | collective-permute-start | bytes 6291464 | tf_op jit(solution)/shard_map/ppermute | solution.py:282
  305.3 0.0 copy-done.3
  305.3 4.0 %collective-permute-done.2 = f32[4096,128]{1,0:T(8,128)S(1)} collective-permute-done((f32[4096,128]{1,0:T(8,128)}, f32[4096,128]{1,0:T(8,128)S(1)}, u32[]{:S(2)}, u32[]{:S(2)}) %collective-permute-start.2) | collective-permute-done | bytes 2097184 | tf_op jit(solution)/shard_map/ppermute | solution.py:282
  309.3 0.0 copy-done.2
  309.3 3.1 fusion.1
  (8 shorter events, 0.0 us)
Async XLA Ops:
  0.6 36.8 %copy-start = (bf16[16,6144]{1,0:T(8,128)(2,1)S(1)}, bf16[16,6144]{1,0:T(8,128)(2,1)}, u32[]{:S(2)}) copy-start(bf16[16,6144]{1,0:T(8,128)(2,1)} %param.13) | copy-start | bytes 589828
  7.6 11.2 %copy-start.4 = (s32[48,14]{0,1:T(8,128)S(1)}, s32[48,14]{0,1:T(8,128)}, u32[]{:S(2)}) copy-start(s32[48,14]{0,1:T(8,128)} %param.12) | copy-start | bytes 8068
  7.6 122.0 %all-to-all-start = ((bf16[64,4,128,128]{3,2,1,0:T(8,128)(2,1)}), bf16[64,4,128,128]{3,2,1,0:T(8,128)(2,1)}, u32[]{:S(2)}, u32[]{:S(2)}) async-start(bf16[64,4,128,128]{3,2,1,0:T(8,128)(2,1)} %bitcast.20), calls=%async_computation | async-start | bytes 16777216 | tf_op jit(solution)/shard_map/all_to_all | solution.py:239
  18.8 18.7 %copy-start.5 = (bf16[16,128]{1,0:T(8,128)(2,1)S(1)}, bf16[16,128]{1,0:T(8,128)(2,1)}, u32[]{:S(2)}) copy-start(bf16[16,128]{1,0:T(8,128)(2,1)} %param.14) | copy-start | bytes 12292
  164.5 125.4 %all-to-all-start.1 = ((bf16[64,4,128,128]{3,2,1,0:T(8,128)(2,1)}), bf16[64,4,128,128]{3,2,1,0:T(8,128)(2,1)}, u32[]{:S(2)}, u32[]{:S(2)}) async-start(bf16[64,4,128,128]{3,2,1,0:T(8,128)(2,1)} %bitcast.21), calls=%async_computation.1 | async-start | bytes 16777216 | tf_op jit(solution)/shard_map/all_to_all | solution.py:271
  175.1 90.1 %collective-permute-start.1 = (bf16[128,128]{1,0:T(8,128)(2,1)S(1)}, bf16[128,128]{1,0:T(8,128)(2,1)S(1)}, u32[]{:S(2)}, u32[]{:S(2)}) collective-permute-start(bf16[128,128]{1,0:T(8,128)(2,1)S(1)} %get-tuple-element.7), channel_id=1, source_target_pairs={{2,0},{4,2},{6,4},{8,6},{10,8},{12,10},{14,12},{16,14},{18,16},{20... | collective-permute-start | bytes 98312 | tf_op jit(solution)/shard_map/ppermute | solution.py:251
  177.5 87.7 %collective-permute-start = (bf16[128,128]{1,0:T(8,128)(2,1)S(1)}, bf16[128,128]{1,0:T(8,128)(2,1)S(1)}, u32[]{:S(2)}, u32[]{:S(2)}) collective-permute-start(bf16[128,128]{1,0:T(8,128)(2,1)S(1)} %get-tuple-element.6), channel_id=1, source_target_pairs={{0,2},{2,4},{4,6},{6,8},{8,10},{10,12},{12,14},{14,16},{16,18},{18... | collective-permute-start | bytes 98312 | tf_op jit(solution)/shard_map/ppermute | solution.py:250
  290.0 15.3 %copy-start.3 = (f32[256,128]{1,0:T(8,128)S(1)}, f32[256,128]{1,0:T(8,128)}, u32[]{:S(2)}) copy-start(f32[256,128]{1,0:T(8,128)} %shard_map.116._) | copy-start | bytes 393220
  290.0 19.3 %copy-start.2 = (f32[3840,128]{1,0:T(8,128)S(1)}, f32[3840,128]{1,0:T(8,128)}, u32[]{:S(2)}) copy-start(f32[3840,128]{1,0:T(8,128)} %shard_map.114._) | copy-start | bytes 5898244
  299.8 9.4 %collective-permute-start.2 = (f32[4096,128]{1,0:T(8,128)}, f32[4096,128]{1,0:T(8,128)S(1)}, u32[]{:S(2)}, u32[]{:S(2)}) collective-permute-start(f32[4096,128]{1,0:T(8,128)} %bitcast.22), channel_id=1, source_target_pairs={{0,1},{1,0},{2,3},{3,2},{4,5},{5,4},{6,7},{7,6},{8,9},{9,8},{10,11... | collective-permute-start | bytes 6291464 | tf_op jit(solution)/shard_map/ppermute | solution.py:282
  309.3 3.1 copy-start.1

commit v9 on v8

--- a/solution.py
+++ b/solution.py
@@ -14,7 +14,8 @@
 
 
 def trip_kernel(
-    pair_count, pb_ref, len_ref, inc_ref, qt_ref, tgt_ref, w_ref, _, pred_ref, out_ref, acc_ref
+    pair_count, trip_steps, pb_ref, len_ref, inc_ref, qt_ref, tgt_ref, w_ref, _, pred_ref, out_ref,
+    acc_ref,
 ):
     step = pl.program_id(0)
     per_step = len_ref.shape[0]
@@ -24,54 +25,66 @@
     def _():
         acc_ref[...] = jnp.zeros_like(acc_ref)
 
-    for u in range(per_step):
-        t = step * per_step + u
-        hidden = None
-        for k in range(0, pair_count, 2):
-            p0 = pb_ref[t * pair_count + k]
-            p1 = pb_ref[t * pair_count + k + 1]
-            lhs = jnp.concatenate([len_ref[u, k], len_ref[u, k + 1]], axis=1)
-            rhs = jnp.concatenate([inc_ref[p0], inc_ref[p1]], axis=0)
-            term = jnp.dot(lhs, rhs, preferred_element_type=F32)
-            hidden = term if hidden is None else hidden + term
-        q_t = qt_ref[:, u * block : (u + 1) * block]
-        pred_row = jnp.sum(hidden.T * q_t, axis=0, keepdims=True)
-        pred_ref[u] = pred_row
-        err_row = w_ref[u] * (pred_row - tgt_ref[u])
-        scaled_t = (err_row * q_t).astype(BF16)
-        for k in range(0, pair_count, 2):
-            p0 = pb_ref[t * pair_count + k]
-            p1 = pb_ref[t * pair_count + k + 1]
-            rhs = jnp.concatenate([len_ref[u, k], len_ref[u, k + 1]], axis=1)
-            both = jnp.dot(scaled_t, rhs, preferred_element_type=F32)
-            acc_ref[p0] += both[:, :block]
-            acc_ref[p1] += both[:, block:]
-
-    @pl.when(step == pl.num_programs(0) - 1)
-    def _():
-        out_ref[...] = acc_ref[...].astype(out_ref.dtype)
-
-
-def trip_pass(pair_flat, lengths, incoming, query_t, tgt, wts, after, per_step=4):
+    @pl.when(step < trip_steps)
+    def _():
+        for u in range(per_step):
+            t = step * per_step + u
+            hidden = None
+            for k in range(0, pair_count, 2):
+                p0 = pb_ref[t * pair_count + k]
+                p1 = pb_ref[t * pair_count + k + 1]
+                lhs = jnp.concatenate([len_ref[u, k], len_ref[u, k + 1]], axis=1)
+                rhs = jnp.concatenate([inc_ref[p0], inc_ref[p1]], axis=0)
+                term = jnp.dot(lhs, rhs, preferred_element_type=F32)
+                hidden = term if hidden is None else hidden + term
+            q_t = qt_ref[:, u * block : (u + 1) * block]
+            pred_row = jnp.sum(hidden.T * q_t, axis=0, keepdims=True)
+            pred_ref[u] = pred_row
+            err_row = w_ref[u] * (pred_row - tgt_ref[u])
+            scaled_t = (err_row * q_t).astype(BF16)
+            for k in range(0, pair_count, 2):
+                p0 = pb_ref[t * pair_count + k]
+                p1 = pb_ref[t * pair_count + k + 1]
+                rhs = jnp.concatenate([len_ref[u, k], len_ref[u, k + 1]], axis=1)
+                both = jnp.dot(scaled_t, rhs, preferred_element_type=F32)
+                acc_ref[p0] += both[:, :block]
+                acc_ref[p1] += both[:, block:]
+
+    @pl.when(step >= trip_steps)
+    def _():
+        chunk = out_ref.shape[0]
+        first = pl.multiple_of((step - trip_steps) * chunk, chunk)
+        out_ref[...] = acc_ref[pl.ds(first, chunk)].astype(out_ref.dtype)
+
+
+def trip_pass(pair_flat, lengths, incoming, query_t, tgt, wts, after, per_step=4, flush=4):
     trip_blocks, pair_count, block, rank = lengths.shape
     slots = incoming.shape[0]
+    trip_steps = trip_blocks // per_step
+    chunk = slots // flush
+    last = trip_steps - 1
     const3 = lambda t, pb: (0, 0, 0)
     return pl.pallas_call(
-        functools.partial(trip_kernel, pair_count),
+        functools.partial(trip_kernel, pair_count, trip_steps),
         grid_spec=pltpu.PrefetchScalarGridSpec(
             num_scalar_prefetch=1,
-            grid=(trip_blocks // per_step,),
+            grid=(trip_steps + flush,),
             in_specs=[
-                pl.BlockSpec((per_step, pair_count, block, block), lambda t, pb: (t, 0, 0, 0)),
+                pl.BlockSpec(
+                    (per_step, pair_count, block, block),
+                    lambda t, pb: (jnp.minimum(t, last), 0, 0, 0),
+                ),
                 pl.BlockSpec((slots, block, rank), const3, pipeline_mode=pl.Buffered(1)),
-                pl.BlockSpec((rank, per_step * block), lambda t, pb: (0, t)),
-                pl.BlockSpec((per_step, 1, block), lambda t, pb: (t, 0, 0)),
-                pl.BlockSpec((per_step, 1, block), lambda t, pb: (t, 0, 0)),
+                pl.BlockSpec((rank, per_step * block), lambda t, pb: (0, jnp.minimum(t, last))),
+                pl.BlockSpec((per_step, 1, block), lambda t, pb: (jnp.minimum(t, last), 0, 0)),
+                pl.BlockSpec((per_step, 1, block), lambda t, pb: (jnp.minimum(t, last), 0, 0)),
                 pl.BlockSpec(memory_space=pl.ANY),
             ],
             out_specs=[
-                pl.BlockSpec((per_step, 1, block), lambda t, pb: (t, 0, 0)),
-                pl.BlockSpec((slots, block, rank), const3, pipeline_mode=pl.Buffered(1)),
+                pl.BlockSpec((per_step, 1, block), lambda t, pb: (jnp.minimum(t, last), 0, 0)),
+                pl.BlockSpec(
+                    (chunk, block, rank), lambda t, pb: (jnp.maximum(t - trip_steps, 0), 0, 0)
+                ),
             ],
             scratch_shapes=[pltpu.VMEM((slots, block, rank), F32)],
         ),
@@ -157,28 +170,28 @@
     )(windows, nb_t, w_t)
 
 
-def owned_kernel(tgt_ref, ret_ref, _, out_ref, acc_ref):
+def owned_kernel(tgt_ref, ret_ref, _, out_ref):
     c = pl.program_id(0)
     chunk = ret_ref.shape[0]
 
     @pl.when(c == 0)
     def _():
-        acc_ref[...] = jnp.zeros_like(acc_ref)
+        out_ref[...] = jnp.zeros_like(out_ref)
 
     for s in range(chunk):
         b = tgt_ref[c * chunk + s]
 
         @pl.when(b >= 0)
         def _():
-            acc_ref[b] += ret_ref[s].astype(F32)
+            out_ref[b] += ret_ref[s].astype(F32)
 
     @pl.when(c == pl.num_programs(0) - 1)
     def _():
-        for b in range(acc_ref.shape[0]):
-            out_ref[b] = acc_ref[b].T
-
-
-def owned_pass(targets, returned, after, block_count, chunk=32):
+        for b in range(out_ref.shape[0]):
+            out_ref[b] = out_ref[b].T
+
+
+def owned_pass(targets, returned, after, block_count, chunk=64):
     slots, rank, block = returned.shape
     return pl.pallas_call(
         owned_kernel,
@@ -190,11 +203,10 @@
                 pl.BlockSpec(memory_space=pl.ANY),
             ],
             out_specs=pl.BlockSpec(
-                (block_count, block, rank), lambda c, tg: (0, 0, 0), pipeline_mode=pl.Buffered(1)
+                (block_count, rank, block), lambda c, tg: (0, 0, 0), pipeline_mode=pl.Buffered(1)
             ),
-            scratch_shapes=[pltpu.VMEM((block_count, rank, block), F32)],
         ),
-        out_shape=jax.ShapeDtypeStruct((block_count, block, rank), F32),
+        out_shape=jax.ShapeDtypeStruct((block_count, rank, block), F32),
         compiler_params=pltpu.CompilerParams(dimension_semantics=("arbitrary",)),
     )(targets, returned, after)
 

time: 317 us -> 315 us (level)
  no operation moved by 1% of the time
where the time goes in v9:
time: 315 us; the launch traced here: 311 us
  waiting for transfers between devices  203 us (64%)
  Pallas kernels  68.9 us (22%)
  starting transfers between devices  28.4 us (9%)
  other arithmetic  4.37 us (1%)
  local copies, waits for them, and re-layouts  3.42 us (1%)
    all_to_all x1, waiting for transfers between devices, local(): lax.all_to_all(outgoing, 'region', split_axis=0, concat_axis=0, tiled=True)  89.9 us
    ppermute x1, waiting for transfers between devices, local(): lax.ppermute(head, 'region', [((i + 1) % count, i) for i in range(count)])  88.4 us
    pallas_call x1, Pallas kernels, trip_pass(): pl.pallas_call(functools.partial(trip_kernel, pair_count, trip_steps), gr...  34.9 us
    all_to_all x1, waiting for transfers between devices, local(): lax.all_to_all(slot_grad.reshape(regions, slot_count, rank_width, block_s...  20.5 us
    pallas_call x1, Pallas kernels, smooth_inner(): pl.pallas_call(smooth_inner_kernel, grid=(inner,), in_specs=[pl.BlockSpec...  17.9 us
    all_to_all x1, starting transfers between devices, local(): lax.all_to_all(outgoing, 'region', split_axis=0, concat_axis=0, tiled=True)  11.2 us
    all_to_all x1, starting transfers between devices, local(): lax.all_to_all(slot_grad.reshape(regions, slot_count, rank_width, block_s...  9.65 us
    pallas_call x1, Pallas kernels, owned_pass(): pl.pallas_call(owned_kernel, grid_spec=pltpu.PrefetchScalarGridSpec(num_s...  8.48 us
  transfers between devices with their start and end apart: 5, of which 4 were waited for; matrix products, arithmetic and copies ran while one was open for 2% of the time, Pallas kernels for 6%

profile of v9, /device:TPU:13, one launch (start us, length us, event | category | flops | bytes accessed | tf_op | source)
XLA Modules:
  0.0 310.9 jit_solution(18202264834795357932)
XLA Ops:
  0.6 0.0 copy-start
  0.6 0.8 copy.13
  1.5 0.1 squeeze.9
  1.6 0.6 compare_select_fusion
  2.2 5.5 %shard_map.113 = bf16[256,128,128]{2,1,0:T(8,128)(2,1)} custom-call(s32[256]{0:T(256)} %get-tuple-element.13.idx_ref, bf16[32,128,128]{2,1,0:T(8,128)(2,1)} %bitcast.23), custom_call_target="tpu_custom_call" | custom-call | tf_op jit(solution)/shard_map/pallas_call | solution.py:223
  7.6 11.2 %all-to-all-start = ((bf16[64,4,128,128]{3,2,1,0:T(8,128)(2,1)}), bf16[64,4,128,128]{3,2,1,0:T(8,128)(2,1)}, u32[]{:S(2)}, u32[]{:S(2)}) async-start(bf16[64,4,128,128]{3,2,1,0:T(8,128)(2,1)} %bitcast.20), calls=%async_computation | async-start | bytes 16777216 | tf_op jit(solution)/shard_map/all_to_all | solution.py:251
  18.8 0.0 copy-done.4
  18.8 0.0 copy-start.5
  18.8 0.1 copy.12
  18.9 0.7 reshape.38.pb_ref
  19.6 17.9 %shard_map.114._ = f32[3840,128]{1,0:T(8,128)} custom-call(bf16[4096,128]{1,0:T(8,128)(2,1)} %emb_ref.1, s32[4,4096]{1,0:T(4,128)} %bitcast.24, f32[4,4096]{1,0:T(4,128)} %bitcast.26), custom_call_target="tpu_custom_call" | custom-call | tf_op jit(solution)/shard_map/pallas_call | solution.py:142
  37.5 0.0 copy-done
  37.5 0.0 copy-done.5
  37.5 2.2 fusion.5.qt_ref
  39.7 89.9 %all-to-all-done = bf16[64,4,128,128]{3,2,1,0:T(8,128)(2,1)} async-done(((bf16[64,4,128,128]{3,2,1,0:T(8,128)(2,1)}), bf16[64,4,128,128]{3,2,1,0:T(8,128)(2,1)}, u32[]{:S(2)}, u32[]{:S(2)}) %all-to-all-start) | async-done | bytes 8388640 | tf_op jit(solution)/shard_map/all_to_all | solution.py:251
  129.6 34.9 %shard_map.115 = (f32[48,1,128]{2,1,0:T(1,128)}, bf16[256,128,128]{2,1,0:T(8,128)(2,1)}) custom-call(s32[672]{0:T(1024)} %reshape.38.pb_ref, bf16[48,14,128,128]{3,2,1,0:T(8,128)(2,1)} %len_ref.1, bf16[256,128,128]{2,1,0:T(8,128)(2,1)} %bitcast.2.inc_ref, f32[128,6144]{1,0:T(8,128)} %fusion.5.qt_ref, f32[48,1,128]{2,1,0:T(1,128)} %bitcast.28, ...), custom_call_target="tpu_custom_call" | custom-call | tf_op jit(solution)/shard_map/pallas_call | solution.py:67
  164.5 9.6 %all-to-all-start.1 = ((bf16[64,4,128,128]{3,2,1,0:T(8,128)(2,1)}), bf16[64,4,128,128]{3,2,1,0:T(8,128)(2,1)}, u32[]{:S(2)}, u32[]{:S(2)}) async-start(bf16[64,4,128,128]{3,2,1,0:T(8,128)(2,1)} %bitcast.21), calls=%async_computation.1 | async-start | bytes 16777216 | tf_op jit(solution)/shard_map/all_to_all | solution.py:283
  174.2 0.8 fusion.2
  175.0 2.4 collective-permute-start.1
  177.4 0.0 collective-permute-start
  177.4 0.9 fusion.3
  178.3 88.4 %collective-permute-done.1 = bf16[128,128]{1,0:T(8,128)(2,1)S(1)} collective-permute-done((bf16[128,128]{1,0:T(8,128)(2,1)S(1)}, bf16[128,128]{1,0:T(8,128)(2,1)S(1)}, u32[]{:S(2)}, u32[]{:S(2)}) %collective-permute-start.1) | collective-permute-done | bytes 32800 | tf_op jit(solution)/shard_map/ppermute | solution.py:263
  266.6 0.0 collective-permute-done
  266.6 0.7 pad_maximum_fusion.win_ref
  267.3 2.2 shard_map.116._
  269.5 20.5 %all-to-all-done.1 = bf16[64,4,128,128]{3,2,1,0:T(8,128)(2,1)} async-done(((bf16[64,4,128,128]{3,2,1,0:T(8,128)(2,1)}), bf16[64,4,128,128]{3,2,1,0:T(8,128)(2,1)}, u32[]{:S(2)}, u32[]{:S(2)}) %all-to-all-start.1) | async-done | bytes 8388640 | tf_op jit(solution)/shard_map/all_to_all | solution.py:283
  290.1 8.5 %shard_map.117 = f32[32,128,128]{2,1,0:T(8,128)} custom-call(s32[256]{0:T(256)} %get-tuple-element.12.tgt_ref, bf16[256,128,128]{2,1,0:T(8,128)(2,1)} %bitcast.9.ret_ref, f32[256,128]{1,0:T(8,128)} %shard_map.116._), custom_call_target="tpu_custom_call" | custom-call | tf_op jit(solution)/shard_map/pallas_call | solution.py:196
  298.5 5.2 %collective-permute-start.2 = (f32[4096,128]{1,0:T(8,128)}, f32[4096,128]{1,0:T(8,128)S(1)}, u32[]{:S(2)}, u32[]{:S(2)}) collective-permute-start(f32[4096,128]{1,0:T(8,128)} %bitcast.22), channel_id=1, source_target_pairs={{0,1},{1,0},{2,3},{3,2},{4,5},{5,4},{6,7},{7,6},{8,9},{9,8},{10,11... | collective-permute-start | bytes 6291464 | tf_op jit(solution)/shard_map/ppermute | solution.py:294
  303.8 0.0 copy-done.3
  303.8 4.0 %collective-permute-done.2 = f32[4096,128]{1,0:T(8,128)S(1)} collective-permute-done((f32[4096,128]{1,0:T(8,128)}, f32[4096,128]{1,0:T(8,128)S(1)}, u32[]{:S(2)}, u32[]{:S(2)}) %collective-permute-start.2) | collective-permute-done | bytes 2097184 | tf_op jit(solution)/shard_map/ppermute | solution.py:294
  307.8 0.0 copy-done.2
  307.8 3.1 fusion.1
  (8 shorter events, 0.0 us)
Async XLA Ops:
  0.6 36.8 %copy-start = (bf16[16,6144]{1,0:T(8,128)(2,1)S(1)}, bf16[16,6144]{1,0:T(8,128)(2,1)}, u32[]{:S(2)}) copy-start(bf16[16,6144]{1,0:T(8,128)(2,1)} %param.13) | copy-start | bytes 589828
  7.6 11.2 %copy-start.4 = (s32[48,14]{0,1:T(8,128)S(1)}, s32[48,14]{0,1:T(8,128)}, u32[]{:S(2)}) copy-start(s32[48,14]{0,1:T(8,128)} %param.12) | copy-start | bytes 8068
  7.6 122.0 %all-to-all-start = ((bf16[64,4,128,128]{3,2,1,0:T(8,128)(2,1)}), bf16[64,4,128,128]{3,2,1,0:T(8,128)(2,1)}, u32[]{:S(2)}, u32[]{:S(2)}) async-start(bf16[64,4,128,128]{3,2,1,0:T(8,128)(2,1)} %bitcast.20), calls=%async_computation | async-start | bytes 16777216 | tf_op jit(solution)/shard_map/all_to_all | solution.py:251
  18.8 18.7 %copy-start.5 = (bf16[16,128]{1,0:T(8,128)(2,1)S(1)}, bf16[16,128]{1,0:T(8,128)(2,1)}, u32[]{:S(2)}) copy-start(bf16[16,128]{1,0:T(8,128)(2,1)} %param.14) | copy-start | bytes 12292
  164.5 125.5 %all-to-all-start.1 = ((bf16[64,4,128,128]{3,2,1,0:T(8,128)(2,1)}), bf16[64,4,128,128]{3,2,1,0:T(8,128)(2,1)}, u32[]{:S(2)}, u32[]{:S(2)}) async-start(bf16[64,4,128,128]{3,2,1,0:T(8,128)(2,1)} %bitcast.21), calls=%async_computation.1 | async-start | bytes 16777216 | tf_op jit(solution)/shard_map/all_to_all | solution.py:283
  175.0 91.6 %collective-permute-start.1 = (bf16[128,128]{1,0:T(8,128)(2,1)S(1)}, bf16[128,128]{1,0:T(8,128)(2,1)S(1)}, u32[]{:S(2)}, u32[]{:S(2)}) collective-permute-start(bf16[128,128]{1,0:T(8,128)(2,1)S(1)} %get-tuple-element.7), channel_id=1, source_target_pairs={{2,0},{4,2},{6,4},{8,6},{10,8},{12,10},{14,12},{16,14},{18,16},{20... | collective-permute-start | bytes 98312 | tf_op jit(solution)/shard_map/ppermute | solution.py:263
  177.4 89.3 %collective-permute-start = (bf16[128,128]{1,0:T(8,128)(2,1)S(1)}, bf16[128,128]{1,0:T(8,128)(2,1)S(1)}, u32[]{:S(2)}, u32[]{:S(2)}) collective-permute-start(bf16[128,128]{1,0:T(8,128)(2,1)S(1)} %get-tuple-element.6), channel_id=1, source_target_pairs={{0,2},{2,4},{4,6},{6,8},{8,10},{10,12},{12,14},{14,16},{16,18},{18... | collective-permute-start | bytes 98312 | tf_op jit(solution)/shard_map/ppermute | solution.py:262
  290.1 13.7 %copy-start.3 = (f32[256,128]{1,0:T(8,128)S(1)}, f32[256,128]{1,0:T(8,128)}, u32[]{:S(2)}) copy-start(f32[256,128]{1,0:T(8,128)} %shard_map.116._) | copy-start | bytes 393220
  290.1 17.7 %copy-start.2 = (f32[3840,128]{1,0:T(8,128)S(1)}, f32[3840,128]{1,0:T(8,128)}, u32[]{:S(2)}) copy-start(f32[3840,128]{1,0:T(8,128)} %shard_map.114._) | copy-start | bytes 5898244
  298.5 9.2 %collective-permute-start.2 = (f32[4096,128]{1,0:T(8,128)}, f32[4096,128]{1,0:T(8,128)S(1)}, u32[]{:S(2)}, u32[]{:S(2)}) collective-permute-start(f32[4096,128]{1,0:T(8,128)} %bitcast.22), channel_id=1, source_target_pairs={{0,1},{1,0},{2,3},{3,2},{4,5},{5,4},{6,7},{7,6},{8,9},{9,8},{10,11... | collective-permute-start | bytes 6291464 | tf_op jit(solution)/shard_map/ppermute | solution.py:294
  307.8 3.1 copy-start.1

commit v10 on v9

--- a/solution.py
+++ b/solution.py
@@ -57,7 +57,7 @@
         out_ref[...] = acc_ref[pl.ds(first, chunk)].astype(out_ref.dtype)
 
 
-def trip_pass(pair_flat, lengths, incoming, query_t, tgt, wts, after, per_step=4, flush=4):
+def trip_pass(pair_flat, lengths, incoming, query_t, tgt, wts, after, per_step=8, flush=4):
     trip_blocks, pair_count, block, rank = lengths.shape
     slots = incoming.shape[0]
     trip_steps = trip_blocks // per_step
@@ -191,7 +191,7 @@
             out_ref[b] = out_ref[b].T
 
 
-def owned_pass(targets, returned, after, block_count, chunk=64):
+def owned_pass(targets, returned, after, block_count, chunk=128):
     slots, rank, block = returned.shape
     return pl.pallas_call(
         owned_kernel,

time: 315 us -> 314 us (level)
  no operation moved by 1% of the time
where the time goes in v10:
time: 314 us; the launch traced here: 309 us
  waiting for transfers between devices  202 us (64%)
  Pallas kernels  67.6 us (22%)
  starting transfers between devices  29.1 us (9%)
  other arithmetic  4.37 us (1%)
  local copies, waits for them, and re-layouts  3.42 us (1%)
    all_to_all x1, waiting for transfers between devices, local(): lax.all_to_all(outgoing, 'region', split_axis=0, concat_axis=0, tiled=True)  89.9 us
    ppermute x1, waiting for transfers between devices, local(): lax.ppermute(head, 'region', [((i + 1) % count, i) for i in range(count)])  88.2 us
    pallas_call x1, Pallas kernels, trip_pass(): pl.pallas_call(functools.partial(trip_kernel, pair_count, trip_steps), gr...  34.1 us
    all_to_all x1, waiting for transfers between devices, local(): lax.all_to_all(slot_grad.reshape(regions, slot_count, rank_width, block_s...  19.9 us
    pallas_call x1, Pallas kernels, smooth_inner(): pl.pallas_call(smooth_inner_kernel, grid=(inner,), in_specs=[pl.BlockSpec...  17.9 us
    all_to_all x1, starting transfers between devices, local(): lax.all_to_all(outgoing, 'region', split_axis=0, concat_axis=0, tiled=True)  11.2 us
    all_to_all x1, starting transfers between devices, local(): lax.all_to_all(slot_grad.reshape(regions, slot_count, rank_width, block_s...  9.65 us
    pallas_call x1, Pallas kernels, owned_pass(): pl.pallas_call(owned_kernel, grid_spec=pltpu.PrefetchScalarGridSpec(num_s...  7.97 us
  transfers between devices with their start and end apart: 5, of which 4 were waited for; matrix products, arithmetic and copies ran while one was open for 2% of the time, Pallas kernels for 6%

profile of v10, /device:TPU:13, one launch (start us, length us, event | category | flops | bytes accessed | tf_op | source)
XLA Modules:
  0.0 309.4 jit_solution(12593156613449899770)
XLA Ops:
  0.6 0.0 copy-start
  0.6 0.8 copy.13
  1.5 0.1 squeeze.9
  1.6 0.6 compare_select_fusion
  2.2 5.5 %shard_map.113 = bf16[256,128,128]{2,1,0:T(8,128)(2,1)} custom-call(s32[256]{0:T(256)} %get-tuple-element.13.idx_ref, bf16[32,128,128]{2,1,0:T(8,128)(2,1)} %bitcast.23), custom_call_target="tpu_custom_call" | custom-call | tf_op jit(solution)/shard_map/pallas_call | solution.py:223
  7.6 11.2 %all-to-all-start = ((bf16[64,4,128,128]{3,2,1,0:T(8,128)(2,1)}), bf16[64,4,128,128]{3,2,1,0:T(8,128)(2,1)}, u32[]{:S(2)}, u32[]{:S(2)}) async-start(bf16[64,4,128,128]{3,2,1,0:T(8,128)(2,1)} %bitcast.20), calls=%async_computation | async-start | bytes 16777216 | tf_op jit(solution)/shard_map/all_to_all | solution.py:251
  18.8 0.0 copy-done.4
  18.8 0.0 copy-start.5
  18.8 0.1 copy.12
  18.9 0.7 reshape.38.pb_ref
  19.6 17.9 %shard_map.114._ = f32[3840,128]{1,0:T(8,128)} custom-call(bf16[4096,128]{1,0:T(8,128)(2,1)} %emb_ref.1, s32[4,4096]{1,0:T(4,128)} %bitcast.24, f32[4,4096]{1,0:T(4,128)} %bitcast.26), custom_call_target="tpu_custom_call" | custom-call | tf_op jit(solution)/shard_map/pallas_call | solution.py:142
  37.5 0.0 copy-done
  37.5 0.0 copy-done.5
  37.5 2.2 fusion.5.qt_ref
  39.7 89.9 %all-to-all-done = bf16[64,4,128,128]{3,2,1,0:T(8,128)(2,1)} async-done(((bf16[64,4,128,128]{3,2,1,0:T(8,128)(2,1)}), bf16[64,4,128,128]{3,2,1,0:T(8,128)(2,1)}, u32[]{:S(2)}, u32[]{:S(2)}) %all-to-all-start) | async-done | bytes 8388640 | tf_op jit(solution)/shard_map/all_to_all | solution.py:251
  129.6 34.1 %shard_map.115 = (f32[48,1,128]{2,1,0:T(1,128)}, bf16[256,128,128]{2,1,0:T(8,128)(2,1)}) custom-call(s32[672]{0:T(1024)} %reshape.38.pb_ref, bf16[48,14,128,128]{3,2,1,0:T(8,128)(2,1)} %len_ref.1, bf16[256,128,128]{2,1,0:T(8,128)(2,1)} %bitcast.2.inc_ref, f32[128,6144]{1,0:T(8,128)} %fusion.5.qt_ref, f32[48,1,128]{2,1,0:T(1,128)} %bitcast.28, ...), custom_call_target="tpu_custom_call" | custom-call | tf_op jit(solution)/shard_map/pallas_call | solution.py:67
  163.7 9.6 %all-to-all-start.1 = ((bf16[64,4,128,128]{3,2,1,0:T(8,128)(2,1)}), bf16[64,4,128,128]{3,2,1,0:T(8,128)(2,1)}, u32[]{:S(2)}, u32[]{:S(2)}) async-start(bf16[64,4,128,128]{3,2,1,0:T(8,128)(2,1)} %bitcast.21), calls=%async_computation.1 | async-start | bytes 16777216 | tf_op jit(solution)/shard_map/all_to_all | solution.py:283
  173.4 0.8 fusion.2
  174.2 2.4 collective-permute-start.1
  176.6 0.0 collective-permute-start
  176.6 0.9 fusion.3
  177.5 88.2 %collective-permute-done.1 = bf16[128,128]{1,0:T(8,128)(2,1)S(1)} collective-permute-done((bf16[128,128]{1,0:T(8,128)(2,1)S(1)}, bf16[128,128]{1,0:T(8,128)(2,1)S(1)}, u32[]{:S(2)}, u32[]{:S(2)}) %collective-permute-start.1) | collective-permute-done | bytes 32800 | tf_op jit(solution)/shard_map/ppermute | solution.py:263
  265.7 0.0 collective-permute-done
  265.7 0.7 pad_maximum_fusion.win_ref
  266.4 2.2 shard_map.116._
  268.6 19.9 %all-to-all-done.1 = bf16[64,4,128,128]{3,2,1,0:T(8,128)(2,1)} async-done(((bf16[64,4,128,128]{3,2,1,0:T(8,128)(2,1)}), bf16[64,4,128,128]{3,2,1,0:T(8,128)(2,1)}, u32[]{:S(2)}, u32[]{:S(2)}) %all-to-all-start.1) | async-done | bytes 8388640 | tf_op jit(solution)/shard_map/all_to_all | solution.py:283
  288.5 8.0 %shard_map.117 = f32[32,128,128]{2,1,0:T(8,128)} custom-call(s32[256]{0:T(256)} %get-tuple-element.12.tgt_ref, bf16[256,128,128]{2,1,0:T(8,128)(2,1)} %bitcast.9.ret_ref, f32[256,128]{1,0:T(8,128)} %shard_map.116._), custom_call_target="tpu_custom_call" | custom-call | tf_op jit(solution)/shard_map/pallas_call | solution.py:196
  296.4 5.9 %collective-permute-start.2 = (f32[4096,128]{1,0:T(8,128)}, f32[4096,128]{1,0:T(8,128)S(1)}, u32[]{:S(2)}, u32[]{:S(2)}) collective-permute-start(f32[4096,128]{1,0:T(8,128)} %bitcast.22), channel_id=1, source_target_pairs={{0,1},{1,0},{2,3},{3,2},{4,5},{5,4},{6,7},{7,6},{8,9},{9,8},{10,11... | collective-permute-start | bytes 6291464 | tf_op jit(solution)/shard_map/ppermute | solution.py:294
  302.3 0.0 copy-done.3
  302.3 4.0 %collective-permute-done.2 = f32[4096,128]{1,0:T(8,128)S(1)} collective-permute-done((f32[4096,128]{1,0:T(8,128)}, f32[4096,128]{1,0:T(8,128)S(1)}, u32[]{:S(2)}, u32[]{:S(2)}) %collective-permute-start.2) | collective-permute-done | bytes 2097184 | tf_op jit(solution)/shard_map/ppermute | solution.py:294
  306.3 0.0 copy-done.2
  306.3 3.1 fusion.1
  (8 shorter events, 0.0 us)
Async XLA Ops:
  0.6 36.8 %copy-start = (bf16[16,6144]{1,0:T(8,128)(2,1)S(1)}, bf16[16,6144]{1,0:T(8,128)(2,1)}, u32[]{:S(2)}) copy-start(bf16[16,6144]{1,0:T(8,128)(2,1)} %param.13) | copy-start | bytes 589828
  7.6 11.2 %copy-start.4 = (s32[48,14]{0,1:T(8,128)S(1)}, s32[48,14]{0,1:T(8,128)}, u32[]{:S(2)}) copy-start(s32[48,14]{0,1:T(8,128)} %param.12) | copy-start | bytes 8068
  7.6 122.0 %all-to-all-start = ((bf16[64,4,128,128]{3,2,1,0:T(8,128)(2,1)}), bf16[64,4,128,128]{3,2,1,0:T(8,128)(2,1)}, u32[]{:S(2)}, u32[]{:S(2)}) async-start(bf16[64,4,128,128]{3,2,1,0:T(8,128)(2,1)} %bitcast.20), calls=%async_computation | async-start | bytes 16777216 | tf_op jit(solution)/shard_map/all_to_all | solution.py:251
  18.8 18.7 %copy-start.5 = (bf16[16,128]{1,0:T(8,128)(2,1)S(1)}, bf16[16,128]{1,0:T(8,128)(2,1)}, u32[]{:S(2)}) copy-start(bf16[16,128]{1,0:T(8,128)(2,1)} %param.14) | copy-start | bytes 12292
  163.7 124.7 %all-to-all-start.1 = ((bf16[64,4,128,128]{3,2,1,0:T(8,128)(2,1)}), bf16[64,4,128,128]{3,2,1,0:T(8,128)(2,1)}, u32[]{:S(2)}, u32[]{:S(2)}) async-start(bf16[64,4,128,128]{3,2,1,0:T(8,128)(2,1)} %bitcast.21), calls=%async_computation.1 | async-start | bytes 16777216 | tf_op jit(solution)/shard_map/all_to_all | solution.py:283
  174.2 91.5 %collective-permute-start.1 = (bf16[128,128]{1,0:T(8,128)(2,1)S(1)}, bf16[128,128]{1,0:T(8,128)(2,1)S(1)}, u32[]{:S(2)}, u32[]{:S(2)}) collective-permute-start(bf16[128,128]{1,0:T(8,128)(2,1)S(1)} %get-tuple-element.7), channel_id=1, source_target_pairs={{2,0},{4,2},{6,4},{8,6},{10,8},{12,10},{14,12},{16,14},{18,16},{20... | collective-permute-start | bytes 98312 | tf_op jit(solution)/shard_map/ppermute | solution.py:263
  176.6 89.1 %collective-permute-start = (bf16[128,128]{1,0:T(8,128)(2,1)S(1)}, bf16[128,128]{1,0:T(8,128)(2,1)S(1)}, u32[]{:S(2)}, u32[]{:S(2)}) collective-permute-start(bf16[128,128]{1,0:T(8,128)(2,1)S(1)} %get-tuple-element.6), channel_id=1, source_target_pairs={{0,2},{2,4},{4,6},{6,8},{8,10},{10,12},{12,14},{14,16},{16,18},{18... | collective-permute-start | bytes 98312 | tf_op jit(solution)/shard_map/ppermute | solution.py:262
  288.5 13.8 %copy-start.3 = (f32[256,128]{1,0:T(8,128)S(1)}, f32[256,128]{1,0:T(8,128)}, u32[]{:S(2)}) copy-start(f32[256,128]{1,0:T(8,128)} %shard_map.116._) | copy-start | bytes 393220
  288.5 17.8 %copy-start.2 = (f32[3840,128]{1,0:T(8,128)S(1)}, f32[3840,128]{1,0:T(8,128)}, u32[]{:S(2)}) copy-start(f32[3840,128]{1,0:T(8,128)} %shard_map.114._) | copy-start | bytes 5898244
  296.4 9.9 %collective-permute-start.2 = (f32[4096,128]{1,0:T(8,128)}, f32[4096,128]{1,0:T(8,128)S(1)}, u32[]{:S(2)}, u32[]{:S(2)}) collective-permute-start(f32[4096,128]{1,0:T(8,128)} %bitcast.22), channel_id=1, source_target_pairs={{0,1},{1,0},{2,3},{3,2},{4,5},{5,4},{6,7},{7,6},{8,9},{9,8},{10,11... | collective-permute-start | bytes 6291464 | tf_op jit(solution)/shard_map/ppermute | solution.py:294
  306.3 3.1 copy-start.1

commit v11 on v10

--- a/solution.py
+++ b/solution.py
@@ -14,8 +14,8 @@
 
 
 def trip_kernel(
-    pair_count, trip_steps, pb_ref, len_ref, inc_ref, qt_ref, tgt_ref, w_ref, _, pred_ref, out_ref,
-    acc_ref,
+    pair_count, trip_steps, pb_ref, len_ref, inc_hbm, qt_ref, tgt_ref, w_ref, _, pred_ref, out_ref,
+    acc_ref, inc_ref, inc_sem,
 ):
     step = pl.program_id(0)
     per_step = len_ref.shape[0]
@@ -23,7 +23,10 @@
 
     @pl.when(step == 0)
     def _():
+        copy = pltpu.make_async_copy(inc_hbm, inc_ref, inc_sem)
+        copy.start()
         acc_ref[...] = jnp.zeros_like(acc_ref)
+        copy.wait()
 
     @pl.when(step < trip_steps)
     def _():
@@ -63,7 +66,6 @@
     trip_steps = trip_blocks // per_step
     chunk = slots // flush
     last = trip_steps - 1
-    const3 = lambda t, pb: (0, 0, 0)
     return pl.pallas_call(
         functools.partial(trip_kernel, pair_count, trip_steps),
         grid_spec=pltpu.PrefetchScalarGridSpec(
@@ -74,7 +76,7 @@
                     (per_step, pair_count, block, block),
                     lambda t, pb: (jnp.minimum(t, last), 0, 0, 0),
                 ),
-                pl.BlockSpec((slots, block, rank), const3, pipeline_mode=pl.Buffered(1)),
+                pl.BlockSpec(memory_space=pl.ANY),
                 pl.BlockSpec((rank, per_step * block), lambda t, pb: (0, jnp.minimum(t, last))),
                 pl.BlockSpec((per_step, 1, block), lambda t, pb: (jnp.minimum(t, last), 0, 0)),
                 pl.BlockSpec((per_step, 1, block), lambda t, pb: (jnp.minimum(t, last), 0, 0)),
@@ -86,7 +88,11 @@
                     (chunk, block, rank), lambda t, pb: (jnp.maximum(t - trip_steps, 0), 0, 0)
                 ),
             ],
-            scratch_shapes=[pltpu.VMEM((slots, block, rank), F32)],
+            scratch_shapes=[
+                pltpu.VMEM((slots, block, rank), F32),
+                pltpu.VMEM(incoming.shape, incoming.dtype),
+                pltpu.SemaphoreType.DMA(()),
+            ],
         ),
         out_shape=[
             jax.ShapeDtypeStruct((trip_blocks, 1, block), F32),

time: 314 us -> 314 us (level)
  no operation moved by 1% of the time
where the time goes in v11:
time: 314 us; the launch traced here: 310 us
  waiting for transfers between devices  202 us (64%)
  Pallas kernels  67.7 us (22%)
  starting transfers between devices  28.8 us (9%)
  other arithmetic  4.37 us (1%)
  local copies, waits for them, and re-layouts  3.42 us (1%)
    all_to_all x1, waiting for transfers between devices, local(): lax.all_to_all(outgoing, 'region', split_axis=0, concat_axis=0, tiled=True)  89.9 us
    ppermute x1, waiting for transfers between devices, local(): lax.ppermute(head, 'region', [((i + 1) % count, i) for i in range(count)])  88.1 us
    pallas_call x1, Pallas kernels, trip_pass(): pl.pallas_call(functools.partial(trip_kernel, pair_count, trip_steps), gr...  34.3 us
    all_to_all x1, waiting for transfers between devices, local(): lax.all_to_all(slot_grad.reshape(regions, slot_count, rank_width, block_s...  20.5 us
    pallas_call x1, Pallas kernels, smooth_inner(): pl.pallas_call(smooth_inner_kernel, grid=(inner,), in_specs=[pl.BlockSpec...  17.9 us
    all_to_all x1, starting transfers between devices, local(): lax.all_to_all(outgoing, 'region', split_axis=0, concat_axis=0, tiled=True)  11.2 us
    all_to_all x1, starting transfers between devices, local(): lax.all_to_all(slot_grad.reshape(regions, slot_count, rank_width, block_s...  9.65 us
    pallas_call x1, Pallas kernels, owned_pass(): pl.pallas_call(owned_kernel, grid_spec=pltpu.PrefetchScalarGridSpec(num_s...  7.92 us
  transfers between devices with their start and end apart: 5, of which 4 were waited for; matrix products, arithmetic and copies ran while one was open for 2% of the time, Pallas kernels for 6%

profile of v11, /device:TPU:13, one launch (start us, length us, event | category | flops | bytes accessed | tf_op | source)
XLA Modules:
  0.0 309.7 jit_solution(639555537326637983)
XLA Ops:
  0.6 0.0 copy-start
  0.6 0.8 copy.13
  1.5 0.1 squeeze.9
  1.6 0.6 compare_select_fusion
  2.2 5.5 %shard_map.113 = bf16[256,128,128]{2,1,0:T(8,128)(2,1)} custom-call(s32[256]{0:T(256)} %get-tuple-element.13.idx_ref, bf16[32,128,128]{2,1,0:T(8,128)(2,1)} %bitcast.23), custom_call_target="tpu_custom_call" | custom-call | tf_op jit(solution)/shard_map/pallas_call | solution.py:229
  7.6 11.2 %all-to-all-start = ((bf16[64,4,128,128]{3,2,1,0:T(8,128)(2,1)}), bf16[64,4,128,128]{3,2,1,0:T(8,128)(2,1)}, u32[]{:S(2)}, u32[]{:S(2)}) async-start(bf16[64,4,128,128]{3,2,1,0:T(8,128)(2,1)} %bitcast.20), calls=%async_computation | async-start | bytes 16777216 | tf_op jit(solution)/shard_map/all_to_all | solution.py:257
  18.8 0.0 copy-done.4
  18.8 0.0 copy-start.5
  18.8 0.1 copy.12
  18.9 0.7 reshape.38.pb_ref
  19.6 17.9 %shard_map.114._ = f32[3840,128]{1,0:T(8,128)} custom-call(bf16[4096,128]{1,0:T(8,128)(2,1)} %emb_ref.1, s32[4,4096]{1,0:T(4,128)} %bitcast.24, f32[4,4096]{1,0:T(4,128)} %bitcast.26), custom_call_target="tpu_custom_call" | custom-call | tf_op jit(solution)/shard_map/pallas_call | solution.py:148
  37.5 0.0 copy-done
  37.5 0.0 copy-done.5
  37.5 2.2 fusion.5.qt_ref
  39.7 89.9 %all-to-all-done = bf16[64,4,128,128]{3,2,1,0:T(8,128)(2,1)} async-done(((bf16[64,4,128,128]{3,2,1,0:T(8,128)(2,1)}), bf16[64,4,128,128]{3,2,1,0:T(8,128)(2,1)}, u32[]{:S(2)}, u32[]{:S(2)}) %all-to-all-start) | async-done | bytes 8388640 | tf_op jit(solution)/shard_map/all_to_all | solution.py:257
  129.6 34.3 %shard_map.115 = (f32[48,1,128]{2,1,0:T(1,128)}, bf16[256,128,128]{2,1,0:T(8,128)(2,1)}) custom-call(s32[672]{0:T(1024)} %reshape.38.pb_ref, bf16[48,14,128,128]{3,2,1,0:T(8,128)(2,1)} %len_ref.1, bf16[256,128,128]{2,1,0:T(8,128)(2,1)} %bitcast.2.inc_hbm, f32[128,6144]{1,0:T(8,128)} %fusion.5.qt_ref, f32[48,1,128]{2,1,0:T(1,128)} %bitcast.28, ...), custom_call_target="tpu_custom_call" | custom-call | tf_op jit(solution)/shard_map/pallas_call | solution.py:69
  163.9 9.7 %all-to-all-start.1 = ((bf16[64,4,128,128]{3,2,1,0:T(8,128)(2,1)}), bf16[64,4,128,128]{3,2,1,0:T(8,128)(2,1)}, u32[]{:S(2)}, u32[]{:S(2)}) async-start(bf16[64,4,128,128]{3,2,1,0:T(8,128)(2,1)} %bitcast.21), calls=%async_computation.1 | async-start | bytes 16777216 | tf_op jit(solution)/shard_map/all_to_all | solution.py:289
  173.6 0.8 fusion.2
  174.3 2.4 collective-permute-start.1
  176.7 0.0 collective-permute-start
  176.7 0.9 fusion.3
  177.6 88.1 %collective-permute-done.1 = bf16[128,128]{1,0:T(8,128)(2,1)S(1)} collective-permute-done((bf16[128,128]{1,0:T(8,128)(2,1)S(1)}, bf16[128,128]{1,0:T(8,128)(2,1)S(1)}, u32[]{:S(2)}, u32[]{:S(2)}) %collective-permute-start.1) | collective-permute-done | bytes 32800 | tf_op jit(solution)/shard_map/ppermute | solution.py:269
  265.7 0.0 collective-permute-done
  265.7 0.7 pad_maximum_fusion.win_ref
  266.4 2.2 shard_map.116._
  268.6 20.5 %all-to-all-done.1 = bf16[64,4,128,128]{3,2,1,0:T(8,128)(2,1)} async-done(((bf16[64,4,128,128]{3,2,1,0:T(8,128)(2,1)}), bf16[64,4,128,128]{3,2,1,0:T(8,128)(2,1)}, u32[]{:S(2)}, u32[]{:S(2)}) %all-to-all-start.1) | async-done | bytes 8388640 | tf_op jit(solution)/shard_map/all_to_all | solution.py:289
  289.1 7.9 %shard_map.117 = f32[32,128,128]{2,1,0:T(8,128)} custom-call(s32[256]{0:T(256)} %get-tuple-element.12.tgt_ref, bf16[256,128,128]{2,1,0:T(8,128)(2,1)} %bitcast.9.ret_ref, f32[256,128]{1,0:T(8,128)} %shard_map.116._), custom_call_target="tpu_custom_call" | custom-call | tf_op jit(solution)/shard_map/pallas_call | solution.py:202
  297.0 5.5 %collective-permute-start.2 = (f32[4096,128]{1,0:T(8,128)}, f32[4096,128]{1,0:T(8,128)S(1)}, u32[]{:S(2)}, u32[]{:S(2)}) collective-permute-start(f32[4096,128]{1,0:T(8,128)} %bitcast.22), channel_id=1, source_target_pairs={{0,1},{1,0},{2,3},{3,2},{4,5},{5,4},{6,7},{7,6},{8,9},{9,8},{10,11... | collective-permute-start | bytes 6291464 | tf_op jit(solution)/shard_map/ppermute | solution.py:300
  302.6 0.0 copy-done.3
  302.6 4.0 %collective-permute-done.2 = f32[4096,128]{1,0:T(8,128)S(1)} collective-permute-done((f32[4096,128]{1,0:T(8,128)}, f32[4096,128]{1,0:T(8,128)S(1)}, u32[]{:S(2)}, u32[]{:S(2)}) %collective-permute-start.2) | collective-permute-done | bytes 2097184 | tf_op jit(solution)/shard_map/ppermute | solution.py:300
  306.6 0.0 copy-done.2
  306.6 3.1 fusion.1
  (8 shorter events, 0.0 us)
Async XLA Ops:
  0.6 36.8 %copy-start = (bf16[16,6144]{1,0:T(8,128)(2,1)S(1)}, bf16[16,6144]{1,0:T(8,128)(2,1)}, u32[]{:S(2)}) copy-start(bf16[16,6144]{1,0:T(8,128)(2,1)} %param.13) | copy-start | bytes 589828
  7.6 11.2 %copy-start.4 = (s32[48,14]{0,1:T(8,128)S(1)}, s32[48,14]{0,1:T(8,128)}, u32[]{:S(2)}) copy-start(s32[48,14]{0,1:T(8,128)} %param.12) | copy-start | bytes 8068
  7.6 122.0 %all-to-all-start = ((bf16[64,4,128,128]{3,2,1,0:T(8,128)(2,1)}), bf16[64,4,128,128]{3,2,1,0:T(8,128)(2,1)}, u32[]{:S(2)}, u32[]{:S(2)}) async-start(bf16[64,4,128,128]{3,2,1,0:T(8,128)(2,1)} %bitcast.20), calls=%async_computation | async-start | bytes 16777216 | tf_op jit(solution)/shard_map/all_to_all | solution.py:257
  18.8 18.7 %copy-start.5 = (bf16[16,128]{1,0:T(8,128)(2,1)S(1)}, bf16[16,128]{1,0:T(8,128)(2,1)}, u32[]{:S(2)}) copy-start(bf16[16,128]{1,0:T(8,128)(2,1)} %param.14) | copy-start | bytes 12292
  163.9 125.2 %all-to-all-start.1 = ((bf16[64,4,128,128]{3,2,1,0:T(8,128)(2,1)}), bf16[64,4,128,128]{3,2,1,0:T(8,128)(2,1)}, u32[]{:S(2)}, u32[]{:S(2)}) async-start(bf16[64,4,128,128]{3,2,1,0:T(8,128)(2,1)} %bitcast.21), calls=%async_computation.1 | async-start | bytes 16777216 | tf_op jit(solution)/shard_map/all_to_all | solution.py:289
  174.3 91.4 %collective-permute-start.1 = (bf16[128,128]{1,0:T(8,128)(2,1)S(1)}, bf16[128,128]{1,0:T(8,128)(2,1)S(1)}, u32[]{:S(2)}, u32[]{:S(2)}) collective-permute-start(bf16[128,128]{1,0:T(8,128)(2,1)S(1)} %get-tuple-element.7), channel_id=1, source_target_pairs={{2,0},{4,2},{6,4},{8,6},{10,8},{12,10},{14,12},{16,14},{18,16},{20... | collective-permute-start | bytes 98312 | tf_op jit(solution)/shard_map/ppermute | solution.py:269
  176.7 89.0 %collective-permute-start = (bf16[128,128]{1,0:T(8,128)(2,1)S(1)}, bf16[128,128]{1,0:T(8,128)(2,1)S(1)}, u32[]{:S(2)}, u32[]{:S(2)}) collective-permute-start(bf16[128,128]{1,0:T(8,128)(2,1)S(1)} %get-tuple-element.6), channel_id=1, source_target_pairs={{0,2},{2,4},{4,6},{6,8},{8,10},{10,12},{12,14},{14,16},{16,18},{18... | collective-permute-start | bytes 98312 | tf_op jit(solution)/shard_map/ppermute | solution.py:268
  289.1 13.5 %copy-start.3 = (f32[256,128]{1,0:T(8,128)S(1)}, f32[256,128]{1,0:T(8,128)}, u32[]{:S(2)}) copy-start(f32[256,128]{1,0:T(8,128)} %shard_map.116._) | copy-start | bytes 393220
  289.1 17.5 %copy-start.2 = (f32[3840,128]{1,0:T(8,128)S(1)}, f32[3840,128]{1,0:T(8,128)}, u32[]{:S(2)}) copy-start(f32[3840,128]{1,0:T(8,128)} %shard_map.114._) | copy-start | bytes 5898244
  297.0 9.5 %collective-permute-start.2 = (f32[4096,128]{1,0:T(8,128)}, f32[4096,128]{1,0:T(8,128)S(1)}, u32[]{:S(2)}, u32[]{:S(2)}) collective-permute-start(f32[4096,128]{1,0:T(8,128)} %bitcast.22), channel_id=1, source_target_pairs={{0,1},{1,0},{2,3},{3,2},{4,5},{5,4},{6,7},{7,6},{8,9},{9,8},{10,11... | collective-permute-start | bytes 6291464 | tf_op jit(solution)/shard_map/ppermute | solution.py:300
  306.6 3.1 copy-start.1

commit v12 on v10

--- a/solution.py
+++ b/solution.py
@@ -256,18 +256,6 @@
     nb_t = nb_index[0]
     w_t = nb_weight[0]
     inner = smooth_inner(emb, nb_t, w_t, block_size)
-    count = regions
-    head = emb[:block_size]
-    tail = emb[seg_rows - block_size :]
-    prev_tail = lax.ppermute(tail, "region", [(i, (i + 1) % count) for i in range(count)])
-    next_head = lax.ppermute(head, "region", [((i + 1) % count, i) for i in range(count)])
-    windows = jnp.stack(
-        [
-            jnp.concatenate([prev_tail, emb[: 2 * block_size]], axis=0),
-            jnp.concatenate([emb[seg_rows - 2 * block_size :], next_head], axis=0),
-        ]
-    )
-    edge = smooth_edge(windows, nb_t, w_t, block_size)
 
     pred_rows, slot_grad = trip_pass(
         pair_block.reshape(-1),
@@ -288,9 +276,22 @@
         tiled=True,
     )
     returned = returned.reshape(regions * slot_count, rank_width, block_size)
+    count = regions
+    returned, head, tail = lax.optimization_barrier(
+        (returned, emb[:block_size], emb[seg_rows - block_size :])
+    )
+    prev_tail = lax.ppermute(tail, "region", [(i, (i + 1) % count) for i in range(count)])
+    next_head = lax.ppermute(head, "region", [((i + 1) % count, i) for i in range(count)])
+    windows = jnp.stack(
+        [
+            jnp.concatenate([prev_tail, emb[: 2 * block_size]], axis=0),
+            jnp.concatenate([emb[seg_rows - 2 * block_size :], next_head], axis=0),
+        ]
+    )
+    edge = smooth_edge(windows, nb_t, w_t, block_size)
 
     target_rows = jnp.where(live_mask, send_rows, -1).reshape(-1)
-    owned = owned_pass(target_rows, returned, edge, block_count).reshape(seg_rows, rank_width)
+    owned = owned_pass(target_rows, returned, inner, block_count).reshape(seg_rows, rank_width)
     partner = lax.ppermute(owned, "rep", [(0, 1), (1, 0)])
     smoothed = jnp.concatenate([edge[:block_size], inner, edge[block_size:]], axis=0)
     gradient = (owned + partner) + LAM * smoothed

time: 314 us -> 322 us (1.025)
  waiting for transfers between devices: 202 us -> 207 us
    all_to_all x1, waiting for transfers between devices: 19.9 us -> 115 us  [local(): lax.all_to_all(slot_grad.reshape(regions, slot_count, rank_width, block_s...]
    ppermute x1, waiting for transfers between devices: 88.2 us -> 2.69 us  [local(): lax.ppermute(head, 'region', [((i + 1) % count, i) for i in range(count)])]
    ppermute x1, starting transfers between devices: 0.01 us -> 4.12 us  [local(): lax.ppermute(tail, 'region', [(i, (i + 1) % count) for i in range(count)])]
    ppermute x1, waiting for transfers between devices: 3.98 us -> 0.01 us  [local(): partner = lax.ppermute(owned, 'rep', [(0, 1), (1, 0)])]
where the time goes in v12:
time: 322 us; the launch traced here: 318 us
  waiting for transfers between devices  207 us (64%)
  Pallas kernels  67.9 us (21%)
  starting transfers between devices  30.4 us (9%)
  other arithmetic  4.84 us (2%)
  local copies, waits for them, and re-layouts  4.29 us (1%)
    all_to_all x1, waiting for transfers between devices, local(): lax.all_to_all(slot_grad.reshape(regions, slot_count, rank_width, block_s...  115 us
    all_to_all x1, waiting for transfers between devices, local(): lax.all_to_all(outgoing, 'region', split_axis=0, concat_axis=0, tiled=True)  89.9 us
    pallas_call x1, Pallas kernels, trip_pass(): pl.pallas_call(functools.partial(trip_kernel, pair_count, trip_steps), gr...  34.1 us
    pallas_call x1, Pallas kernels, smooth_inner(): pl.pallas_call(smooth_inner_kernel, grid=(inner,), in_specs=[pl.BlockSpec...  17.9 us
    all_to_all x1, starting transfers between devices, local(): lax.all_to_all(outgoing, 'region', split_axis=0, concat_axis=0, tiled=True)  11.2 us
    all_to_all x1, starting transfers between devices, local(): lax.all_to_all(slot_grad.reshape(regions, slot_count, rank_width, block_s...  9.64 us
    pallas_call x1, Pallas kernels, owned_pass(): pl.pallas_call(owned_kernel, grid_spec=pltpu.PrefetchScalarGridSpec(num_s...  8.25 us
  transfers between devices with their start and end apart: 5, of which 4 were waited for; matrix products, arithmetic and copies ran while one was open for 2% of the time, Pallas kernels for 6%

profile of v12, /device:TPU:13, one launch (start us, length us, event | category | flops | bytes accessed | tf_op | source)
XLA Modules:
  0.0 317.9 jit_solution(3254081370469980099)
XLA Ops:
  0.6 0.0 copy-start
  0.6 0.8 copy.13
  1.5 0.1 squeeze.9
  1.6 0.6 compare_select_fusion
  2.2 5.4 %shard_map.113 = bf16[256,128,128]{2,1,0:T(8,128)(2,1)} custom-call(s32[256]{0:T(256)} %get-tuple-element.19.idx_ref, bf16[32,128,128]{2,1,0:T(8,128)(2,1)} %bitcast.23), custom_call_target="tpu_custom_call" | custom-call | tf_op jit(solution)/shard_map/pallas_call | solution.py:223
  7.6 11.2 %all-to-all-start = ((bf16[64,4,128,128]{3,2,1,0:T(8,128)(2,1)}), bf16[64,4,128,128]{3,2,1,0:T(8,128)(2,1)}, u32[]{:S(2)}, u32[]{:S(2)}) async-start(bf16[64,4,128,128]{3,2,1,0:T(8,128)(2,1)} %bitcast.20), calls=%async_computation | async-start | bytes 16777216 | tf_op jit(solution)/shard_map/all_to_all | solution.py:251
  18.8 0.0 copy-done.3
  18.8 0.0 copy-start.4
  18.8 0.1 copy.12
  18.9 0.7 reshape.38.pb_ref
  19.6 17.9 %shard_map.114._ = f32[3840,128]{1,0:T(8,128)} custom-call(bf16[4096,128]{1,0:T(8,128)(2,1)} %emb_ref.1, s32[4,4096]{1,0:T(4,128)} %bitcast.24, f32[4,4096]{1,0:T(4,128)} %bitcast.26), custom_call_target="tpu_custom_call" | custom-call | tf_op jit(solution)/shard_map/pallas_call | solution.py:142
  37.5 0.0 copy-done
  37.5 0.0 copy-done.4
  37.5 2.2 fusion.5.qt_ref
  39.8 89.9 %all-to-all-done = bf16[64,4,128,128]{3,2,1,0:T(8,128)(2,1)} async-done(((bf16[64,4,128,128]{3,2,1,0:T(8,128)(2,1)}), bf16[64,4,128,128]{3,2,1,0:T(8,128)(2,1)}, u32[]{:S(2)}, u32[]{:S(2)}) %all-to-all-start) | async-done | bytes 8388640 | tf_op jit(solution)/shard_map/all_to_all | solution.py:251
  129.6 34.1 %shard_map.115 = (f32[48,1,128]{2,1,0:T(1,128)}, bf16[256,128,128]{2,1,0:T(8,128)(2,1)}) custom-call(s32[672]{0:T(1024)} %reshape.38.pb_ref, bf16[48,14,128,128]{3,2,1,0:T(8,128)(2,1)} %len_ref.1, bf16[256,128,128]{2,1,0:T(8,128)(2,1)} %bitcast.2.inc_ref, f32[128,6144]{1,0:T(8,128)} %fusion.5.qt_ref, f32[48,1,128]{2,1,0:T(1,128)} %bitcast.28, ...), custom_call_target="tpu_custom_call" | custom-call | tf_op jit(solution)/shard_map/pallas_call | solution.py:67
  163.7 9.6 %all-to-all-start.1 = ((bf16[64,4,128,128]{3,2,1,0:T(8,128)(2,1)}), bf16[64,4,128,128]{3,2,1,0:T(8,128)(2,1)}, u32[]{:S(2)}, u32[]{:S(2)}) async-start(bf16[64,4,128,128]{3,2,1,0:T(8,128)(2,1)} %bitcast.22), calls=%async_computation.1 | async-start | bytes 16777216 | tf_op jit(solution)/shard_map/all_to_all | solution.py:271
  173.4 0.8 fusion.3
  174.2 114.9 %all-to-all-done.1 = bf16[64,4,128,128]{3,2,1,0:T(8,128)(2,1)} async-done(((bf16[64,4,128,128]{3,2,1,0:T(8,128)(2,1)}), bf16[64,4,128,128]{3,2,1,0:T(8,128)(2,1)}, u32[]{:S(2)}, u32[]{:S(2)}) %all-to-all-start.1) | async-done | bytes 8388640 | tf_op jit(solution)/shard_map/all_to_all | solution.py:271
  289.0 8.2 %shard_map.116 = f32[32,128,128]{2,1,0:T(8,128)} custom-call(s32[256]{0:T(256)} %get-tuple-element.18.tgt_ref, bf16[256,128,128]{2,1,0:T(8,128)(2,1)} %bitcast.9.ret_ref, f32[3840,128]{1,0:T(8,128)} %shard_map.114._), custom_call_target="tpu_custom_call" | custom-call | tf_op jit(solution)/shard_map/pallas_call | solution.py:196
  297.3 5.4 %collective-permute-start = (f32[4096,128]{1,0:T(8,128)}, f32[4096,128]{1,0:T(8,128)}, u32[]{:S(2)}, u32[]{:S(2)}) collective-permute-start(f32[4096,128]{1,0:T(8,128)} %bitcast.21), channel_id=1, source_target_pairs={{0,1},{1,0},{2,3},{3,2},{4,5},{5,4},{6,7},{7,6},{8,9},{9,8},{10,11... | collective-permute-start | bytes 6291464 | tf_op jit(solution)/shard_map/ppermute | solution.py:295
  302.7 4.1 %collective-permute-start.1 = (bf16[128,128]{1,0:T(8,128)(2,1)S(1)}, bf16[128,128]{1,0:T(8,128)(2,1)S(1)}, u32[]{:S(2)}, u32[]{:S(2)}) collective-permute-start(bf16[128,128]{1,0:T(8,128)(2,1)S(1)} %get-tuple-element.10), channel_id=1, source_target_pairs={{0,2},{2,4},{4,6},{6,8},{8,10},{10,12},{12,14},{14,16},{16,18},{18... | collective-permute-start | bytes 98312 | tf_op jit(solution)/shard_map/ppermute | solution.py:283
  306.8 0.9 fusion.2
  307.7 0.1 collective-permute-start.2
  307.7 0.1 collective-permute-done.1
  307.8 2.7 collective-permute-done.2
  310.5 0.7 pad_maximum_fusion.win_ref
  311.2 2.2 shard_map.117
  313.4 0.9 fusion.4
  314.3 0.0 collective-permute-done
  314.3 0.0 copy-start.1
  314.3 3.5 %fusion.1 = bf16[4096,128]{1,0:T(8,128)(2,1)} fusion(f32[128,128]{1,0:T(8,128)S(1)} %get-tuple-element.17, f32[3840,128]{1,0:T(8,128)S(1)} %copy-done.2, f32[128,128]{1,0:T(8,128)S(1)} %get-tuple-element.16, f32[4096,128]{1,0:T(8,128)} %collective-permute-done, f32[32,128,128]{2,1,0:T(8,128)} %shard_map.116), kind=kLoop, calls=%fused_computation.2 | loop fusion | flops 3145728 | bytes 7340032 | tf_op jit(solution)/shard_map/convert_element_type | solution.py:298
  (6 shorter events, 0.0 us)
Async XLA Ops:
  0.6 36.9 %copy-start = (bf16[16,6144]{1,0:T(8,128)(2,1)S(1)}, bf16[16,6144]{1,0:T(8,128)(2,1)}, u32[]{:S(2)}) copy-start(bf16[16,6144]{1,0:T(8,128)(2,1)} %param.13) | copy-start | bytes 589828
  7.6 11.2 %copy-start.3 = (s32[48,14]{0,1:T(8,128)S(1)}, s32[48,14]{0,1:T(8,128)}, u32[]{:S(2)}) copy-start(s32[48,14]{0,1:T(8,128)} %param.12) | copy-start | bytes 8068
  7.6 122.0 %all-to-all-start = ((bf16[64,4,128,128]{3,2,1,0:T(8,128)(2,1)}), bf16[64,4,128,128]{3,2,1,0:T(8,128)(2,1)}, u32[]{:S(2)}, u32[]{:S(2)}) async-start(bf16[64,4,128,128]{3,2,1,0:T(8,128)(2,1)} %bitcast.20), calls=%async_computation | async-start | bytes 16777216 | tf_op jit(solution)/shard_map/all_to_all | solution.py:251
  18.8 18.8 %copy-start.4 = (bf16[16,128]{1,0:T(8,128)(2,1)S(1)}, bf16[16,128]{1,0:T(8,128)(2,1)}, u32[]{:S(2)}) copy-start(bf16[16,128]{1,0:T(8,128)(2,1)} %param.14) | copy-start | bytes 12292
  163.7 125.3 %all-to-all-start.1 = ((bf16[64,4,128,128]{3,2,1,0:T(8,128)(2,1)}), bf16[64,4,128,128]{3,2,1,0:T(8,128)(2,1)}, u32[]{:S(2)}, u32[]{:S(2)}) async-start(bf16[64,4,128,128]{3,2,1,0:T(8,128)(2,1)} %bitcast.22), calls=%async_computation.1 | async-start | bytes 16777216 | tf_op jit(solution)/shard_map/all_to_all | solution.py:271
  289.0 25.3 %copy-start.2 = (f32[3840,128]{1,0:T(8,128)S(1)}, f32[3840,128]{1,0:T(8,128)}, u32[]{:S(2)}) copy-start(f32[3840,128]{1,0:T(8,128)} %shard_map.114._) | copy-start | bytes 5898244
  297.3 17.0 %collective-permute-start = (f32[4096,128]{1,0:T(8,128)}, f32[4096,128]{1,0:T(8,128)}, u32[]{:S(2)}, u32[]{:S(2)}) collective-permute-start(f32[4096,128]{1,0:T(8,128)} %bitcast.21), channel_id=1, source_target_pairs={{0,1},{1,0},{2,3},{3,2},{4,5},{5,4},{6,7},{7,6},{8,9},{9,8},{10,11... | collective-permute-start | bytes 6291464 | tf_op jit(solution)/shard_map/ppermute | solution.py:295
  302.7 5.1 %collective-permute-start.1 = (bf16[128,128]{1,0:T(8,128)(2,1)S(1)}, bf16[128,128]{1,0:T(8,128)(2,1)S(1)}, u32[]{:S(2)}, u32[]{:S(2)}) collective-permute-start(bf16[128,128]{1,0:T(8,128)(2,1)S(1)} %get-tuple-element.10), channel_id=1, source_target_pairs={{0,2},{2,4},{4,6},{6,8},{8,10},{10,12},{12,14},{14,16},{16,18},{18... | collective-permute-start | bytes 98312 | tf_op jit(solution)/shard_map/ppermute | solution.py:283
  307.7 2.8 collective-permute-start.2
  314.3 3.6 %copy-start.1 = (bf16[16,6144]{1,0:T(8,128)(2,1)S(1)}, bf16[16,6144]{1,0:T(8,128)(2,1)}, u32[]{:S(2)}) copy-start(bf16[16,6144]{1,0:T(8,128)(2,1)} %param.13) | copy-start | bytes 589828

commit v13 on v10

--- a/solution.py
+++ b/solution.py
@@ -57,7 +57,7 @@
         out_ref[...] = acc_ref[pl.ds(first, chunk)].astype(out_ref.dtype)
 
 
-def trip_pass(pair_flat, lengths, incoming, query_t, tgt, wts, after, per_step=8, flush=4):
+def trip_pass(pair_flat, lengths, incoming, query_t, tgt, wts, after, per_step=12, flush=4):
     trip_blocks, pair_count, block, rank = lengths.shape
     slots = incoming.shape[0]
     trip_steps = trip_blocks // per_step

time: 314 us -> 314 us (level)
  no operation moved by 1% of the time
where the time goes in v13:
time: 314 us; the launch traced here: 310 us
  waiting for transfers between devices  203 us (65%)
  Pallas kernels  67.7 us (22%)
  starting transfers between devices  28.7 us (9%)
  other arithmetic  4.37 us (1%)
  local copies, waits for them, and re-layouts  3.42 us (1%)
    all_to_all x1, waiting for transfers between devices, local(): lax.all_to_all(outgoing, 'region', split_axis=0, concat_axis=0, tiled=True)  89.9 us
    ppermute x1, waiting for transfers between devices, local(): lax.ppermute(head, 'region', [((i + 1) % count, i) for i in range(count)])  88.3 us
    pallas_call x1, Pallas kernels, trip_pass(): pl.pallas_call(functools.partial(trip_kernel, pair_count, trip_steps), gr...  34.3 us
    all_to_all x1, waiting for transfers between devices, local(): lax.all_to_all(slot_grad.reshape(regions, slot_count, rank_width, block_s...  20.6 us
    pallas_call x1, Pallas kernels, smooth_inner(): pl.pallas_call(smooth_inner_kernel, grid=(inner,), in_specs=[pl.BlockSpec...  17.9 us
    all_to_all x1, starting transfers between devices, local(): lax.all_to_all(outgoing, 'region', split_axis=0, concat_axis=0, tiled=True)  11.2 us
    all_to_all x1, starting transfers between devices, local(): lax.all_to_all(slot_grad.reshape(regions, slot_count, rank_width, block_s...  9.66 us
    pallas_call x1, Pallas kernels, owned_pass(): pl.pallas_call(owned_kernel, grid_spec=pltpu.PrefetchScalarGridSpec(num_s...  7.93 us
  transfers between devices with their start and end apart: 5, of which 4 were waited for; matrix products, arithmetic and copies ran while one was open for 2% of the time, Pallas kernels for 6%

profile of v13, /device:TPU:13, one launch (start us, length us, event | category | flops | bytes accessed | tf_op | source)
XLA Modules:
  0.0 309.9 jit_solution(11660936544239603893)
XLA Ops:
  0.6 0.0 copy-start
  0.6 0.8 copy.13
  1.5 0.1 squeeze.9
  1.6 0.6 compare_select_fusion
  2.2 5.5 %shard_map.113 = bf16[256,128,128]{2,1,0:T(8,128)(2,1)} custom-call(s32[256]{0:T(256)} %get-tuple-element.13.idx_ref, bf16[32,128,128]{2,1,0:T(8,128)(2,1)} %bitcast.23), custom_call_target="tpu_custom_call" | custom-call | tf_op jit(solution)/shard_map/pallas_call | solution.py:223
  7.6 11.2 %all-to-all-start = ((bf16[64,4,128,128]{3,2,1,0:T(8,128)(2,1)}), bf16[64,4,128,128]{3,2,1,0:T(8,128)(2,1)}, u32[]{:S(2)}, u32[]{:S(2)}) async-start(bf16[64,4,128,128]{3,2,1,0:T(8,128)(2,1)} %bitcast.20), calls=%async_computation | async-start | bytes 16777216 | tf_op jit(solution)/shard_map/all_to_all | solution.py:251
  18.8 0.0 copy-done.4
  18.8 0.0 copy-start.5
  18.8 0.1 copy.12
  18.9 0.7 reshape.38.pb_ref
  19.6 17.9 %shard_map.114._ = f32[3840,128]{1,0:T(8,128)} custom-call(bf16[4096,128]{1,0:T(8,128)(2,1)} %emb_ref.1, s32[4,4096]{1,0:T(4,128)} %bitcast.24, f32[4,4096]{1,0:T(4,128)} %bitcast.26), custom_call_target="tpu_custom_call" | custom-call | tf_op jit(solution)/shard_map/pallas_call | solution.py:142
  37.5 0.0 copy-done
  37.5 0.0 copy-done.5
  37.5 2.2 fusion.5.qt_ref
  39.7 89.9 %all-to-all-done = bf16[64,4,128,128]{3,2,1,0:T(8,128)(2,1)} async-done(((bf16[64,4,128,128]{3,2,1,0:T(8,128)(2,1)}), bf16[64,4,128,128]{3,2,1,0:T(8,128)(2,1)}, u32[]{:S(2)}, u32[]{:S(2)}) %all-to-all-start) | async-done | bytes 8388640 | tf_op jit(solution)/shard_map/all_to_all | solution.py:251
  129.6 34.3 %shard_map.115 = (f32[48,1,128]{2,1,0:T(1,128)}, bf16[256,128,128]{2,1,0:T(8,128)(2,1)}) custom-call(s32[672]{0:T(1024)} %reshape.38.pb_ref, bf16[48,14,128,128]{3,2,1,0:T(8,128)(2,1)} %len_ref.1, bf16[256,128,128]{2,1,0:T(8,128)(2,1)} %bitcast.2.inc_ref, f32[128,6144]{1,0:T(8,128)} %fusion.5.qt_ref, f32[48,1,128]{2,1,0:T(1,128)} %bitcast.28, ...), custom_call_target="tpu_custom_call" | custom-call | tf_op jit(solution)/shard_map/pallas_call | solution.py:67
  163.9 9.7 %all-to-all-start.1 = ((bf16[64,4,128,128]{3,2,1,0:T(8,128)(2,1)}), bf16[64,4,128,128]{3,2,1,0:T(8,128)(2,1)}, u32[]{:S(2)}, u32[]{:S(2)}) async-start(bf16[64,4,128,128]{3,2,1,0:T(8,128)(2,1)} %bitcast.21), calls=%async_computation.1 | async-start | bytes 16777216 | tf_op jit(solution)/shard_map/all_to_all | solution.py:283
  173.6 0.8 fusion.2
  174.4 2.4 collective-permute-start.1
  176.7 0.0 collective-permute-start
  176.8 0.9 fusion.3
  177.6 88.3 %collective-permute-done.1 = bf16[128,128]{1,0:T(8,128)(2,1)S(1)} collective-permute-done((bf16[128,128]{1,0:T(8,128)(2,1)S(1)}, bf16[128,128]{1,0:T(8,128)(2,1)S(1)}, u32[]{:S(2)}, u32[]{:S(2)}) %collective-permute-start.1) | collective-permute-done | bytes 32800 | tf_op jit(solution)/shard_map/ppermute | solution.py:263
  265.9 0.0 collective-permute-done
  266.0 0.7 pad_maximum_fusion.win_ref
  266.6 2.2 shard_map.116._
  268.8 20.6 %all-to-all-done.1 = bf16[64,4,128,128]{3,2,1,0:T(8,128)(2,1)} async-done(((bf16[64,4,128,128]{3,2,1,0:T(8,128)(2,1)}), bf16[64,4,128,128]{3,2,1,0:T(8,128)(2,1)}, u32[]{:S(2)}, u32[]{:S(2)}) %all-to-all-start.1) | async-done | bytes 8388640 | tf_op jit(solution)/shard_map/all_to_all | solution.py:283
  289.4 7.9 %shard_map.117 = f32[32,128,128]{2,1,0:T(8,128)} custom-call(s32[256]{0:T(256)} %get-tuple-element.12.tgt_ref, bf16[256,128,128]{2,1,0:T(8,128)(2,1)} %bitcast.9.ret_ref, f32[256,128]{1,0:T(8,128)} %shard_map.116._), custom_call_target="tpu_custom_call" | custom-call | tf_op jit(solution)/shard_map/pallas_call | solution.py:196
  297.3 5.5 %collective-permute-start.2 = (f32[4096,128]{1,0:T(8,128)}, f32[4096,128]{1,0:T(8,128)S(1)}, u32[]{:S(2)}, u32[]{:S(2)}) collective-permute-start(f32[4096,128]{1,0:T(8,128)} %bitcast.22), channel_id=1, source_target_pairs={{0,1},{1,0},{2,3},{3,2},{4,5},{5,4},{6,7},{7,6},{8,9},{9,8},{10,11... | collective-permute-start | bytes 6291464 | tf_op jit(solution)/shard_map/ppermute | solution.py:294
  302.8 0.0 copy-done.3
  302.8 4.0 %collective-permute-done.2 = f32[4096,128]{1,0:T(8,128)S(1)} collective-permute-done((f32[4096,128]{1,0:T(8,128)}, f32[4096,128]{1,0:T(8,128)S(1)}, u32[]{:S(2)}, u32[]{:S(2)}) %collective-permute-start.2) | collective-permute-done | bytes 2097184 | tf_op jit(solution)/shard_map/ppermute | solution.py:294
  306.8 0.0 copy-done.2
  306.8 3.1 fusion.1
  (8 shorter events, 0.0 us)
Async XLA Ops:
  0.6 36.8 %copy-start = (bf16[16,6144]{1,0:T(8,128)(2,1)S(1)}, bf16[16,6144]{1,0:T(8,128)(2,1)}, u32[]{:S(2)}) copy-start(bf16[16,6144]{1,0:T(8,128)(2,1)} %param.13) | copy-start | bytes 589828
  7.6 11.2 %copy-start.4 = (s32[48,14]{0,1:T(8,128)S(1)}, s32[48,14]{0,1:T(8,128)}, u32[]{:S(2)}) copy-start(s32[48,14]{0,1:T(8,128)} %param.12) | copy-start | bytes 8068
  7.6 122.0 %all-to-all-start = ((bf16[64,4,128,128]{3,2,1,0:T(8,128)(2,1)}), bf16[64,4,128,128]{3,2,1,0:T(8,128)(2,1)}, u32[]{:S(2)}, u32[]{:S(2)}) async-start(bf16[64,4,128,128]{3,2,1,0:T(8,128)(2,1)} %bitcast.20), calls=%async_computation | async-start | bytes 16777216 | tf_op jit(solution)/shard_map/all_to_all | solution.py:251
  18.8 18.7 %copy-start.5 = (bf16[16,128]{1,0:T(8,128)(2,1)S(1)}, bf16[16,128]{1,0:T(8,128)(2,1)}, u32[]{:S(2)}) copy-start(bf16[16,128]{1,0:T(8,128)(2,1)} %param.14) | copy-start | bytes 12292
  163.9 125.5 %all-to-all-start.1 = ((bf16[64,4,128,128]{3,2,1,0:T(8,128)(2,1)}), bf16[64,4,128,128]{3,2,1,0:T(8,128)(2,1)}, u32[]{:S(2)}, u32[]{:S(2)}) async-start(bf16[64,4,128,128]{3,2,1,0:T(8,128)(2,1)} %bitcast.21), calls=%async_computation.1 | async-start | bytes 16777216 | tf_op jit(solution)/shard_map/all_to_all | solution.py:283
  174.4 91.6 %collective-permute-start.1 = (bf16[128,128]{1,0:T(8,128)(2,1)S(1)}, bf16[128,128]{1,0:T(8,128)(2,1)S(1)}, u32[]{:S(2)}, u32[]{:S(2)}) collective-permute-start(bf16[128,128]{1,0:T(8,128)(2,1)S(1)} %get-tuple-element.7), channel_id=1, source_target_pairs={{2,0},{4,2},{6,4},{8,6},{10,8},{12,10},{14,12},{16,14},{18,16},{20... | collective-permute-start | bytes 98312 | tf_op jit(solution)/shard_map/ppermute | solution.py:263
  176.7 89.2 %collective-permute-start = (bf16[128,128]{1,0:T(8,128)(2,1)S(1)}, bf16[128,128]{1,0:T(8,128)(2,1)S(1)}, u32[]{:S(2)}, u32[]{:S(2)}) collective-permute-start(bf16[128,128]{1,0:T(8,128)(2,1)S(1)} %get-tuple-element.6), channel_id=1, source_target_pairs={{0,2},{2,4},{4,6},{6,8},{8,10},{10,12},{12,14},{14,16},{16,18},{18... | collective-permute-start | bytes 98312 | tf_op jit(solution)/shard_map/ppermute | solution.py:262
  289.4 13.4 %copy-start.3 = (f32[256,128]{1,0:T(8,128)S(1)}, f32[256,128]{1,0:T(8,128)}, u32[]{:S(2)}) copy-start(f32[256,128]{1,0:T(8,128)} %shard_map.116._) | copy-start | bytes 393220
  289.4 17.4 %copy-start.2 = (f32[3840,128]{1,0:T(8,128)S(1)}, f32[3840,128]{1,0:T(8,128)}, u32[]{:S(2)}) copy-start(f32[3840,128]{1,0:T(8,128)} %shard_map.114._) | copy-start | bytes 5898244
  297.3 9.5 %collective-permute-start.2 = (f32[4096,128]{1,0:T(8,128)}, f32[4096,128]{1,0:T(8,128)S(1)}, u32[]{:S(2)}, u32[]{:S(2)}) collective-permute-start(f32[4096,128]{1,0:T(8,128)} %bitcast.22), channel_id=1, source_target_pairs={{0,1},{1,0},{2,3},{3,2},{4,5},{5,4},{6,7},{7,6},{8,9},{9,8},{10,11... | collective-permute-start | bytes 6291464 | tf_op jit(solution)/shard_map/ppermute | solution.py:294
  306.8 3.1 copy-start.1

commit v14 on v13

--- a/solution.py
+++ b/solution.py
@@ -42,13 +42,9 @@
             pred_ref[u] = pred_row
             err_row = w_ref[u] * (pred_row - tgt_ref[u])
             scaled_t = (err_row * q_t).astype(BF16)
-            for k in range(0, pair_count, 2):
-                p0 = pb_ref[t * pair_count + k]
-                p1 = pb_ref[t * pair_count + k + 1]
-                rhs = jnp.concatenate([len_ref[u, k], len_ref[u, k + 1]], axis=1)
-                both = jnp.dot(scaled_t, rhs, preferred_element_type=F32)
-                acc_ref[p0] += both[:, :block]
-                acc_ref[p1] += both[:, block:]
+            for k in range(pair_count):
+                p = pb_ref[t * pair_count + k]
+                acc_ref[p] += jnp.dot(scaled_t, len_ref[u, k], preferred_element_type=F32)
 
     @pl.when(step >= trip_steps)
     def _():

time: 314 us -> 314 us (level)
  no operation moved by 1% of the time
where the time goes in v14:
time: 314 us; the launch traced here: 310 us
  waiting for transfers between devices  202 us (64%)
  Pallas kernels  68.3 us (22%)
  starting transfers between devices  29 us (9%)
  other arithmetic  4.37 us (1%)
  local copies, waits for them, and re-layouts  3.42 us (1%)
    all_to_all x1, waiting for transfers between devices, local(): lax.all_to_all(outgoing, 'region', split_axis=0, concat_axis=0, tiled=True)  89.9 us
    ppermute x1, waiting for transfers between devices, local(): lax.ppermute(head, 'region', [((i + 1) % count, i) for i in range(count)])  88.2 us
    pallas_call x1, Pallas kernels, trip_pass(): pl.pallas_call(functools.partial(trip_kernel, pair_count, trip_steps), gr...  34.6 us
    all_to_all x1, waiting for transfers between devices, local(): lax.all_to_all(slot_grad.reshape(regions, slot_count, rank_width, block_s...  19.9 us
    pallas_call x1, Pallas kernels, smooth_inner(): pl.pallas_call(smooth_inner_kernel, grid=(inner,), in_specs=[pl.BlockSpec...  17.9 us
    all_to_all x1, starting transfers between devices, local(): lax.all_to_all(outgoing, 'region', split_axis=0, concat_axis=0, tiled=True)  11.2 us
    all_to_all x1, starting transfers between devices, local(): lax.all_to_all(slot_grad.reshape(regions, slot_count, rank_width, block_s...  9.64 us
    pallas_call x1, Pallas kernels, owned_pass(): pl.pallas_call(owned_kernel, grid_spec=pltpu.PrefetchScalarGridSpec(num_s...  8.26 us
  transfers between devices with their start and end apart: 5, of which 4 were waited for; matrix products, arithmetic and copies ran while one was open for 2% of the time, Pallas kernels for 6%

profile of v14, /device:TPU:13, one launch (start us, length us, event | category | flops | bytes accessed | tf_op | source)
XLA Modules:
  0.0 310.1 jit_solution(14315387178534693493)
XLA Ops:
  0.6 0.0 copy-start
  0.6 0.8 copy.13
  1.5 0.1 squeeze.9
  1.6 0.6 compare_select_fusion
  2.2 5.5 %shard_map.113 = bf16[256,128,128]{2,1,0:T(8,128)(2,1)} custom-call(s32[256]{0:T(256)} %get-tuple-element.13.idx_ref, bf16[32,128,128]{2,1,0:T(8,128)(2,1)} %bitcast.23), custom_call_target="tpu_custom_call" | custom-call | tf_op jit(solution)/shard_map/pallas_call | solution.py:219
  7.6 11.2 %all-to-all-start = ((bf16[64,4,128,128]{3,2,1,0:T(8,128)(2,1)}), bf16[64,4,128,128]{3,2,1,0:T(8,128)(2,1)}, u32[]{:S(2)}, u32[]{:S(2)}) async-start(bf16[64,4,128,128]{3,2,1,0:T(8,128)(2,1)} %bitcast.20), calls=%async_computation | async-start | bytes 16777216 | tf_op jit(solution)/shard_map/all_to_all | solution.py:247
  18.8 0.0 copy-done.4
  18.8 0.0 copy-start.5
  18.8 0.1 copy.12
  18.9 0.7 reshape.38.pb_ref
  19.6 17.9 %shard_map.114._ = f32[3840,128]{1,0:T(8,128)} custom-call(bf16[4096,128]{1,0:T(8,128)(2,1)} %emb_ref.1, s32[4,4096]{1,0:T(4,128)} %bitcast.24, f32[4,4096]{1,0:T(4,128)} %bitcast.26), custom_call_target="tpu_custom_call" | custom-call | tf_op jit(solution)/shard_map/pallas_call | solution.py:138
  37.5 0.0 copy-done
  37.5 0.0 copy-done.5
  37.5 2.2 fusion.5.qt_ref
  39.7 89.9 %all-to-all-done = bf16[64,4,128,128]{3,2,1,0:T(8,128)(2,1)} async-done(((bf16[64,4,128,128]{3,2,1,0:T(8,128)(2,1)}), bf16[64,4,128,128]{3,2,1,0:T(8,128)(2,1)}, u32[]{:S(2)}, u32[]{:S(2)}) %all-to-all-start) | async-done | bytes 8388640 | tf_op jit(solution)/shard_map/all_to_all | solution.py:247
  129.6 34.6 %shard_map.115 = (f32[48,1,128]{2,1,0:T(1,128)}, bf16[256,128,128]{2,1,0:T(8,128)(2,1)}) custom-call(s32[672]{0:T(1024)} %reshape.38.pb_ref, bf16[48,14,128,128]{3,2,1,0:T(8,128)(2,1)} %len_ref.1, bf16[256,128,128]{2,1,0:T(8,128)(2,1)} %bitcast.2.inc_ref, f32[128,6144]{1,0:T(8,128)} %fusion.5.qt_ref, f32[48,1,128]{2,1,0:T(1,128)} %bitcast.28, ...), custom_call_target="tpu_custom_call" | custom-call | tf_op jit(solution)/shard_map/pallas_call | solution.py:63
  164.2 9.6 %all-to-all-start.1 = ((bf16[64,4,128,128]{3,2,1,0:T(8,128)(2,1)}), bf16[64,4,128,128]{3,2,1,0:T(8,128)(2,1)}, u32[]{:S(2)}, u32[]{:S(2)}) async-start(bf16[64,4,128,128]{3,2,1,0:T(8,128)(2,1)} %bitcast.21), calls=%async_computation.1 | async-start | bytes 16777216 | tf_op jit(solution)/shard_map/all_to_all | solution.py:279
  173.9 0.8 fusion.2
  174.7 2.4 collective-permute-start.1
  177.0 0.0 collective-permute-start
  177.1 0.9 fusion.3
  177.9 88.2 %collective-permute-done.1 = bf16[128,128]{1,0:T(8,128)(2,1)S(1)} collective-permute-done((bf16[128,128]{1,0:T(8,128)(2,1)S(1)}, bf16[128,128]{1,0:T(8,128)(2,1)S(1)}, u32[]{:S(2)}, u32[]{:S(2)}) %collective-permute-start.1) | collective-permute-done | bytes 32800 | tf_op jit(solution)/shard_map/ppermute | solution.py:259
  266.1 0.0 collective-permute-done
  266.2 0.7 pad_maximum_fusion.win_ref
  266.9 2.2 shard_map.116._
  269.0 19.9 %all-to-all-done.1 = bf16[64,4,128,128]{3,2,1,0:T(8,128)(2,1)} async-done(((bf16[64,4,128,128]{3,2,1,0:T(8,128)(2,1)}), bf16[64,4,128,128]{3,2,1,0:T(8,128)(2,1)}, u32[]{:S(2)}, u32[]{:S(2)}) %all-to-all-start.1) | async-done | bytes 8388640 | tf_op jit(solution)/shard_map/all_to_all | solution.py:279
  289.0 8.3 %shard_map.117 = f32[32,128,128]{2,1,0:T(8,128)} custom-call(s32[256]{0:T(256)} %get-tuple-element.12.tgt_ref, bf16[256,128,128]{2,1,0:T(8,128)(2,1)} %bitcast.9.ret_ref, f32[256,128]{1,0:T(8,128)} %shard_map.116._), custom_call_target="tpu_custom_call" | custom-call | tf_op jit(solution)/shard_map/pallas_call | solution.py:192
  297.2 5.8 %collective-permute-start.2 = (f32[4096,128]{1,0:T(8,128)}, f32[4096,128]{1,0:T(8,128)S(1)}, u32[]{:S(2)}, u32[]{:S(2)}) collective-permute-start(f32[4096,128]{1,0:T(8,128)} %bitcast.22), channel_id=1, source_target_pairs={{0,1},{1,0},{2,3},{3,2},{4,5},{5,4},{6,7},{7,6},{8,9},{9,8},{10,11... | collective-permute-start | bytes 6291464 | tf_op jit(solution)/shard_map/ppermute | solution.py:290
  303.0 0.0 copy-done.3
  303.1 4.0 %collective-permute-done.2 = f32[4096,128]{1,0:T(8,128)S(1)} collective-permute-done((f32[4096,128]{1,0:T(8,128)}, f32[4096,128]{1,0:T(8,128)S(1)}, u32[]{:S(2)}, u32[]{:S(2)}) %collective-permute-start.2) | collective-permute-done | bytes 2097184 | tf_op jit(solution)/shard_map/ppermute | solution.py:290
  307.0 0.0 copy-done.2
  307.0 3.1 fusion.1
  (8 shorter events, 0.0 us)
Async XLA Ops:
  0.6 36.8 %copy-start = (bf16[16,6144]{1,0:T(8,128)(2,1)S(1)}, bf16[16,6144]{1,0:T(8,128)(2,1)}, u32[]{:S(2)}) copy-start(bf16[16,6144]{1,0:T(8,128)(2,1)} %param.13) | copy-start | bytes 589828
  7.6 11.2 %copy-start.4 = (s32[48,14]{0,1:T(8,128)S(1)}, s32[48,14]{0,1:T(8,128)}, u32[]{:S(2)}) copy-start(s32[48,14]{0,1:T(8,128)} %param.12) | copy-start | bytes 8068
  7.6 122.0 %all-to-all-start = ((bf16[64,4,128,128]{3,2,1,0:T(8,128)(2,1)}), bf16[64,4,128,128]{3,2,1,0:T(8,128)(2,1)}, u32[]{:S(2)}, u32[]{:S(2)}) async-start(bf16[64,4,128,128]{3,2,1,0:T(8,128)(2,1)} %bitcast.20), calls=%async_computation | async-start | bytes 16777216 | tf_op jit(solution)/shard_map/all_to_all | solution.py:247
  18.8 18.7 %copy-start.5 = (bf16[16,128]{1,0:T(8,128)(2,1)S(1)}, bf16[16,128]{1,0:T(8,128)(2,1)}, u32[]{:S(2)}) copy-start(bf16[16,128]{1,0:T(8,128)(2,1)} %param.14) | copy-start | bytes 12292
  164.2 124.7 %all-to-all-start.1 = ((bf16[64,4,128,128]{3,2,1,0:T(8,128)(2,1)}), bf16[64,4,128,128]{3,2,1,0:T(8,128)(2,1)}, u32[]{:S(2)}, u32[]{:S(2)}) async-start(bf16[64,4,128,128]{3,2,1,0:T(8,128)(2,1)} %bitcast.21), calls=%async_computation.1 | async-start | bytes 16777216 | tf_op jit(solution)/shard_map/all_to_all | solution.py:279
  174.7 91.5 %collective-permute-start.1 = (bf16[128,128]{1,0:T(8,128)(2,1)S(1)}, bf16[128,128]{1,0:T(8,128)(2,1)S(1)}, u32[]{:S(2)}, u32[]{:S(2)}) collective-permute-start(bf16[128,128]{1,0:T(8,128)(2,1)S(1)} %get-tuple-element.7), channel_id=1, source_target_pairs={{2,0},{4,2},{6,4},{8,6},{10,8},{12,10},{14,12},{16,14},{18,16},{20... | collective-permute-start | bytes 98312 | tf_op jit(solution)/shard_map/ppermute | solution.py:259
  177.0 89.1 %collective-permute-start = (bf16[128,128]{1,0:T(8,128)(2,1)S(1)}, bf16[128,128]{1,0:T(8,128)(2,1)S(1)}, u32[]{:S(2)}, u32[]{:S(2)}) collective-permute-start(bf16[128,128]{1,0:T(8,128)(2,1)S(1)} %get-tuple-element.6), channel_id=1, source_target_pairs={{0,2},{2,4},{4,6},{6,8},{8,10},{10,12},{12,14},{14,16},{16,18},{18... | collective-permute-start | bytes 98312 | tf_op jit(solution)/shard_map/ppermute | solution.py:258
  289.0 14.1 %copy-start.3 = (f32[256,128]{1,0:T(8,128)S(1)}, f32[256,128]{1,0:T(8,128)}, u32[]{:S(2)}) copy-start(f32[256,128]{1,0:T(8,128)} %shard_map.116._) | copy-start | bytes 393220
  289.0 18.1 %copy-start.2 = (f32[3840,128]{1,0:T(8,128)S(1)}, f32[3840,128]{1,0:T(8,128)}, u32[]{:S(2)}) copy-start(f32[3840,128]{1,0:T(8,128)} %shard_map.114._) | copy-start | bytes 5898244
  297.2 9.8 %collective-permute-start.2 = (f32[4096,128]{1,0:T(8,128)}, f32[4096,128]{1,0:T(8,128)S(1)}, u32[]{:S(2)}, u32[]{:S(2)}) collective-permute-start(f32[4096,128]{1,0:T(8,128)} %bitcast.22), channel_id=1, source_target_pairs={{0,1},{1,0},{2,3},{3,2},{4,5},{5,4},{6,7},{7,6},{8,9},{9,8},{10,11... | collective-permute-start | bytes 6291464 | tf_op jit(solution)/shard_map/ppermute | solution.py:290
  307.0 3.1 copy-start.1

commit v15 on v13

--- a/solution.py
+++ b/solution.py
@@ -218,7 +218,7 @@
         out_ref[s] = src_ref[idx_ref[c * chunk + s]]
 
 
-def gather_blocks(idx, blocks, chunk=128):
+def gather_blocks(idx, blocks, chunk=64):
     count = idx.shape[0]
     return pl.pallas_call(
         gather_kernel,

time: 314 us -> 314 us (level)
  no operation moved by 1% of the time
where the time goes in v15:
time: 314 us; the launch traced here: 310 us
  waiting for transfers between devices  202 us (64%)
  Pallas kernels  67.8 us (22%)
  starting transfers between devices  28.7 us (9%)
  other arithmetic  4.37 us (1%)
  local copies, waits for them, and re-layouts  3.42 us (1%)
    all_to_all x1, waiting for transfers between devices, local(): lax.all_to_all(outgoing, 'region', split_axis=0, concat_axis=0, tiled=True)  89.9 us
    ppermute x1, waiting for transfers between devices, local(): lax.ppermute(head, 'region', [((i + 1) % count, i) for i in range(count)])  88 us
    pallas_call x1, Pallas kernels, trip_pass(): pl.pallas_call(functools.partial(trip_kernel, pair_count, trip_steps), gr...  34.3 us
    all_to_all x1, waiting for transfers between devices, local(): lax.all_to_all(slot_grad.reshape(regions, slot_count, rank_width, block_s...  20.5 us
    pallas_call x1, Pallas kernels, smooth_inner(): pl.pallas_call(smooth_inner_kernel, grid=(inner,), in_specs=[pl.BlockSpec...  17.9 us
    all_to_all x1, starting transfers between devices, local(): lax.all_to_all(outgoing, 'region', split_axis=0, concat_axis=0, tiled=True)  11.2 us
    all_to_all x1, starting transfers between devices, local(): lax.all_to_all(slot_grad.reshape(regions, slot_count, rank_width, block_s...  9.65 us
    pallas_call x1, Pallas kernels, owned_pass(): pl.pallas_call(owned_kernel, grid_spec=pltpu.PrefetchScalarGridSpec(num_s...  7.99 us
  transfers between devices with their start and end apart: 5, of which 4 were waited for; matrix products, arithmetic and copies ran while one was open for 2% of the time, Pallas kernels for 6%

profile of v15, /device:TPU:13, one launch (start us, length us, event | category | flops | bytes accessed | tf_op | source)
XLA Modules:
  0.0 309.7 jit_solution(5416906155496483856)
XLA Ops:
  0.6 0.0 copy-start
  0.6 0.8 copy.13
  1.5 0.1 squeeze.9
  1.6 0.6 compare_select_fusion
  2.2 5.5 %shard_map.113 = bf16[256,128,128]{2,1,0:T(8,128)(2,1)} custom-call(s32[256]{0:T(256)} %get-tuple-element.13.idx_ref, bf16[32,128,128]{2,1,0:T(8,128)(2,1)} %bitcast.23), custom_call_target="tpu_custom_call" | custom-call | tf_op jit(solution)/shard_map/pallas_call | solution.py:223
  7.7 11.2 %all-to-all-start = ((bf16[64,4,128,128]{3,2,1,0:T(8,128)(2,1)}), bf16[64,4,128,128]{3,2,1,0:T(8,128)(2,1)}, u32[]{:S(2)}, u32[]{:S(2)}) async-start(bf16[64,4,128,128]{3,2,1,0:T(8,128)(2,1)} %bitcast.20), calls=%async_computation | async-start | bytes 16777216 | tf_op jit(solution)/shard_map/all_to_all | solution.py:251
  18.8 0.0 copy-done.4
  18.8 0.0 copy-start.5
  18.9 0.1 copy.12
  18.9 0.7 reshape.38.pb_ref
  19.7 17.9 %shard_map.114._ = f32[3840,128]{1,0:T(8,128)} custom-call(bf16[4096,128]{1,0:T(8,128)(2,1)} %emb_ref.1, s32[4,4096]{1,0:T(4,128)} %bitcast.24, f32[4,4096]{1,0:T(4,128)} %bitcast.26), custom_call_target="tpu_custom_call" | custom-call | tf_op jit(solution)/shard_map/pallas_call | solution.py:142
  37.5 0.0 copy-done
  37.5 0.0 copy-done.5
  37.5 2.2 fusion.5.qt_ref
  39.8 89.9 %all-to-all-done = bf16[64,4,128,128]{3,2,1,0:T(8,128)(2,1)} async-done(((bf16[64,4,128,128]{3,2,1,0:T(8,128)(2,1)}), bf16[64,4,128,128]{3,2,1,0:T(8,128)(2,1)}, u32[]{:S(2)}, u32[]{:S(2)}) %all-to-all-start) | async-done | bytes 8388640 | tf_op jit(solution)/shard_map/all_to_all | solution.py:251
  129.7 34.3 %shard_map.115 = (f32[48,1,128]{2,1,0:T(1,128)}, bf16[256,128,128]{2,1,0:T(8,128)(2,1)}) custom-call(s32[672]{0:T(1024)} %reshape.38.pb_ref, bf16[48,14,128,128]{3,2,1,0:T(8,128)(2,1)} %len_ref.1, bf16[256,128,128]{2,1,0:T(8,128)(2,1)} %bitcast.2.inc_ref, f32[128,6144]{1,0:T(8,128)} %fusion.5.qt_ref, f32[48,1,128]{2,1,0:T(1,128)} %bitcast.28, ...), custom_call_target="tpu_custom_call" | custom-call | tf_op jit(solution)/shard_map/pallas_call | solution.py:67
  164.0 9.6 %all-to-all-start.1 = ((bf16[64,4,128,128]{3,2,1,0:T(8,128)(2,1)}), bf16[64,4,128,128]{3,2,1,0:T(8,128)(2,1)}, u32[]{:S(2)}, u32[]{:S(2)}) async-start(bf16[64,4,128,128]{3,2,1,0:T(8,128)(2,1)} %bitcast.21), calls=%async_computation.1 | async-start | bytes 16777216 | tf_op jit(solution)/shard_map/all_to_all | solution.py:283
  173.6 0.8 fusion.2
  174.4 2.4 collective-permute-start.1
  176.8 0.0 collective-permute-start
  176.8 0.9 fusion.3
  177.7 88.0 %collective-permute-done.1 = bf16[128,128]{1,0:T(8,128)(2,1)S(1)} collective-permute-done((bf16[128,128]{1,0:T(8,128)(2,1)S(1)}, bf16[128,128]{1,0:T(8,128)(2,1)S(1)}, u32[]{:S(2)}, u32[]{:S(2)}) %collective-permute-start.1) | collective-permute-done | bytes 32800 | tf_op jit(solution)/shard_map/ppermute | solution.py:263
  265.7 0.0 collective-permute-done
  265.7 0.7 pad_maximum_fusion.win_ref
  266.4 2.2 shard_map.116._
  268.6 20.5 %all-to-all-done.1 = bf16[64,4,128,128]{3,2,1,0:T(8,128)(2,1)} async-done(((bf16[64,4,128,128]{3,2,1,0:T(8,128)(2,1)}), bf16[64,4,128,128]{3,2,1,0:T(8,128)(2,1)}, u32[]{:S(2)}, u32[]{:S(2)}) %all-to-all-start.1) | async-done | bytes 8388640 | tf_op jit(solution)/shard_map/all_to_all | solution.py:283
  289.1 8.0 %shard_map.117 = f32[32,128,128]{2,1,0:T(8,128)} custom-call(s32[256]{0:T(256)} %get-tuple-element.12.tgt_ref, bf16[256,128,128]{2,1,0:T(8,128)(2,1)} %bitcast.9.ret_ref, f32[256,128]{1,0:T(8,128)} %shard_map.116._), custom_call_target="tpu_custom_call" | custom-call | tf_op jit(solution)/shard_map/pallas_call | solution.py:196
  297.1 5.5 %collective-permute-start.2 = (f32[4096,128]{1,0:T(8,128)}, f32[4096,128]{1,0:T(8,128)S(1)}, u32[]{:S(2)}, u32[]{:S(2)}) collective-permute-start(f32[4096,128]{1,0:T(8,128)} %bitcast.22), channel_id=1, source_target_pairs={{0,1},{1,0},{2,3},{3,2},{4,5},{5,4},{6,7},{7,6},{8,9},{9,8},{10,11... | collective-permute-start | bytes 6291464 | tf_op jit(solution)/shard_map/ppermute | solution.py:294
  302.6 0.0 copy-done.3
  302.6 4.0 %collective-permute-done.2 = f32[4096,128]{1,0:T(8,128)S(1)} collective-permute-done((f32[4096,128]{1,0:T(8,128)}, f32[4096,128]{1,0:T(8,128)S(1)}, u32[]{:S(2)}, u32[]{:S(2)}) %collective-permute-start.2) | collective-permute-done | bytes 2097184 | tf_op jit(solution)/shard_map/ppermute | solution.py:294
  306.6 0.0 copy-done.2
  306.6 3.1 fusion.1
  (8 shorter events, 0.0 us)
Async XLA Ops:
  0.6 36.9 %copy-start = (bf16[16,6144]{1,0:T(8,128)(2,1)S(1)}, bf16[16,6144]{1,0:T(8,128)(2,1)}, u32[]{:S(2)}) copy-start(bf16[16,6144]{1,0:T(8,128)(2,1)} %param.13) | copy-start | bytes 589828
  7.7 11.2 %copy-start.4 = (s32[48,14]{0,1:T(8,128)S(1)}, s32[48,14]{0,1:T(8,128)}, u32[]{:S(2)}) copy-start(s32[48,14]{0,1:T(8,128)} %param.12) | copy-start | bytes 8068
  7.7 122.0 %all-to-all-start = ((bf16[64,4,128,128]{3,2,1,0:T(8,128)(2,1)}), bf16[64,4,128,128]{3,2,1,0:T(8,128)(2,1)}, u32[]{:S(2)}, u32[]{:S(2)}) async-start(bf16[64,4,128,128]{3,2,1,0:T(8,128)(2,1)} %bitcast.20), calls=%async_computation | async-start | bytes 16777216 | tf_op jit(solution)/shard_map/all_to_all | solution.py:251
  18.8 18.7 %copy-start.5 = (bf16[16,128]{1,0:T(8,128)(2,1)S(1)}, bf16[16,128]{1,0:T(8,128)(2,1)}, u32[]{:S(2)}) copy-start(bf16[16,128]{1,0:T(8,128)(2,1)} %param.14) | copy-start | bytes 12292
  164.0 125.1 %all-to-all-start.1 = ((bf16[64,4,128,128]{3,2,1,0:T(8,128)(2,1)}), bf16[64,4,128,128]{3,2,1,0:T(8,128)(2,1)}, u32[]{:S(2)}, u32[]{:S(2)}) async-start(bf16[64,4,128,128]{3,2,1,0:T(8,128)(2,1)} %bitcast.21), calls=%async_computation.1 | async-start | bytes 16777216 | tf_op jit(solution)/shard_map/all_to_all | solution.py:283
  174.4 91.2 %collective-permute-start.1 = (bf16[128,128]{1,0:T(8,128)(2,1)S(1)}, bf16[128,128]{1,0:T(8,128)(2,1)S(1)}, u32[]{:S(2)}, u32[]{:S(2)}) collective-permute-start(bf16[128,128]{1,0:T(8,128)(2,1)S(1)} %get-tuple-element.7), channel_id=1, source_target_pairs={{2,0},{4,2},{6,4},{8,6},{10,8},{12,10},{14,12},{16,14},{18,16},{20... | collective-permute-start | bytes 98312 | tf_op jit(solution)/shard_map/ppermute | solution.py:263
  176.8 88.9 %collective-permute-start = (bf16[128,128]{1,0:T(8,128)(2,1)S(1)}, bf16[128,128]{1,0:T(8,128)(2,1)S(1)}, u32[]{:S(2)}, u32[]{:S(2)}) collective-permute-start(bf16[128,128]{1,0:T(8,128)(2,1)S(1)} %get-tuple-element.6), channel_id=1, source_target_pairs={{0,2},{2,4},{4,6},{6,8},{8,10},{10,12},{12,14},{14,16},{16,18},{18... | collective-permute-start | bytes 98312 | tf_op jit(solution)/shard_map/ppermute | solution.py:262
  289.1 13.5 %copy-start.3 = (f32[256,128]{1,0:T(8,128)S(1)}, f32[256,128]{1,0:T(8,128)}, u32[]{:S(2)}) copy-start(f32[256,128]{1,0:T(8,128)} %shard_map.116._) | copy-start | bytes 393220
  289.1 17.5 %copy-start.2 = (f32[3840,128]{1,0:T(8,128)S(1)}, f32[3840,128]{1,0:T(8,128)}, u32[]{:S(2)}) copy-start(f32[3840,128]{1,0:T(8,128)} %shard_map.114._) | copy-start | bytes 5898244
  297.1 9.5 %collective-permute-start.2 = (f32[4096,128]{1,0:T(8,128)}, f32[4096,128]{1,0:T(8,128)S(1)}, u32[]{:S(2)}, u32[]{:S(2)}) collective-permute-start(f32[4096,128]{1,0:T(8,128)} %bitcast.22), channel_id=1, source_target_pairs={{0,1},{1,0},{2,3},{3,2},{4,5},{5,4},{6,7},{7,6},{8,9},{9,8},{10,11... | collective-permute-start | bytes 6291464 | tf_op jit(solution)/shard_map/ppermute | solution.py:294
  306.6 3.1 copy-start.1
